TPU v7x, 512 devices: a whole 4x8x8 slice. The times are simulated.
512 devices in a mesh: dom: 128 (over z, y, core), feat: 4 (over x).
Axes of the slice: x: 4, y: 8, z: 8, core: 2. Of those that a mesh axis runs over, the one named last changes fastest.
Arguments:
- features: bfloat16 [57344, 128], P('dom'), may hold values from -6 to 6
- perturb: bfloat16 [57344, 128], P('dom'), may hold values from -0.5 to 0.5
- w_self: bfloat16 [128, 1024], P(None, 'feat'), may hold values from -0.5 to 0.5
- w_neigh: bfloat16 [128, 1024], P(None, 'feat'), may hold values from -0.5 to 0.5
- bias: float32 [1024], P('feat'), may hold values from -3 to 3
- upstream: bfloat16 [57344, 1024], P('dom', 'feat'), may hold values from -0.0234375 to 0.0234375
- hub_rows: int32 [128, 2], P('dom'), may hold values from 0 to 447, as said below
- send_rows: int32 [128, 4, 56], P('dom'), may hold values from -1 to 447, as said below
- neighbors: int32 [57344, 15], P('dom'), may hold values from 0 to 927, as said below
Outputs:
- new_perturb: bfloat16 [57344, 128], P('dom', 'feat')
- grad_self: float32 [128, 1024], P(None, 'feat')
- grad_neigh: float32 [128, 1024], P(None, 'feat')
Inputs may be any that keep to these rules, and one draw needn't show every extreme that they name: hub_rows[s] are distinct rows of partition s. send_rows[s, o] lists distinct rows of partition s sent to partition s + off(o) mod 128; live entries come first, at least 14 of them, and in every draw some list is full with 56 live entries. `neighbors`: indices below 448 are rows of the node's own partition; indices 448 + o * 56 + j refer only to live slots of the list that partition s = p - off(o) mod 128 sends to p; indices from 672 on are hub nodes.
All inputs are finite; a program needn't handle non-finite values.
Results may differ from a plain program's by a relative error of at most 0.001.
The roundings to bfloat16 on the way count: a program that leaves them out, or rounds other values in their place, can miss the bound.
Values may be sent and summed in bfloat16 or wider, within the bound.
No kernel may reach another device: no remote copies, remote signals or barrier semaphores. Data moves between devices by JAX's collectives and lax.ppermute only.
A program may use at most 64 MiB of HBM per device.

v0:
```python
import jax
import jax.numpy as jnp
from jax import lax
from jax.sharding import PartitionSpec as P

K = 15
NOFF = 4
F32 = jnp.float32
BF16 = jnp.bfloat16
HIGH = lax.Precision.HIGHEST


def from_behind(x, axis, by):
    size = lax.axis_size(axis)
    return lax.ppermute(x, axis, [(i, (i + by) % size) for i in range(size)])


def offset_of(direction):
    return direction - 2 if direction < 2 else direction - 1


def contract_rows(left, right, precision=None):
    return lax.dot_general(
        left, right, (((0,), (0,)), ((), ())), preferred_element_type=F32, precision=precision
    )


def gather_all(x, axis):
    n = lax.axis_size(axis)
    rep = jnp.broadcast_to(x[None], (n,) + x.shape).reshape((n * x.shape[0],) + x.shape[1:])
    out = lax.all_to_all(rep, axis, 0, 0, tiled=True)
    return out.reshape((n,) + x.shape)


def per_device(features, perturb, w_self, w_neigh, bias, upstream, hub_rows, send_rows, neighbors):
    rows_here, feat_in = features.shape
    hidden_here = w_self.shape[1]
    slots = send_rows.shape[2]
    hub_dev = hub_rows.shape[1]
    dom_count = lax.axis_size("dom")
    feat_count = lax.axis_size("feat")
    column = lax.axis_index("feat")
    slice_width = feat_in // feat_count
    halo_rows = NOFF * slots
    table_rows = rows_here + halo_rows + dom_count * hub_dev

    perturbed = (features.astype(F32) + perturb.astype(F32)).astype(BF16)

    send_flat = send_rows[0].reshape(halo_rows)
    pick = (send_flat[:, None] == lax.broadcasted_iota(jnp.int32, (halo_rows, rows_here), 1))
    hub_pick = (hub_rows[0][:, None] == lax.broadcasted_iota(jnp.int32, (hub_dev, rows_here), 1))
    halo_out = jnp.dot(pick.astype(BF16), perturbed, preferred_element_type=F32).astype(BF16)
    hub_out = jnp.dot(hub_pick.astype(BF16), perturbed, preferred_element_type=F32).astype(BF16)

    pieces = [
        from_behind(halo_out[o * slots : (o + 1) * slots], "dom", offset_of(o)) for o in range(NOFF)
    ]
    hubs = gather_all(hub_out, "dom").reshape(dom_count * hub_dev, feat_in)
    table = jnp.concatenate([perturbed] + pieces + [hubs], 0)

    t_iota = lax.broadcasted_iota(jnp.int32, (rows_here, K, table_rows), 2)
    counts = jnp.sum((neighbors[:, :, None] == t_iota).astype(F32), axis=1)
    gathered_sum = jnp.dot(counts.astype(BF16), table, preferred_element_type=F32)
    neighbor_mean = (gathered_sum / K).astype(BF16)

    preact = jnp.dot(perturbed, w_self, preferred_element_type=F32)
    preact = preact + jnp.dot(neighbor_mean, w_neigh, preferred_element_type=F32) + bias
    sigmoid_pre = jax.nn.sigmoid(preact)
    grad_pre = (
        upstream.astype(F32) * sigmoid_pre * (1.0 + preact * (1.0 - sigmoid_pre))
    ).astype(BF16)
    part_self = contract_rows(perturbed, grad_pre)
    part_neigh = contract_rows(neighbor_mean, grad_pre)

    payload = jnp.concatenate([grad_pre, w_self, w_neigh], 0)
    got = gather_all(payload, "feat")
    gp_all = got[:, :rows_here]
    ws_all = got[:, rows_here : rows_here + feat_in]
    wn_all = got[:, rows_here + feat_in :]
    dims = (((0, 2), (0, 2)), ((), ()))
    own_grad = lax.dot_general(gp_all, ws_all, dims, preferred_element_type=F32)
    spread = lax.dot_general(gp_all, wn_all, dims, preferred_element_type=F32) / K

    table_grad = contract_rows(counts, spread, HIGH)

    returned = jnp.concatenate(
        [
            from_behind(
                table_grad[rows_here + o * slots : rows_here + (o + 1) * slots],
                "dom",
                -offset_of(o),
            )
            for o in range(NOFF)
        ],
        0,
    )

    weight_flat = jnp.concatenate([part_self.reshape(-1), part_neigh.reshape(-1)])
    weight_chunks = weight_flat.reshape(dom_count, -1)
    hub_chunks = table_grad[rows_here + halo_rows :].reshape(dom_count, hub_dev * feat_in)
    sent = jnp.concatenate([hub_chunks, weight_chunks], 1)
    recv = lax.all_to_all(sent, "dom", 0, 0, tiled=True)
    totals = jnp.sum(recv, axis=0)
    hub_total = totals[: hub_dev * feat_in].reshape(hub_dev, feat_in)
    weight_part = totals[hub_dev * feat_in :]

    grad_in = own_grad + table_grad[:rows_here]
    grad_in = grad_in + contract_rows(pick.astype(F32), returned, HIGH)
    grad_in = grad_in + contract_rows(hub_pick.astype(F32), hub_total, HIGH)

    mean_square = jnp.mean(grad_in * grad_in, axis=1, keepdims=True)
    own_cols = lax.dynamic_slice_in_dim(grad_in, column * slice_width, slice_width, 1)
    own_perturb = lax.dynamic_slice_in_dim(perturb, column * slice_width, slice_width, 1).astype(F32)
    new_perturb = (own_perturb + 0.5 * own_cols / jnp.sqrt(mean_square + 1e-06)).astype(BF16)

    weights = gather_all(weight_part, "dom").reshape(2, feat_in, hidden_here)
    return (new_perturb, weights[0], weights[1])


def solution(mesh):
    in_specs = (
        P("dom", None),
        P("dom", None),
        P(None, "feat"),
        P(None, "feat"),
        P("feat"),
        P("dom", "feat"),
        P("dom", None),
        P("dom", None, None),
        P("dom", None),
    )
    out_specs = (P("dom", "feat"), P(None, "feat"), P(None, "feat"))
    return jax.shard_map(
        per_device, mesh=mesh, in_specs=in_specs, out_specs=out_specs, check_vma=False
    )
```

profile of v0, /device:TPU:1, one launch (start us, length us, event | category | flops | bytes accessed | tf_op | source)
XLA Modules:
  0.0 129.9 jit_solution(4145228172987175372)
XLA Ops:
  0.6 0.8 eq.30
  1.4 1.0 constant_dynamic-update-slice_fusion.5
  2.4 0.3 convolution_convert_fusion
  2.7 14.4 %collective-permute-start = (bf16[56,128]{1,0:T(8,128)(2,1)S(1)}, bf16[56,128]{1,0:T(8,128)(2,1)S(1)}, u32[]{:S(2)}, u32[]{:S(2)}) collective-permute-start(bf16[56,128]{1,0:T(8,128)(2,1)S(1)} %get-tuple-element.23), channel_id=1, source_target_pairs={{0,504},{4,508},{8,0},{12,4},{16,8},{20,12},{24,16},{28,20},{32,24... | collective-permute-start | bytes 43016 | tf_op jit(solution)/shard_map/ppermute | solution.py:15
  17.1 2.9 %collective-permute-start.1 = (bf16[56,128]{1,0:T(8,128)(2,1)S(1)}, bf16[56,128]{1,0:T(8,128)(2,1)S(1)}, u32[]{:S(2)}, u32[]{:S(2)}) collective-permute-start(bf16[56,128]{1,0:T(8,128)(2,1)S(1)} %get-tuple-element.22), channel_id=1, source_target_pairs={{0,508},{4,0},{8,4},{12,8},{16,12},{20,16},{24,20},{28,24},{32,28}... | collective-permute-start | bytes 43016 | tf_op jit(solution)/shard_map/ppermute | solution.py:15
  20.0 2.7 %collective-permute-start.2 = (bf16[56,128]{1,0:T(8,128)(2,1)S(1)}, bf16[56,128]{1,0:T(8,128)(2,1)S(1)}, u32[]{:S(2)}, u32[]{:S(2)}) collective-permute-start(bf16[56,128]{1,0:T(8,128)(2,1)S(1)} %get-tuple-element.21), channel_id=1, source_target_pairs={{0,4},{4,8},{8,12},{12,16},{16,20},{20,24},{24,28},{28,32},{32,36}... | collective-permute-start | bytes 43016 | tf_op jit(solution)/shard_map/ppermute | solution.py:15
  22.7 1.9 %collective-permute-start.3 = (bf16[56,128]{1,0:T(8,128)(2,1)S(1)}, bf16[56,128]{1,0:T(8,128)(2,1)S(1)}, u32[]{:S(2)}, u32[]{:S(2)}) collective-permute-start(bf16[56,128]{1,0:T(8,128)(2,1)S(1)} %get-tuple-element.20), channel_id=1, source_target_pairs={{0,8},{4,12},{8,16},{12,20},{16,24},{20,28},{24,32},{28,36},{32,40... | collective-permute-start | bytes 43016 | tf_op jit(solution)/shard_map/ppermute | solution.py:15
  24.6 0.8 convolution_convert_fusion.1
  25.5 0.7 broadcast_in_dim.4
  26.1 8.6 %all-to-all-start = ((bf16[128,2,128]{2,1,0:T(2,128)(2,1)}), bf16[128,2,128]{2,1,0:T(2,128)(2,1)S(1)}, u32[]{:S(2)}, u32[]{:S(2)}) async-start(bf16[128,2,128]{2,1,0:T(2,128)(2,1)} %broadcast_in_dim.4), calls=%async_computation | async-start | bytes 131072 | tf_op jit(solution)/shard_map/all_to_all | solution.py:31
  34.7 5.0 %convert_reduce_fusion = f32[448,928]{1,0:T(8,128)S(1)} fusion(s32[448,15]{0,1:T(8,128)} %param.17), kind=kLoop, calls=%fused_computation | loop fusion | flops 18292736 | bytes 1689856 | tf_op jit(solution)/shard_map/reduce_sum | solution.py:62
  39.7 0.0 copy-start.7
  39.8 0.0 copy-start.9
  39.8 0.2 fusion.27
  40.1 6.1 %all-to-all-done = bf16[128,2,128]{2,1,0:T(2,128)(2,1)S(1)} async-done(((bf16[128,2,128]{2,1,0:T(2,128)(2,1)}), bf16[128,2,128]{2,1,0:T(2,128)(2,1)S(1)}, u32[]{:S(2)}, u32[]{:S(2)}) %all-to-all-start) | async-done | bytes 65568 | tf_op jit(solution)/shard_map/all_to_all | solution.py:31
  46.1 0.4 fusion.4
  46.6 0.0 copy-start.5
  46.6 0.3 multiply_convert_fusion
  47.0 1.2 broadcast_in_dim.5
  48.2 4.0 %all-to-all-start.1 = ((bf16[4,704,256]{2,1,0:T(8,128)(2,1)}), bf16[4,704,256]{2,1,0:T(8,128)(2,1)S(1)}, u32[]{:S(2)}, u32[]{:S(2)}) async-start(bf16[4,704,256]{2,1,0:T(8,128)(2,1)} %broadcast_in_dim.5), calls=%async_computation.1 | async-start | bytes 2883584 | tf_op jit(solution)/shard_map/all_to_all | solution.py:31
  52.2 1.8 %fusion.30 = f32[128,256]{1,0:T(8,128)} fusion(bf16[448,128]{1,0:T(8,128)(2,1)} %copy-done.5, bf16[448,256]{1,0:T(8,128)(2,1)S(1)} %multiply_convert_fusion), kind=kOutput, calls=%fused_computation.56 | convolution fusion | flops 29360128 | bytes 475136 | tf_op jit(solution)/shard_map/dot_general | solution.py:23
  54.0 1.6 %concatenate.24 = f32[64,512]{1,0:T(8,128)} reshape(f32[128,256]{1,0:T(8,128)} %fusion.30) | data formatting | bytes 262144 | tf_op jit(solution)/shard_map/concatenate | solution.py:98
  55.6 1.8 %fusion.29 = f32[128,256]{1,0:T(8,128)} fusion(bf16[448,128]{1,0:T(8,128)(2,1)} %copy-done.2, bf16[448,256]{1,0:T(8,128)(2,1)S(1)} %multiply_convert_fusion), kind=kOutput, calls=%fused_computation.55 | convolution fusion | flops 29360128 | bytes 475136 | tf_op jit(solution)/shard_map/dot_general | solution.py:23
  57.4 0.9 concatenate.23
  58.3 12.5 %all-to-all-done.1 = bf16[4,704,256]{2,1,0:T(8,128)(2,1)S(1)} async-done(((bf16[4,704,256]{2,1,0:T(8,128)(2,1)}), bf16[4,704,256]{2,1,0:T(8,128)(2,1)S(1)}, u32[]{:S(2)}, u32[]{:S(2)}) %all-to-all-start.1) | async-done | bytes 1441824 | tf_op jit(solution)/shard_map/all_to_all | solution.py:31
  70.8 0.4 fusion.2
  71.2 3.4 %fusion.28 = f32[928,128]{1,0:T(8,128)S(1)} fusion(f32[448,928]{1,0:T(8,128)S(1)} %convert_reduce_fusion, f32[448,128]{1,0:T(8,128)S(1)} %fusion.2), kind=kOutput, calls=%fused_computation.54 | convolution fusion | flops 638582784 | bytes 2367488 | tf_op jit(solution)/shard_map/dot_general | solution.py:23
  74.6 0.8 copy-done
  75.5 0.0 copy-start.8
  75.5 1.0 all_to_all.25
  76.5 9.2 %all-to-all-start.2 = ((f32[128,1,768]{2,1,0:T(1,128)}), f32[128,1,768]{2,1,0:T(1,128)S(1)}, u32[]{:S(2)}, u32[]{:S(2)}) async-start(f32[128,1,768]{2,1,0:T(1,128)} %all_to_all.25), calls=%async_computation.2 | async-start | bytes 786432 | tf_op jit(solution)/shard_map/all_to_all | solution.py:102
  85.7 7.3 %collective-permute-start.7 = (f32[56,128]{1,0:T(8,128)S(1)}, f32[56,128]{1,0:T(8,128)S(1)}, u32[]{:S(2)}, u32[]{:S(2)}) collective-permute-start(f32[56,128]{1,0:T(8,128)S(1)} %get-tuple-element.17), channel_id=1, source_target_pairs={{0,504},{4,508},{8,0},{12,4},{16,8},{20,12},{24,16},{28,20},{32,24... | collective-permute-start | bytes 86024 | tf_op jit(solution)/shard_map/ppermute | solution.py:15
  93.0 2.6 %collective-permute-start.6 = (f32[56,128]{1,0:T(8,128)S(1)}, f32[56,128]{1,0:T(8,128)S(1)}, u32[]{:S(2)}, u32[]{:S(2)}) collective-permute-start(f32[56,128]{1,0:T(8,128)S(1)} %get-tuple-element.18), channel_id=1, source_target_pairs={{0,508},{4,0},{8,4},{12,8},{16,12},{20,16},{24,20},{28,24},{32,28}... | collective-permute-start | bytes 86024 | tf_op jit(solution)/shard_map/ppermute | solution.py:15
  95.6 3.0 %collective-permute-start.5 = (f32[56,128]{1,0:T(8,128)S(1)}, f32[56,128]{1,0:T(8,128)S(1)}, u32[]{:S(2)}, u32[]{:S(2)}) collective-permute-start(f32[56,128]{1,0:T(8,128)S(1)} %get-tuple-element.19), channel_id=1, source_target_pairs={{0,4},{4,8},{8,12},{12,16},{16,20},{20,24},{24,28},{28,32},{32,36}... | collective-permute-start | bytes 86024 | tf_op jit(solution)/shard_map/ppermute | solution.py:15
  98.6 2.1 %collective-permute-start.4 = (f32[56,128]{1,0:T(8,128)S(1)}, f32[56,128]{1,0:T(8,128)S(1)}, u32[]{:S(2)}, u32[]{:S(2)}) collective-permute-start(f32[56,128]{1,0:T(8,128)S(1)} %get-tuple-element.16), channel_id=1, source_target_pairs={{0,8},{4,12},{8,16},{12,20},{16,24},{20,28},{24,32},{28,36},{32,40... | collective-permute-start | bytes 86024 | tf_op jit(solution)/shard_map/ppermute | solution.py:15
  100.7 0.4 fusion.3
  101.1 2.4 %all-to-all-done.2 = f32[128,1,768]{2,1,0:T(1,128)S(1)} async-done(((f32[128,1,768]{2,1,0:T(1,128)}), f32[128,1,768]{2,1,0:T(1,128)S(1)}, u32[]{:S(2)}, u32[]{:S(2)}) %all-to-all-start.2) | async-done | bytes 393248 | tf_op jit(solution)/shard_map/all_to_all | solution.py:102
  103.5 0.3 reduce_sum.28
  103.8 0.4 fusion.19
  104.3 0.8 all_to_all.27
  105.1 7.6 %all-to-all-start.3 = ((f32[128,512,1]{1,2,0:T(1,128)}), f32[128,512,1]{1,2,0:T(1,128)S(1)}, u32[]{:S(2)}, u32[]{:S(2)}) async-start(f32[128,512,1]{1,2,0:T(1,128)} %all_to_all.27), calls=%async_computation.3 | async-start | bytes 524288 | tf_op jit(solution)/shard_map/all_to_all | solution.py:31
  112.7 0.8 multiply_reduce_fusion
  113.5 0.2 add_convert_fusion
  113.7 0.7 copy.16
  114.4 13.5 %all-to-all-done.3 = f32[128,512,1]{1,2,0:T(1,128)S(1)} async-done(((f32[128,512,1]{1,2,0:T(1,128)}), f32[128,512,1]{1,2,0:T(1,128)S(1)}, u32[]{:S(2)}, u32[]{:S(2)}) %all-to-all-start.3) | async-done | bytes 262176 | tf_op jit(solution)/shard_map/all_to_all | solution.py:31
  127.9 0.7 slice_reduce_fusion
  128.6 0.7 slice.88
  129.3 0.7 slice.90
  (38 shorter events, 0.2 us)
Async XLA Ops:
  0.6 39.1 %copy-start.6 = (bf16[128,256]{1,0:T(8,128)(2,1)S(1)}, bf16[128,256]{1,0:T(8,128)(2,1)}, u32[]{:S(2)}) copy-start(bf16[128,256]{1,0:T(8,128)(2,1)} %param.11) | copy-start | bytes 196612
  2.4 44.1 %copy-start.2 = (bf16[448,128]{1,0:T(8,128)(2,1)}, bf16[448,128]{1,0:T(8,128)(2,1)S(1)}, u32[]{:S(2)}) copy-start(bf16[448,128]{1,0:T(8,128)(2,1)S(1)} %get-tuple-element.15) | copy-start | bytes 344068
  2.7 37.3 %collective-permute-start = (bf16[56,128]{1,0:T(8,128)(2,1)S(1)}, bf16[56,128]{1,0:T(8,128)(2,1)S(1)}, u32[]{:S(2)}, u32[]{:S(2)}) collective-permute-start(bf16[56,128]{1,0:T(8,128)(2,1)S(1)} %get-tuple-element.23), channel_id=1, source_target_pairs={{0,504},{4,508},{8,0},{12,4},{16,8},{20,12},{24,16},{28,20},{32,24... | collective-permute-start | bytes 43016 | tf_op jit(solution)/shard_map/ppermute | solution.py:15
  17.1 22.9 %collective-permute-start.1 = (bf16[56,128]{1,0:T(8,128)(2,1)S(1)}, bf16[56,128]{1,0:T(8,128)(2,1)S(1)}, u32[]{:S(2)}, u32[]{:S(2)}) collective-permute-start(bf16[56,128]{1,0:T(8,128)(2,1)S(1)} %get-tuple-element.22), channel_id=1, source_target_pairs={{0,508},{4,0},{8,4},{12,8},{16,12},{20,16},{24,20},{28,24},{32,28}... | collective-permute-start | bytes 43016 | tf_op jit(solution)/shard_map/ppermute | solution.py:15
  20.0 20.0 %collective-permute-start.2 = (bf16[56,128]{1,0:T(8,128)(2,1)S(1)}, bf16[56,128]{1,0:T(8,128)(2,1)S(1)}, u32[]{:S(2)}, u32[]{:S(2)}) collective-permute-start(bf16[56,128]{1,0:T(8,128)(2,1)S(1)} %get-tuple-element.21), channel_id=1, source_target_pairs={{0,4},{4,8},{8,12},{12,16},{16,20},{20,24},{24,28},{28,32},{32,36}... | collective-permute-start | bytes 43016 | tf_op jit(solution)/shard_map/ppermute | solution.py:15
  22.7 17.4 %collective-permute-start.3 = (bf16[56,128]{1,0:T(8,128)(2,1)S(1)}, bf16[56,128]{1,0:T(8,128)(2,1)S(1)}, u32[]{:S(2)}, u32[]{:S(2)}) collective-permute-start(bf16[56,128]{1,0:T(8,128)(2,1)S(1)} %get-tuple-element.20), channel_id=1, source_target_pairs={{0,8},{4,12},{8,16},{12,20},{16,24},{20,28},{24,32},{28,36},{32,40... | collective-permute-start | bytes 43016 | tf_op jit(solution)/shard_map/ppermute | solution.py:15
  26.1 20.0 %all-to-all-start = ((bf16[128,2,128]{2,1,0:T(2,128)(2,1)}), bf16[128,2,128]{2,1,0:T(2,128)(2,1)S(1)}, u32[]{:S(2)}, u32[]{:S(2)}) async-start(bf16[128,2,128]{2,1,0:T(2,128)(2,1)} %broadcast_in_dim.4), calls=%async_computation | async-start | bytes 131072 | tf_op jit(solution)/shard_map/all_to_all | solution.py:31
  39.7 6.8 %copy-start.7 = (bf16[128,256]{1,0:T(8,128)(2,1)S(1)}, bf16[128,256]{1,0:T(8,128)(2,1)}, u32[]{:S(2)}) copy-start(bf16[128,256]{1,0:T(8,128)(2,1)} %param.12) | copy-start | bytes 196612
  39.8 6.8 %copy-start.9 = (bf16[448,256]{1,0:T(8,128)(2,1)S(1)}, bf16[448,256]{1,0:T(8,128)(2,1)}, u32[]{:S(2)}) copy-start(bf16[448,256]{1,0:T(8,128)(2,1)} %param.14) | copy-start | bytes 688132
  39.8 6.8 %copy-start.10 = (f32[256]{0:T(256)S(1)}, f32[256]{0:T(256)}, u32[]{:S(2)}) copy-start(f32[256]{0:T(256)} %param.13) | copy-start | bytes 3076
  46.6 1.6 %copy-start.5 = (bf16[448,128]{1,0:T(8,128)(2,1)}, bf16[448,128]{1,0:T(8,128)(2,1)S(1)}, u32[]{:S(2)}) copy-start(bf16[448,128]{1,0:T(8,128)(2,1)S(1)} %fusion.4) | copy-start | bytes 344068
  48.2 22.6 %all-to-all-start.1 = ((bf16[4,704,256]{2,1,0:T(8,128)(2,1)}), bf16[4,704,256]{2,1,0:T(8,128)(2,1)S(1)}, u32[]{:S(2)}, u32[]{:S(2)}) async-start(bf16[4,704,256]{2,1,0:T(8,128)(2,1)} %broadcast_in_dim.5), calls=%async_computation.1 | async-start | bytes 2883584 | tf_op jit(solution)/shard_map/all_to_all | solution.py:31
  71.2 4.3 %copy-start.3 = (f32[64,512]{1,0:T(8,128)S(1)}, f32[64,512]{1,0:T(8,128)}, u32[]{:S(2)}) copy-start(f32[64,512]{1,0:T(8,128)} %concatenate.24) | copy-start | bytes 393220
  74.6 0.8 copy-start
  75.4 10.3 %copy-start.1 = (f32[928,128]{1,0:T(8,128)S(1)}, f32[928,128]{1,0:T(8,128)}, u32[]{:S(2)}) copy-start(f32[928,128]{1,0:T(8,128)} %copy-done) | copy-start | bytes 1425412
  75.5 28.3 %copy-start.8 = (s32[1,2]{1,0:T(1,128)S(1)}, s32[1,2]{1,0:T(1,128)}, u32[]{:S(2)}) copy-start(s32[1,2]{1,0:T(1,128)} %param.15) | copy-start | bytes 28
  76.5 27.0 %all-to-all-start.2 = ((f32[128,1,768]{2,1,0:T(1,128)}), f32[128,1,768]{2,1,0:T(1,128)S(1)}, u32[]{:S(2)}, u32[]{:S(2)}) async-start(f32[128,1,768]{2,1,0:T(1,128)} %all_to_all.25), calls=%async_computation.2 | async-start | bytes 786432 | tf_op jit(solution)/shard_map/all_to_all | solution.py:102
  85.7 27.0 %collective-permute-start.7 = (f32[56,128]{1,0:T(8,128)S(1)}, f32[56,128]{1,0:T(8,128)S(1)}, u32[]{:S(2)}, u32[]{:S(2)}) collective-permute-start(f32[56,128]{1,0:T(8,128)S(1)} %get-tuple-element.17), channel_id=1, source_target_pairs={{0,504},{4,508},{8,0},{12,4},{16,8},{20,12},{24,16},{28,20},{32,24... | collective-permute-start | bytes 86024 | tf_op jit(solution)/shard_map/ppermute | solution.py:15
  93.0 19.7 %collective-permute-start.6 = (f32[56,128]{1,0:T(8,128)S(1)}, f32[56,128]{1,0:T(8,128)S(1)}, u32[]{:S(2)}, u32[]{:S(2)}) collective-permute-start(f32[56,128]{1,0:T(8,128)S(1)} %get-tuple-element.18), channel_id=1, source_target_pairs={{0,508},{4,0},{8,4},{12,8},{16,12},{20,16},{24,20},{28,24},{32,28}... | collective-permute-start | bytes 86024 | tf_op jit(solution)/shard_map/ppermute | solution.py:15
  95.6 17.1 %collective-permute-start.5 = (f32[56,128]{1,0:T(8,128)S(1)}, f32[56,128]{1,0:T(8,128)S(1)}, u32[]{:S(2)}, u32[]{:S(2)}) collective-permute-start(f32[56,128]{1,0:T(8,128)S(1)} %get-tuple-element.19), channel_id=1, source_target_pairs={{0,4},{4,8},{8,12},{12,16},{16,20},{20,24},{24,28},{28,32},{32,36}... | collective-permute-start | bytes 86024 | tf_op jit(solution)/shard_map/ppermute | solution.py:15
  98.6 14.9 %copy-start.4 = (bf16[448,128]{1,0:T(8,128)(2,1)S(1)}, bf16[448,128]{1,0:T(8,128)(2,1)}, u32[]{:S(2)}) copy-start(bf16[448,128]{1,0:T(8,128)(2,1)} %param.10) | copy-start | bytes 344068
  98.6 14.1 %collective-permute-start.4 = (f32[56,128]{1,0:T(8,128)S(1)}, f32[56,128]{1,0:T(8,128)S(1)}, u32[]{:S(2)}, u32[]{:S(2)}) collective-permute-start(f32[56,128]{1,0:T(8,128)S(1)} %get-tuple-element.16), channel_id=1, source_target_pairs={{0,8},{4,12},{8,16},{12,20},{16,24},{20,28},{24,32},{28,36},{32,40... | collective-permute-start | bytes 86024 | tf_op jit(solution)/shard_map/ppermute | solution.py:15
  105.1 22.8 %all-to-all-start.3 = ((f32[128,512,1]{1,2,0:T(1,128)}), f32[128,512,1]{1,2,0:T(1,128)S(1)}, u32[]{:S(2)}, u32[]{:S(2)}) async-start(f32[128,512,1]{1,2,0:T(1,128)} %all_to_all.27), calls=%async_computation.3 | async-start | bytes 524288 | tf_op jit(solution)/shard_map/all_to_all | solution.py:31
where the time goes:
time: 131 us; the launch traced here: 130 us
  starting transfers between devices  66.1 us (50%)
  waiting for transfers between devices  34.4 us (26%)
  matrix products  11 us (8%)
  local copies, waits for them, and re-layouts  10.7 us (8%)
  other arithmetic  6.56 us (5%)
    ppermute x8, starting transfers between devices, from_behind(): return lax.ppermute(x, axis, [(i, (i + by) % size) for i in range(size)])  36.8 us
    all_to_all x3, waiting for transfers between devices, gather_all(): out = lax.all_to_all(rep, axis, 0, 0, tiled=True)  32 us
    all_to_all x3, starting transfers between devices, gather_all(): out = lax.all_to_all(rep, axis, 0, 0, tiled=True)  20.2 us
    all_to_all x1, starting transfers between devices, per_device(): recv = lax.all_to_all(sent, 'dom', 0, 0, tiled=True)  9.15 us
    dot_general x5, matrix products, contract_rows(): lax.dot_general(left, right, (((0,), (0,)), ((), ())), preferred_element_...  8.15 us
    reduce_sum x1, other arithmetic, per_device(): counts = jnp.sum((neighbors[:, :, None] == t_iota).astype(F32), axis=1)  5.01 us
  transfers between devices with their start and end apart: 12, of which 4 were waited for; matrix products, arithmetic and copies ran while one was open for 12% of the time, Pallas kernels for 0%

commit v1 on v0

--- a/solution.py
+++ b/solution.py
@@ -44,6 +44,18 @@
     halo_rows = NOFF * slots
     table_rows = rows_here + halo_rows + dom_count * hub_dev
 
+    bias_hi = lax.reduce_precision(bias, exponent_bits=8, mantissa_bits=7)
+    bias_rest = bias - bias_hi
+    bias_mid = lax.reduce_precision(bias_rest, exponent_bits=8, mantissa_bits=7)
+    bias_lo = bias_rest - bias_mid
+    bias_parts = jnp.stack([bias_hi, bias_mid, bias_lo]).astype(BF16)
+    payload = jnp.concatenate([upstream, w_self, w_neigh, bias_parts], 0)
+    got = gather_all(payload, "feat")
+    up_all = got[:, :rows_here]
+    ws_all = got[:, rows_here : rows_here + feat_in]
+    wn_all = got[:, rows_here + feat_in : rows_here + 2 * feat_in]
+    bias_all = jnp.sum(got[:, rows_here + 2 * feat_in :].astype(F32), axis=1)
+
     perturbed = (features.astype(F32) + perturb.astype(F32)).astype(BF16)
 
     send_flat = send_rows[0].reshape(halo_rows)
@@ -63,20 +75,20 @@
     gathered_sum = jnp.dot(counts.astype(BF16), table, preferred_element_type=F32)
     neighbor_mean = (gathered_sum / K).astype(BF16)
 
-    preact = jnp.dot(perturbed, w_self, preferred_element_type=F32)
-    preact = preact + jnp.dot(neighbor_mean, w_neigh, preferred_element_type=F32) + bias
+    preact = jnp.einsum("nc,fch->fnh", perturbed, ws_all, preferred_element_type=F32)
+    preact = preact + jnp.einsum("nc,fch->fnh", neighbor_mean, wn_all, preferred_element_type=F32)
+    preact = preact + bias_all[:, None, :]
     sigmoid_pre = jax.nn.sigmoid(preact)
-    grad_pre = (
-        upstream.astype(F32) * sigmoid_pre * (1.0 + preact * (1.0 - sigmoid_pre))
+    gp_all = (
+        up_all.astype(F32) * sigmoid_pre * (1.0 + preact * (1.0 - sigmoid_pre))
     ).astype(BF16)
+    grad_pre = lax.dynamic_index_in_dim(gp_all, column, 0, keepdims=False)
     part_self = contract_rows(perturbed, grad_pre)
     part_neigh = contract_rows(neighbor_mean, grad_pre)
 
-    payload = jnp.concatenate([grad_pre, w_self, w_neigh], 0)
-    got = gather_all(payload, "feat")
-    gp_all = got[:, :rows_here]
-    ws_all = got[:, rows_here : rows_here + feat_in]
-    wn_all = got[:, rows_here + feat_in :]
+    weight_flat = jnp.concatenate([part_self.reshape(-1), part_neigh.reshape(-1)])
+    weight_recv = lax.all_to_all(weight_flat.reshape(dom_count, -1), "dom", 0, 0, tiled=True)
+
     dims = (((0, 2), (0, 2)), ((), ()))
     own_grad = lax.dot_general(gp_all, ws_all, dims, preferred_element_type=F32)
     spread = lax.dot_general(gp_all, wn_all, dims, preferred_element_type=F32) / K
@@ -95,14 +107,13 @@
         0,
     )
 
-    weight_flat = jnp.concatenate([part_self.reshape(-1), part_neigh.reshape(-1)])
-    weight_chunks = weight_flat.reshape(dom_count, -1)
+    weight_part = jnp.sum(weight_recv, axis=0)
     hub_chunks = table_grad[rows_here + halo_rows :].reshape(dom_count, hub_dev * feat_in)
-    sent = jnp.concatenate([hub_chunks, weight_chunks], 1)
+    weight_rep = jnp.broadcast_to(weight_part[None], (dom_count, weight_part.shape[0]))
+    sent = jnp.concatenate([hub_chunks, weight_rep], 1)
     recv = lax.all_to_all(sent, "dom", 0, 0, tiled=True)
-    totals = jnp.sum(recv, axis=0)
-    hub_total = totals[: hub_dev * feat_in].reshape(hub_dev, feat_in)
-    weight_part = totals[hub_dev * feat_in :]
+    hub_total = jnp.sum(recv[:, : hub_dev * feat_in], axis=0).reshape(hub_dev, feat_in)
+    weights = recv[:, hub_dev * feat_in :].reshape(2, feat_in, hidden_here)
 
     grad_in = own_grad + table_grad[:rows_here]
     grad_in = grad_in + contract_rows(pick.astype(F32), returned, HIGH)
@@ -113,7 +124,6 @@
     own_perturb = lax.dynamic_slice_in_dim(perturb, column * slice_width, slice_width, 1).astype(F32)
     new_perturb = (own_perturb + 0.5 * own_cols / jnp.sqrt(mean_square + 1e-06)).astype(BF16)
 
-    weights = gather_all(weight_part, "dom").reshape(2, feat_in, hidden_here)
     return (new_perturb, weights[0], weights[1])
 
 

time: 131 us -> 129 us (0.985)
  starting transfers between devices: 66.1 us -> 61.8 us
  matrix products: 11 us -> 12.8 us
  waiting for transfers between devices: 34.4 us -> 35.8 us
    all_to_all x0 -> x1, waiting for transfers between devices: none -> 10.4 us  [per_device(): lax.all_to_all(weight_flat.reshape(dom_count, -1), 'dom', 0, 0, tiled=True)]
    all_to_all x3 -> x2, waiting for transfers between devices: 32 us -> 22.9 us  [gather_all(): out = lax.all_to_all(rep, axis, 0, 0, tiled=True)]
    all_to_all x3 -> x2, starting transfers between devices: 20.2 us -> 13 us  [gather_all(): out = lax.all_to_all(rep, axis, 0, 0, tiled=True)]
    all_to_all x0 -> x1, starting transfers between devices: none -> 6.75 us  [per_device(): lax.all_to_all(weight_flat.reshape(dom_count, -1), 'dom', 0, 0, tiled=True)]
    all_to_all x1, starting transfers between devices: 9.15 us -> 5.72 us  [per_device(): recv = lax.all_to_all(sent, 'dom', 0, 0, tiled=True)]
    dot_general x5, matrix products: 8.15 us -> 5.05 us  [contract_rows(): lax.dot_general(left, right, (((0,), (0,)), ((), ())), preferred_element_...]
    dot_general x2, matrix products: 0.54 us -> 3.5 us  [the longest x1 2.18 us: per_device(): jnp.einsum('nc,fch->fnh', neighbor_mean, wn_all, preferred_element_type=F32)]
    concatenate x0 -> x2, local copies, waits for them, and re-layouts: none -> 2.69 us  [the longest x1 2.68 us: per_device(): payload = jnp.concatenate([upstream, w_self, w_neigh, bias_parts], 0)]
  transfers between devices with their start and end apart: 12 -> 12, of which waited for: 4 -> 4; matrix products, arithmetic and copies ran while one was open for 12% -> 13% of each run, Pallas kernels for 0% -> 0%
where the time goes in v1:
time: 129 us; the launch traced here: 128 us
  starting transfers between devices  61.8 us (48%)
  waiting for transfers between devices  35.8 us (28%)
  matrix products  12.8 us (10%)
  local copies, waits for them, and re-layouts  9.56 us (7%)
  other arithmetic  6.59 us (5%)
    ppermute x8, starting transfers between devices, from_behind(): return lax.ppermute(x, axis, [(i, (i + by) % size) for i in range(size)])  36.4 us
    all_to_all x2, waiting for transfers between devices, gather_all(): out = lax.all_to_all(rep, axis, 0, 0, tiled=True)  22.9 us
    all_to_all x2, starting transfers between devices, gather_all(): out = lax.all_to_all(rep, axis, 0, 0, tiled=True)  13 us
    all_to_all x1, waiting for transfers between devices, per_device(): lax.all_to_all(weight_flat.reshape(dom_count, -1), 'dom', 0, 0, tiled=True)  10.4 us
    all_to_all x1, starting transfers between devices, per_device(): lax.all_to_all(weight_flat.reshape(dom_count, -1), 'dom', 0, 0, tiled=True)  6.75 us
    all_to_all x1, starting transfers between devices, per_device(): recv = lax.all_to_all(sent, 'dom', 0, 0, tiled=True)  5.72 us
    dot_general x5, matrix products, contract_rows(): lax.dot_general(left, right, (((0,), (0,)), ((), ())), preferred_element_...  5.05 us
    reduce_sum x1, other arithmetic, per_device(): counts = jnp.sum((neighbors[:, :, None] == t_iota).astype(F32), axis=1)  3.65 us
  transfers between devices with their start and end apart: 12, of which 4 were waited for; matrix products, arithmetic and copies ran while one was open for 13% of the time, Pallas kernels for 0%

profile of v1, /device:TPU:1, one launch (start us, length us, event | category | flops | bytes accessed | tf_op | source)
XLA Modules:
  0.0 127.6 jit_solution(6626524902932015628)
XLA Ops:
  0.6 0.8 eq.30
  1.4 1.0 constant_dynamic-update-slice_fusion.5
  2.4 0.3 convolution_convert_fusion
  2.7 14.4 %collective-permute-start = (bf16[56,128]{1,0:T(8,128)(2,1)S(1)}, bf16[56,128]{1,0:T(8,128)(2,1)S(1)}, u32[]{:S(2)}, u32[]{:S(2)}) collective-permute-start(bf16[56,128]{1,0:T(8,128)(2,1)S(1)} %get-tuple-element.23), channel_id=1, source_target_pairs={{0,504},{4,508},{8,0},{12,4},{16,8},{20,12},{24,16},{28,20},{32,24... | collective-permute-start | bytes 43016 | tf_op jit(solution)/shard_map/ppermute | solution.py:15
  17.1 2.9 %collective-permute-start.1 = (bf16[56,128]{1,0:T(8,128)(2,1)S(1)}, bf16[56,128]{1,0:T(8,128)(2,1)S(1)}, u32[]{:S(2)}, u32[]{:S(2)}) collective-permute-start(bf16[56,128]{1,0:T(8,128)(2,1)S(1)} %get-tuple-element.22), channel_id=1, source_target_pairs={{0,508},{4,0},{8,4},{12,8},{16,12},{20,16},{24,20},{28,24},{32,28}... | collective-permute-start | bytes 43016 | tf_op jit(solution)/shard_map/ppermute | solution.py:15
  19.9 2.7 %collective-permute-start.2 = (bf16[56,128]{1,0:T(8,128)(2,1)S(1)}, bf16[56,128]{1,0:T(8,128)(2,1)S(1)}, u32[]{:S(2)}, u32[]{:S(2)}) collective-permute-start(bf16[56,128]{1,0:T(8,128)(2,1)S(1)} %get-tuple-element.21), channel_id=1, source_target_pairs={{0,4},{4,8},{8,12},{12,16},{16,20},{20,24},{24,28},{28,32},{32,36}... | collective-permute-start | bytes 43016 | tf_op jit(solution)/shard_map/ppermute | solution.py:15
  22.6 1.9 %collective-permute-start.3 = (bf16[56,128]{1,0:T(8,128)(2,1)S(1)}, bf16[56,128]{1,0:T(8,128)(2,1)S(1)}, u32[]{:S(2)}, u32[]{:S(2)}) collective-permute-start(bf16[56,128]{1,0:T(8,128)(2,1)S(1)} %get-tuple-element.20), channel_id=1, source_target_pairs={{0,8},{4,12},{8,16},{12,20},{16,24},{20,28},{24,32},{28,36},{32,40... | collective-permute-start | bytes 43016 | tf_op jit(solution)/shard_map/ppermute | solution.py:15
  24.6 0.8 convolution_convert_fusion.1
  25.4 0.7 broadcast_in_dim.7
  26.1 8.6 %all-to-all-start.1 = ((bf16[128,2,128]{2,1,0:T(2,128)(2,1)}), bf16[128,2,128]{2,1,0:T(2,128)(2,1)S(1)}, u32[]{:S(2)}, u32[]{:S(2)}) async-start(bf16[128,2,128]{2,1,0:T(2,128)(2,1)} %broadcast_in_dim.7), calls=%async_computation.1 | async-start | bytes 131072 | tf_op jit(solution)/shard_map/all_to_all | solution.py:31
  34.7 0.7 fusion.36
  35.4 2.7 %concatenate.21 = bf16[707,256]{1,0:T(8,128)(2,1)S(1)} concatenate(bf16[448,256]{1,0:T(8,128)(2,1)} %param.14, bf16[128,256]{1,0:T(8,128)(2,1)} %param.11, bf16[128,256]{1,0:T(8,128)(2,1)} %param.12, bf16[1,256]{1,0:T(2,128)(2,1)S(1)} %stack.14, bf16[1,256]{1,0:T(2,128)(2,1)S(1)} %stack.15, bf16[1,256]{1,0:T(2,128)(2,1)S(1)} %stack.16), dimensions={0} | concatenate | bytes 723968 | tf_op jit(solution)/shard_map/concatenate | solution.py:52
  38.1 8.0 %all-to-all-done.1 = bf16[128,2,128]{2,1,0:T(2,128)(2,1)S(1)} async-done(((bf16[128,2,128]{2,1,0:T(2,128)(2,1)}), bf16[128,2,128]{2,1,0:T(2,128)(2,1)S(1)}, u32[]{:S(2)}, u32[]{:S(2)}) %all-to-all-start.1) | async-done | bytes 65568 | tf_op jit(solution)/shard_map/all_to_all | solution.py:31
  46.1 1.2 broadcast_in_dim.6
  47.3 4.4 %all-to-all-start = ((bf16[4,707,256]{2,1,0:T(8,128)(2,1)}), bf16[4,707,256]{2,1,0:T(8,128)(2,1)}, u32[]{:S(2)}, u32[]{:S(2)}) async-start(bf16[4,707,256]{2,1,0:T(8,128)(2,1)} %broadcast_in_dim.6), calls=%async_computation | async-start | bytes 2916352 | tf_op jit(solution)/shard_map/all_to_all | solution.py:31
  51.8 3.6 %convert_reduce_fusion = f32[448,928]{1,0:T(8,128)S(1)} fusion(s32[448,15]{0,1:T(8,128)S(1)} %copy-done.1), kind=kLoop, calls=%fused_computation | loop fusion | flops 18292736 | bytes 1689856 | tf_op jit(solution)/shard_map/reduce_sum | solution.py:74
  55.4 0.0 collective-permute-done.1
  55.5 0.0 collective-permute-done.2
  55.5 0.0 collective-permute-done.3
  55.5 0.4 fusion.9
  55.9 14.9 %all-to-all-done = bf16[4,707,256]{2,1,0:T(8,128)(2,1)} async-done(((bf16[4,707,256]{2,1,0:T(8,128)(2,1)}), bf16[4,707,256]{2,1,0:T(8,128)(2,1)}, u32[]{:S(2)}, u32[]{:S(2)}) %all-to-all-start) | async-done | bytes 1447968 | tf_op jit(solution)/shard_map/all_to_all | solution.py:31
  70.8 1.3 %fusion.14 = f32[4,256,448]{1,2,0:T(8,128)S(1)} fusion(bf16[4,707,256]{2,1,0:T(8,128)(2,1)} %all-to-all-done, bf16[448,128]{1,0:T(8,128)(2,1)S(1)} %get-tuple-element.13), kind=kOutput, calls=%fused_computation.28 | convolution fusion | flops 117440512 | bytes 2211840 | tf_op jit(solution)/shard_map/nc,fch->fnh/dot_general | solution.py:78
  72.1 0.7 convert_reduce_fusion.1
  72.9 2.2 %fusion.5 = bf16[4,448,256]{2,1,0:T(8,128)(2,1)S(1)} fusion(f32[4,256,448]{1,2,0:T(8,128)S(1)} %fusion.14, bf16[4,707,256]{2,1,0:T(8,128)(2,1)} %all-to-all-done, f32[4,256]{1,0:T(4,128)S(1)} %convert_reduce_fusion.1, bf16[448,128]{1,0:T(8,128)(2,1)S(1)} %fusion.9), kind=kOutput, calls=%fused_computation.9 | convolution fusion | flops 122945536 | bytes 4050944 | tf_op jit(solution)/shard_map/nc,fch->fnh/dot_general | solution.py:79
  75.1 0.2 fusion.16
  75.3 0.2 fusion.18
  75.7 0.9 all_to_all.27
  76.5 6.8 %all-to-all-start.2 = ((f32[128,1,512]{2,1,0:T(1,128)}), f32[128,1,512]{2,1,0:T(1,128)S(1)}, u32[]{:S(2)}, u32[]{:S(2)}) async-start(f32[128,1,512]{2,1,0:T(1,128)} %all_to_all.27), calls=%async_computation.2 | async-start | bytes 524288 | tf_op jit(solution)/shard_map/all_to_all | solution.py:90
  83.3 1.4 %fusion.7 = f32[448,128]{1,0:T(8,128)S(1)} fusion(bf16[4,448,256]{2,1,0:T(8,128)(2,1)S(1)} %fusion.5, bf16[4,707,256]{2,1,0:T(8,128)(2,1)} %all-to-all-done), kind=kOutput, calls=%fused_computation.13 | convolution fusion | flops 117497856 | bytes 1409024 | tf_op jit(solution)/shard_map/dot_general | solution.py:94
  84.7 3.4 %fusion.44 = f32[928,128]{1,0:T(8,128)S(1)} fusion(f32[448,928]{1,0:T(8,128)S(1)} %convert_reduce_fusion, f32[448,128]{1,0:T(8,128)S(1)} %fusion.7), kind=kOutput, calls=%fused_computation.75 | convolution fusion | flops 638582784 | bytes 2367488 | tf_op jit(solution)/shard_map/dot_general | solution.py:23
  88.1 10.4 %all-to-all-done.2 = f32[128,1,512]{2,1,0:T(1,128)S(1)} async-done(((f32[128,1,512]{2,1,0:T(1,128)}), f32[128,1,512]{2,1,0:T(1,128)S(1)}, u32[]{:S(2)}, u32[]{:S(2)}) %all-to-all-start.2) | async-done | bytes 262176 | tf_op jit(solution)/shard_map/all_to_all | solution.py:90
  98.5 0.2 reduce_sum.47
  98.8 1.0 all_to_all.29
  99.8 5.7 %all-to-all-start.3 = ((f32[128,1,768]{2,1,0:T(1,128)}), f32[128,1,768]{2,1,0:T(1,128)S(1)}, u32[]{:S(2)}, u32[]{:S(2)}) async-start(f32[128,1,768]{2,1,0:T(1,128)} %all_to_all.29), calls=%async_computation.3 | async-start | bytes 786432 | tf_op jit(solution)/shard_map/all_to_all | solution.py:114
  105.5 0.0 copy-start.2
  105.6 3.3 %collective-permute-start.4 = (f32[56,128]{1,0:T(8,128)S(1)}, f32[56,128]{1,0:T(8,128)S(1)}, u32[]{:S(2)}, u32[]{:S(2)}) collective-permute-start(f32[56,128]{1,0:T(8,128)S(1)} %get-tuple-element.14), channel_id=1, source_target_pairs={{0,8},{4,12},{8,16},{12,20},{16,24},{20,28},{24,32},{28,36},{32,40... | collective-permute-start | bytes 86024 | tf_op jit(solution)/shard_map/ppermute | solution.py:15
  108.8 3.7 %collective-permute-start.5 = (f32[56,128]{1,0:T(8,128)S(1)}, f32[56,128]{1,0:T(8,128)S(1)}, u32[]{:S(2)}, u32[]{:S(2)}) collective-permute-start(f32[56,128]{1,0:T(8,128)S(1)} %get-tuple-element.17), channel_id=1, source_target_pairs={{0,4},{4,8},{8,12},{12,16},{16,20},{20,24},{24,28},{28,32},{32,36}... | collective-permute-start | bytes 86024 | tf_op jit(solution)/shard_map/ppermute | solution.py:15
  112.5 1.9 %collective-permute-start.6 = (f32[56,128]{1,0:T(8,128)S(1)}, f32[56,128]{1,0:T(8,128)S(1)}, u32[]{:S(2)}, u32[]{:S(2)}) collective-permute-start(f32[56,128]{1,0:T(8,128)S(1)} %get-tuple-element.16), channel_id=1, source_target_pairs={{0,508},{4,0},{8,4},{12,8},{16,12},{20,16},{24,20},{28,24},{32,28}... | collective-permute-start | bytes 86024 | tf_op jit(solution)/shard_map/ppermute | solution.py:15
  114.4 0.0 copy-start
  114.5 5.6 %collective-permute-start.7 = (f32[56,128]{1,0:T(8,128)S(1)}, f32[56,128]{1,0:T(8,128)S(1)}, u32[]{:S(2)}, u32[]{:S(2)}) collective-permute-start(f32[56,128]{1,0:T(8,128)S(1)} %get-tuple-element.15), channel_id=1, source_target_pairs={{0,504},{4,508},{8,0},{12,4},{16,8},{20,12},{24,16},{28,20},{32,24... | collective-permute-start | bytes 86024 | tf_op jit(solution)/shard_map/ppermute | solution.py:15
  120.1 1.4 %fusion.8 = f32[448,128]{1,0:T(8,128)S(1)} fusion(bf16[4,448,256]{2,1,0:T(8,128)(2,1)S(1)} %fusion.5, bf16[4,707,256]{2,1,0:T(8,128)(2,1)} %all-to-all-done, f32[928,128]{1,0:T(8,128)S(1)} %fusion.44), kind=kOutput, calls=%fused_computation.16 | convolution fusion | flops 117497856 | bytes 1638400 | tf_op jit(solution)/shard_map/dot_general | solution.py:93
  121.5 2.5 %all-to-all-done.3 = f32[128,1,768]{2,1,0:T(1,128)S(1)} async-done(((f32[128,1,768]{2,1,0:T(1,128)}), f32[128,1,768]{2,1,0:T(1,128)S(1)}, u32[]{:S(2)}, u32[]{:S(2)}) %all-to-all-start.3) | async-done | bytes 393248 | tf_op jit(solution)/shard_map/all_to_all | solution.py:114
  124.0 0.4 fusion.33
  124.5 0.8 multiply_reduce_fusion
  125.3 0.2 add_convert_fusion
  125.5 0.7 copy.16
  126.2 0.7 squeeze.11
  126.9 0.7 squeeze.12
  (30 shorter events, 0.4 us)
Async XLA Ops:
  2.7 52.7 %collective-permute-start = (bf16[56,128]{1,0:T(8,128)(2,1)S(1)}, bf16[56,128]{1,0:T(8,128)(2,1)S(1)}, u32[]{:S(2)}, u32[]{:S(2)}) collective-permute-start(bf16[56,128]{1,0:T(8,128)(2,1)S(1)} %get-tuple-element.23), channel_id=1, source_target_pairs={{0,504},{4,508},{8,0},{12,4},{16,8},{20,12},{24,16},{28,20},{32,24... | collective-permute-start | bytes 43016 | tf_op jit(solution)/shard_map/ppermute | solution.py:15
  17.1 38.4 %collective-permute-start.1 = (bf16[56,128]{1,0:T(8,128)(2,1)S(1)}, bf16[56,128]{1,0:T(8,128)(2,1)S(1)}, u32[]{:S(2)}, u32[]{:S(2)}) collective-permute-start(bf16[56,128]{1,0:T(8,128)(2,1)S(1)} %get-tuple-element.22), channel_id=1, source_target_pairs={{0,508},{4,0},{8,4},{12,8},{16,12},{20,16},{24,20},{28,24},{32,28}... | collective-permute-start | bytes 43016 | tf_op jit(solution)/shard_map/ppermute | solution.py:15
  19.9 35.5 %collective-permute-start.2 = (bf16[56,128]{1,0:T(8,128)(2,1)S(1)}, bf16[56,128]{1,0:T(8,128)(2,1)S(1)}, u32[]{:S(2)}, u32[]{:S(2)}) collective-permute-start(bf16[56,128]{1,0:T(8,128)(2,1)S(1)} %get-tuple-element.21), channel_id=1, source_target_pairs={{0,4},{4,8},{8,12},{12,16},{16,20},{20,24},{24,28},{28,32},{32,36}... | collective-permute-start | bytes 43016 | tf_op jit(solution)/shard_map/ppermute | solution.py:15
  22.6 32.8 %collective-permute-start.3 = (bf16[56,128]{1,0:T(8,128)(2,1)S(1)}, bf16[56,128]{1,0:T(8,128)(2,1)S(1)}, u32[]{:S(2)}, u32[]{:S(2)}) collective-permute-start(bf16[56,128]{1,0:T(8,128)(2,1)S(1)} %get-tuple-element.20), channel_id=1, source_target_pairs={{0,8},{4,12},{8,16},{12,20},{16,24},{20,28},{24,32},{28,36},{32,40... | collective-permute-start | bytes 43016 | tf_op jit(solution)/shard_map/ppermute | solution.py:15
  26.1 20.0 %all-to-all-start.1 = ((bf16[128,2,128]{2,1,0:T(2,128)(2,1)}), bf16[128,2,128]{2,1,0:T(2,128)(2,1)S(1)}, u32[]{:S(2)}, u32[]{:S(2)}) async-start(bf16[128,2,128]{2,1,0:T(2,128)(2,1)} %broadcast_in_dim.7), calls=%async_computation.1 | async-start | bytes 131072 | tf_op jit(solution)/shard_map/all_to_all | solution.py:31
  47.3 4.5 %copy-start.1 = (s32[448,15]{0,1:T(8,128)S(1)}, s32[448,15]{0,1:T(8,128)}, u32[]{:S(2)}) copy-start(s32[448,15]{0,1:T(8,128)} %param.17) | copy-start | bytes 80644
  47.3 23.5 %all-to-all-start = ((bf16[4,707,256]{2,1,0:T(8,128)(2,1)}), bf16[4,707,256]{2,1,0:T(8,128)(2,1)}, u32[]{:S(2)}, u32[]{:S(2)}) async-start(bf16[4,707,256]{2,1,0:T(8,128)(2,1)} %broadcast_in_dim.6), calls=%async_computation | async-start | bytes 2916352 | tf_op jit(solution)/shard_map/all_to_all | solution.py:31
  76.5 22.0 %all-to-all-start.2 = ((f32[128,1,512]{2,1,0:T(1,128)}), f32[128,1,512]{2,1,0:T(1,128)S(1)}, u32[]{:S(2)}, u32[]{:S(2)}) async-start(f32[128,1,512]{2,1,0:T(1,128)} %all_to_all.27), calls=%async_computation.2 | async-start | bytes 524288 | tf_op jit(solution)/shard_map/all_to_all | solution.py:90
  99.8 24.1 %all-to-all-start.3 = ((f32[128,1,768]{2,1,0:T(1,128)}), f32[128,1,768]{2,1,0:T(1,128)S(1)}, u32[]{:S(2)}, u32[]{:S(2)}) async-start(f32[128,1,768]{2,1,0:T(1,128)} %all_to_all.29), calls=%async_computation.3 | async-start | bytes 786432 | tf_op jit(solution)/shard_map/all_to_all | solution.py:114
  105.5 18.5 %copy-start.2 = (s32[1,2]{1,0:T(1,128)S(1)}, s32[1,2]{1,0:T(1,128)}, u32[]{:S(2)}) copy-start(s32[1,2]{1,0:T(1,128)} %param.15) | copy-start | bytes 28
  105.6 18.9 %collective-permute-start.4 = (f32[56,128]{1,0:T(8,128)S(1)}, f32[56,128]{1,0:T(8,128)S(1)}, u32[]{:S(2)}, u32[]{:S(2)}) collective-permute-start(f32[56,128]{1,0:T(8,128)S(1)} %get-tuple-element.14), channel_id=1, source_target_pairs={{0,8},{4,12},{8,16},{12,20},{16,24},{20,28},{24,32},{28,36},{32,40... | collective-permute-start | bytes 86024 | tf_op jit(solution)/shard_map/ppermute | solution.py:15
  108.8 15.6 %collective-permute-start.5 = (f32[56,128]{1,0:T(8,128)S(1)}, f32[56,128]{1,0:T(8,128)S(1)}, u32[]{:S(2)}, u32[]{:S(2)}) collective-permute-start(f32[56,128]{1,0:T(8,128)S(1)} %get-tuple-element.17), channel_id=1, source_target_pairs={{0,4},{4,8},{8,12},{12,16},{16,20},{20,24},{24,28},{28,32},{32,36}... | collective-permute-start | bytes 86024 | tf_op jit(solution)/shard_map/ppermute | solution.py:15
  112.5 12.0 %collective-permute-start.6 = (f32[56,128]{1,0:T(8,128)S(1)}, f32[56,128]{1,0:T(8,128)S(1)}, u32[]{:S(2)}, u32[]{:S(2)}) collective-permute-start(f32[56,128]{1,0:T(8,128)S(1)} %get-tuple-element.16), channel_id=1, source_target_pairs={{0,508},{4,0},{8,4},{12,8},{16,12},{20,16},{24,20},{28,24},{32,28}... | collective-permute-start | bytes 86024 | tf_op jit(solution)/shard_map/ppermute | solution.py:15
  114.4 10.9 %copy-start = (bf16[448,128]{1,0:T(8,128)(2,1)S(1)}, bf16[448,128]{1,0:T(8,128)(2,1)}, u32[]{:S(2)}) copy-start(bf16[448,128]{1,0:T(8,128)(2,1)} %param.10) | copy-start | bytes 344068
  114.5 10.1 %collective-permute-start.7 = (f32[56,128]{1,0:T(8,128)S(1)}, f32[56,128]{1,0:T(8,128)S(1)}, u32[]{:S(2)}, u32[]{:S(2)}) collective-permute-start(f32[56,128]{1,0:T(8,128)S(1)} %get-tuple-element.15), channel_id=1, source_target_pairs={{0,504},{4,508},{8,0},{12,4},{16,8},{20,12},{24,16},{28,20},{32,24... | collective-permute-start | bytes 86024 | tf_op jit(solution)/shard_map/ppermute | solution.py:15

commit v2 on v0

--- a/solution.py
+++ b/solution.py
@@ -2,6 +2,7 @@
 import jax.numpy as jnp
 from jax import lax
 from jax.sharding import PartitionSpec as P
+
 
 K = 15
 NOFF = 4
@@ -53,13 +54,15 @@
     hub_out = jnp.dot(hub_pick.astype(BF16), perturbed, preferred_element_type=F32).astype(BF16)
 
     pieces = [
-        from_behind(halo_out[o * slots : (o + 1) * slots], "dom", offset_of(o)) for o in range(NOFF)
+        from_behind(halo_out[o * slots : (o + 1) * slots], "dom", offset_of(o))
+        for o in range(NOFF)
     ]
+    t_iota = lax.broadcasted_iota(jnp.int32, (rows_here, K, table_rows), 2)
+    counts = jnp.sum((neighbors[:, :, None] == t_iota).astype(F32), axis=1)
+    hub_out, counts = lax.optimization_barrier((hub_out, counts))
+
     hubs = gather_all(hub_out, "dom").reshape(dom_count * hub_dev, feat_in)
     table = jnp.concatenate([perturbed] + pieces + [hubs], 0)
-
-    t_iota = lax.broadcasted_iota(jnp.int32, (rows_here, K, table_rows), 2)
-    counts = jnp.sum((neighbors[:, :, None] == t_iota).astype(F32), axis=1)
     gathered_sum = jnp.dot(counts.astype(BF16), table, preferred_element_type=F32)
     neighbor_mean = (gathered_sum / K).astype(BF16)
 
@@ -69,11 +72,17 @@
     grad_pre = (
         upstream.astype(F32) * sigmoid_pre * (1.0 + preact * (1.0 - sigmoid_pre))
     ).astype(BF16)
+
+    payload = jnp.concatenate([grad_pre, w_self, w_neigh], 0)
+    got = jnp.stack(
+        [payload] + [from_behind(payload, "feat", shift) for shift in range(1, feat_count)]
+    )
+
     part_self = contract_rows(perturbed, grad_pre)
     part_neigh = contract_rows(neighbor_mean, grad_pre)
+    weight_flat = jnp.concatenate([part_self.reshape(-1), part_neigh.reshape(-1)])
+    weight_recv = lax.all_to_all(weight_flat.reshape(dom_count, -1), "dom", 0, 0, tiled=True)
 
-    payload = jnp.concatenate([grad_pre, w_self, w_neigh], 0)
-    got = gather_all(payload, "feat")
     gp_all = got[:, :rows_here]
     ws_all = got[:, rows_here : rows_here + feat_in]
     wn_all = got[:, rows_here + feat_in :]
@@ -95,14 +104,13 @@
         0,
     )
 
-    weight_flat = jnp.concatenate([part_self.reshape(-1), part_neigh.reshape(-1)])
-    weight_chunks = weight_flat.reshape(dom_count, -1)
+    weight_part = jnp.sum(weight_recv, axis=0)
     hub_chunks = table_grad[rows_here + halo_rows :].reshape(dom_count, hub_dev * feat_in)
-    sent = jnp.concatenate([hub_chunks, weight_chunks], 1)
+    weight_rep = jnp.broadcast_to(weight_part[None], (dom_count, weight_part.shape[0]))
+    sent = jnp.concatenate([hub_chunks, weight_rep], 1)
     recv = lax.all_to_all(sent, "dom", 0, 0, tiled=True)
-    totals = jnp.sum(recv, axis=0)
-    hub_total = totals[: hub_dev * feat_in].reshape(hub_dev, feat_in)
-    weight_part = totals[hub_dev * feat_in :]
+    hub_total = jnp.sum(recv[:, : hub_dev * feat_in], axis=0).reshape(hub_dev, feat_in)
+    weights = recv[:, hub_dev * feat_in :].reshape(2, feat_in, hidden_here)
 
     grad_in = own_grad + table_grad[:rows_here]
     grad_in = grad_in + contract_rows(pick.astype(F32), returned, HIGH)
@@ -113,7 +121,6 @@
     own_perturb = lax.dynamic_slice_in_dim(perturb, column * slice_width, slice_width, 1).astype(F32)
     new_perturb = (own_perturb + 0.5 * own_cols / jnp.sqrt(mean_square + 1e-06)).astype(BF16)
 
-    weights = gather_all(weight_part, "dom").reshape(2, feat_in, hidden_here)
     return (new_perturb, weights[0], weights[1])
 
 
@@ -130,6 +137,5 @@
         P("dom", None),
     )
     out_specs = (P("dom", "feat"), P(None, "feat"), P(None, "feat"))
-    return jax.shard_map(
-        per_device, mesh=mesh, in_specs=in_specs, out_specs=out_specs, check_vma=False
-    )
+
+    return jax.shard_map(per_device, mesh=mesh, in_specs=in_specs, out_specs=out_specs, check_vma=False)

time: 131 us -> 121 us (0.924)
  waiting for transfers between devices: 34.4 us -> 18.9 us
  starting transfers between devices: 66.1 us -> 70.1 us
  other arithmetic: 6.56 us -> 9.98 us
    all_to_all x3 -> x1, waiting for transfers between devices: 32 us -> 11.1 us  [gather_all(): out = lax.all_to_all(rep, axis, 0, 0, tiled=True)]
    all_to_all x3 -> x1, starting transfers between devices: 20.2 us -> 10.2 us  [gather_all(): out = lax.all_to_all(rep, axis, 0, 0, tiled=True)]
    ppermute x8 -> x11, starting transfers between devices: 36.8 us -> 46.8 us  [from_behind(): return lax.ppermute(x, axis, [(i, (i + by) % size) for i in range(size)])]
    all_to_all x0 -> x1, starting transfers between devices: none -> 6.56 us  [per_device(): lax.all_to_all(weight_flat.reshape(dom_count, -1), 'dom', 0, 0, tiled=True)]
    all_to_all x0 -> x1, waiting for transfers between devices: none -> 4.92 us  [per_device(): lax.all_to_all(weight_flat.reshape(dom_count, -1), 'dom', 0, 0, tiled=True)]
    all_to_all x1, starting transfers between devices: 9.15 us -> 6.57 us  [per_device(): recv = lax.all_to_all(sent, 'dom', 0, 0, tiled=True)]
    another operation x0 -> x2, other arithmetic: none -> 2.53 us  [per_device(): jnp.stack([payload] + [from_behind(payload, 'feat', shift) for shift in r...]
    concatenate x2, local copies, waits for them, and re-layouts: 2.54 us -> 0.08 us  [per_device(): jnp.concatenate([part_self.reshape(-1), part_neigh.reshape(-1)])]
  transfers between devices with their start and end apart: 12 -> 14, of which waited for: 4 -> 4; matrix products, arithmetic and copies ran while one was open for 12% -> 15% of each run, Pallas kernels for 0% -> 0%
where the time goes in v2:
time: 121 us; the launch traced here: 120 us
  starting transfers between devices  70.1 us (58%)
  waiting for transfers between devices  18.9 us (16%)
  matrix products  10.6 us (9%)
  other arithmetic  9.98 us (8%)
  local copies, waits for them, and re-layouts  9.52 us (8%)
    ppermute x11, starting transfers between devices, from_behind(): return lax.ppermute(x, axis, [(i, (i + by) % size) for i in range(size)])  46.8 us
    all_to_all x1, waiting for transfers between devices, gather_all(): out = lax.all_to_all(rep, axis, 0, 0, tiled=True)  11.1 us
    all_to_all x1, starting transfers between devices, gather_all(): out = lax.all_to_all(rep, axis, 0, 0, tiled=True)  10.2 us
    all_to_all x1, starting transfers between devices, per_device(): recv = lax.all_to_all(sent, 'dom', 0, 0, tiled=True)  6.57 us
    all_to_all x1, starting transfers between devices, per_device(): lax.all_to_all(weight_flat.reshape(dom_count, -1), 'dom', 0, 0, tiled=True)  6.56 us
    dot_general x5, matrix products, contract_rows(): lax.dot_general(left, right, (((0,), (0,)), ((), ())), preferred_element_...  5.84 us
    reduce_sum x1, other arithmetic, per_device(): counts = jnp.sum((neighbors[:, :, None] == t_iota).astype(F32), axis=1)  5.01 us
    all_to_all x1, waiting for transfers between devices, per_device(): lax.all_to_all(weight_flat.reshape(dom_count, -1), 'dom', 0, 0, tiled=True)  4.92 us
  transfers between devices with their start and end apart: 14, of which 4 were waited for; matrix products, arithmetic and copies ran while one was open for 15% of the time, Pallas kernels for 0%

profile of v2, /device:TPU:1, one launch (start us, length us, event | category | flops | bytes accessed | tf_op | source)
XLA Modules:
  0.0 120.2 jit_solution(10960296933532005678)
XLA Ops:
  0.6 0.8 eq.33
  1.4 1.0 constant_dynamic-update-slice_fusion.5
  2.4 0.3 convolution_convert_fusion
  2.7 4.0 %collective-permute-start.3 = (bf16[56,128]{1,0:T(8,128)(2,1)S(1)}, bf16[56,128]{1,0:T(8,128)(2,1)S(1)}, u32[]{:S(2)}, u32[]{:S(2)}) collective-permute-start(bf16[56,128]{1,0:T(8,128)(2,1)S(1)} %get-tuple-element.26), channel_id=1, source_target_pairs={{0,8},{4,12},{8,16},{12,20},{16,24},{20,28},{24,32},{28,36},{32,40... | collective-permute-start | bytes 43016 | tf_op jit(solution)/shard_map/ppermute | solution.py:16
  6.7 4.0 %collective-permute-start.2 = (bf16[56,128]{1,0:T(8,128)(2,1)S(1)}, bf16[56,128]{1,0:T(8,128)(2,1)S(1)}, u32[]{:S(2)}, u32[]{:S(2)}) collective-permute-start(bf16[56,128]{1,0:T(8,128)(2,1)S(1)} %get-tuple-element.27), channel_id=1, source_target_pairs={{0,4},{4,8},{8,12},{12,16},{16,20},{20,24},{24,28},{28,32},{32,36}... | collective-permute-start | bytes 43016 | tf_op jit(solution)/shard_map/ppermute | solution.py:16
  10.8 4.5 %collective-permute-start.1 = (bf16[56,128]{1,0:T(8,128)(2,1)S(1)}, bf16[56,128]{1,0:T(8,128)(2,1)S(1)}, u32[]{:S(2)}, u32[]{:S(2)}) collective-permute-start(bf16[56,128]{1,0:T(8,128)(2,1)S(1)} %get-tuple-element.28), channel_id=1, source_target_pairs={{0,508},{4,0},{8,4},{12,8},{16,12},{20,16},{24,20},{28,24},{32,28}... | collective-permute-start | bytes 43016 | tf_op jit(solution)/shard_map/ppermute | solution.py:16
  15.3 8.2 %collective-permute-start = (bf16[56,128]{1,0:T(8,128)(2,1)S(1)}, bf16[56,128]{1,0:T(8,128)(2,1)S(1)}, u32[]{:S(2)}, u32[]{:S(2)}) collective-permute-start(bf16[56,128]{1,0:T(8,128)(2,1)S(1)} %get-tuple-element.29), channel_id=1, source_target_pairs={{0,504},{4,508},{8,0},{12,4},{16,8},{20,12},{24,16},{28,20},{32,24... | collective-permute-start | bytes 43016 | tf_op jit(solution)/shard_map/ppermute | solution.py:16
  23.6 0.8 convolution_convert_fusion.1
  24.4 5.0 %convert_reduce_fusion = f32[448,928]{1,0:T(8,128)S(1)} fusion(s32[448,15]{0,1:T(8,128)} %param.17), kind=kLoop, calls=%fused_computation | loop fusion | flops 18292736 | bytes 1689856 | tf_op jit(solution)/shard_map/reduce_sum | solution.py:61
  29.4 0.7 broadcast_in_dim.4
  30.1 10.2 %all-to-all-start = ((bf16[128,2,128]{2,1,0:T(2,128)(2,1)}), bf16[128,2,128]{2,1,0:T(2,128)(2,1)S(1)}, u32[]{:S(2)}, u32[]{:S(2)}) async-start(bf16[128,2,128]{2,1,0:T(2,128)(2,1)} %broadcast_in_dim.4), calls=%async_computation | async-start | bytes 131072 | tf_op jit(solution)/shard_map/all_to_all | solution.py:32
  40.3 0.2 fusion.42
  40.6 11.1 %all-to-all-done = bf16[128,2,128]{2,1,0:T(2,128)(2,1)S(1)} async-done(((bf16[128,2,128]{2,1,0:T(2,128)(2,1)}), bf16[128,2,128]{2,1,0:T(2,128)(2,1)S(1)}, u32[]{:S(2)}, u32[]{:S(2)}) %all-to-all-start) | async-done | bytes 65568 | tf_op jit(solution)/shard_map/all_to_all | solution.py:32
  51.7 0.4 fusion.4
  52.2 1.3 %multiply_convert_fusion = bf16[448,256]{1,0:T(8,128)(2,1)S(1)} fusion(f32[448,256]{1,0:T(8,128)S(1)} %fusion.42, bf16[448,128]{1,0:T(8,128)(2,1)S(1)} %fusion.4, bf16[128,256]{1,0:T(8,128)(2,1)S(1)} %copy-done.14, bf16[448,256]{1,0:T(8,128)(2,1)} %param.14, f32[256]{0:T(256)S(1)} %copy-done.16), kind=kOutput, calls=%fused_computation.18 | convolution fusion | flops 30736384 | bytes 1098752 | tf_op jit(solution)/shard_map/dot_general | solution.py:70
  53.4 0.9 fusion.38
  54.4 4.6 %collective-permute-start.5 = (bf16[704,256]{1,0:T(8,128)(2,1)}, bf16[704,256]{1,0:T(8,128)(2,1)S(1)}, u32[]{:S(2)}, u32[]{:S(2)}) collective-permute-start(bf16[704,256]{1,0:T(8,128)(2,1)} %get-tuple-element.25), channel_id=1, source_target_pairs={{0,2},{1,3},{2,0},{3,1},{4,6},{5,7},{6,4},{7,5},{8,10},{9,11},{10,... | collective-permute-start | bytes 1081352 | tf_op jit(solution)/shard_map/ppermute | solution.py:16
  59.0 2.2 %collective-permute-start.4 = (bf16[704,256]{1,0:T(8,128)(2,1)}, bf16[704,256]{1,0:T(8,128)(2,1)S(1)}, u32[]{:S(2)}, u32[]{:S(2)}) collective-permute-start(bf16[704,256]{1,0:T(8,128)(2,1)} %get-tuple-element.25), channel_id=1, source_target_pairs={{0,1},{1,2},{2,3},{3,0},{4,5},{5,6},{6,7},{7,4},{8,9},{9,10},{10,1... | collective-permute-start | bytes 1081352 | tf_op jit(solution)/shard_map/ppermute | solution.py:16
  61.2 4.3 %collective-permute-start.6 = (bf16[704,256]{1,0:T(8,128)(2,1)}, bf16[704,256]{1,0:T(8,128)(2,1)S(1)}, u32[]{:S(2)}, u32[]{:S(2)}) collective-permute-start(bf16[704,256]{1,0:T(8,128)(2,1)} %get-tuple-element.25), channel_id=1, source_target_pairs={{0,3},{1,0},{2,1},{3,2},{4,7},{5,4},{6,5},{7,6},{8,11},{9,8},{10,9... | collective-permute-start | bytes 1081352 | tf_op jit(solution)/shard_map/ppermute | solution.py:16
  65.5 0.2 fusion.45
  65.8 0.2 fusion.44
  66.1 0.9 all_to_all.22
  67.0 6.6 %all-to-all-start.1 = ((f32[128,1,512]{2,1,0:T(1,128)}), f32[128,1,512]{2,1,0:T(1,128)S(1)}, u32[]{:S(2)}, u32[]{:S(2)}) async-start(f32[128,1,512]{2,1,0:T(1,128)} %all_to_all.22), calls=%async_computation.1 | async-start | bytes 524288 | tf_op jit(solution)/shard_map/all_to_all | solution.py:84
  73.6 2.4 %collective-permute-done.4 = bf16[704,256]{1,0:T(8,128)(2,1)S(1)} collective-permute-done((bf16[704,256]{1,0:T(8,128)(2,1)}, bf16[704,256]{1,0:T(8,128)(2,1)S(1)}, u32[]{:S(2)}, u32[]{:S(2)}) %collective-permute-start.4) | collective-permute-done | bytes 360480 | tf_op jit(solution)/shard_map/ppermute | solution.py:16
  76.0 0.8 copy-done.5
  76.9 1.6 %pad_maximum_fusion = bf16[4,704,256]{2,1,0:T(8,128)(2,1)S(1)} fusion(bf16[1,704,256]{2,1,0:T(8,128)(2,1)} %bitcast.40, bf16[1,704,256]{2,1,0:T(8,128)(2,1)} %bitcast.34, bf16[1,704,256]{2,1,0:T(8,128)(2,1)} %bitcast.37, bf16[1,704,256]{2,1,0:T(8,128)(2,1)} %get-tuple-element.24), kind=kLoop, calls=%fused_computation.2 | loop fusion | flops 2162688 | bytes 2883584 | tf_op jit(solution)/shard_map/stack | solution.py:77
  78.6 0.4 fusion.2
  79.0 3.4 %fusion.43 = f32[928,128]{1,0:T(8,128)S(1)} fusion(f32[448,928]{1,0:T(8,128)S(1)} %convert_reduce_fusion, f32[448,128]{1,0:T(8,128)S(1)} %fusion.2), kind=kOutput, calls=%fused_computation.71 | convolution fusion | flops 638582784 | bytes 2367488 | tf_op jit(solution)/shard_map/dot_general | solution.py:24
  82.4 0.8 copy-done.11
  83.3 0.7 reshape.46
  84.0 4.9 %all-to-all-done.1 = f32[128,1,512]{2,1,0:T(1,128)S(1)} async-done(((f32[128,1,512]{2,1,0:T(1,128)}), f32[128,1,512]{2,1,0:T(1,128)S(1)}, u32[]{:S(2)}, u32[]{:S(2)}) %all-to-all-start.1) | async-done | bytes 262176 | tf_op jit(solution)/shard_map/all_to_all | solution.py:84
  88.9 0.2 reduce_sum.37
  89.1 0.9 pad_maximum_fusion.1
  90.1 1.0 all_to_all.24
  91.1 6.6 %all-to-all-start.2 = ((f32[128,1,768]{2,1,0:T(1,128)}), f32[128,1,768]{2,1,0:T(1,128)S(1)}, u32[]{:S(2)}, u32[]{:S(2)}) async-start(f32[128,1,768]{2,1,0:T(1,128)} %all_to_all.24), calls=%async_computation.2 | async-start | bytes 786432 | tf_op jit(solution)/shard_map/all_to_all | solution.py:111
  97.7 1.4 %fusion.39 = (f32[56,128]{1,0:T(8,128)}, f32[56,128]{1,0:T(8,128)}, f32[56,128]{1,0:T(8,128)}, f32[56,128]{1,0:T(8,128)S(1)}) fusion(f32[928,128]{1,0:T(8,128)} %copy-done.11), kind=kLoop, calls=%fused_computation.67 | loop fusion | bytes 229376 | tf_op jit(solution)/shard_map/slice | solution.py:98
  99.1 3.3 %collective-permute-start.7 = (f32[56,128]{1,0:T(8,128)}, f32[56,128]{1,0:T(8,128)}, u32[]{:S(2)}, u32[]{:S(2)}) collective-permute-start(f32[56,128]{1,0:T(8,128)} %get-tuple-element.18), channel_id=1, source_target_pairs={{0,8},{4,12},{8,16},{12,20},{16,24},{20,28},{24,32},{28,36},{32,40... | collective-permute-start | bytes 86024 | tf_op jit(solution)/shard_map/ppermute | solution.py:16
  102.4 6.0 %collective-permute-start.10 = (f32[56,128]{1,0:T(8,128)}, f32[56,128]{1,0:T(8,128)}, u32[]{:S(2)}, u32[]{:S(2)}) collective-permute-start(f32[56,128]{1,0:T(8,128)} %get-tuple-element.19), channel_id=1, source_target_pairs={{0,504},{4,508},{8,0},{12,4},{16,8},{20,12},{24,16},{28,20},{32,24... | collective-permute-start | bytes 86024 | tf_op jit(solution)/shard_map/ppermute | solution.py:16
  108.4 2.7 %collective-permute-start.9 = (f32[56,128]{1,0:T(8,128)}, f32[56,128]{1,0:T(8,128)}, u32[]{:S(2)}, u32[]{:S(2)}) collective-permute-start(f32[56,128]{1,0:T(8,128)} %get-tuple-element.20), channel_id=1, source_target_pairs={{0,508},{4,0},{8,4},{12,8},{16,12},{20,16},{24,20},{28,24},{32,28}... | collective-permute-start | bytes 86024 | tf_op jit(solution)/shard_map/ppermute | solution.py:16
  111.1 2.8 %collective-permute-start.8 = (f32[56,128]{1,0:T(8,128)S(1)}, f32[56,128]{1,0:T(8,128)}, u32[]{:S(2)}, u32[]{:S(2)}) collective-permute-start(f32[56,128]{1,0:T(8,128)S(1)} %get-tuple-element.21), channel_id=1, source_target_pairs={{0,4},{4,8},{8,12},{12,16},{16,20},{20,24},{24,28},{28,32},{32,36}... | collective-permute-start | bytes 86024 | tf_op jit(solution)/shard_map/ppermute | solution.py:16
  114.0 1.3 %fusion.3 = f32[448,128]{1,0:T(8,128)S(1)} fusion(bf16[4,704,256]{2,1,0:T(8,128)(2,1)S(1)} %pad_maximum_fusion, bf16[1,704,256]{2,1,0:T(8,128)(2,1)S(1)} %bitcast.42, bf16[1,704,256]{2,1,0:T(8,128)(2,1)S(1)} %bitcast.36, bf16[1,704,256]{2,1,0:T(8,128)(2,1)S(1)} %bitcast.39, bf16[1,704,256]{2,1,0:T(8,128)(2,1)S(1)} %copy-done.1, f32[928,128]{1,0:T(8,128)} %copy-done.11), kind=kOutput, calls=%fused_computation.11 | convolution fusion | flops 118546432 | bytes 2818048 | tf_op jit(solution)/shard_map/dot_general | solution.py:90
  115.3 0.4 all-to-all-done.2
  115.9 0.4 fusion.31
  116.3 0.7 squeeze.7
  117.0 0.7 squeeze.6
  117.7 1.6 %multiply_reduce_fusion = (f32[448]{0:T(512)S(1)}, f32[448,128]{1,0:T(8,128)S(1)}) fusion(f32[448,128]{1,0:T(8,128)S(1)} %fusion.31, f32[448,128]{1,0:T(8,128)S(1)} %fusion.3, f32[56,128]{1,0:T(8,128)} %collective-permute-done.10, f32[56,128]{1,0:T(8,128)} %collective-permute-done.9, f32[56,128]{1,0:T(8,128)} %collective-permute-done.8, ...), kind=kOutput, calls=%fused_computation.39 | convolution fusion | flops 154555968 | bytes 805504 | tf_op jit(solution)/shard_map/dot_general | solution.py:24
  119.3 0.2 add_convert_fusion
  119.5 0.7 copy.16
  (57 shorter events, 0.5 us)
Async XLA Ops:
  1.4 38.9 %copy-start.13 = (bf16[128,256]{1,0:T(8,128)(2,1)S(1)}, bf16[128,256]{1,0:T(8,128)(2,1)}, u32[]{:S(2)}) copy-start(bf16[128,256]{1,0:T(8,128)(2,1)} %param.11) | copy-start | bytes 196612
  2.7 37.9 %collective-permute-start.3 = (bf16[56,128]{1,0:T(8,128)(2,1)S(1)}, bf16[56,128]{1,0:T(8,128)(2,1)S(1)}, u32[]{:S(2)}, u32[]{:S(2)}) collective-permute-start(bf16[56,128]{1,0:T(8,128)(2,1)S(1)} %get-tuple-element.26), channel_id=1, source_target_pairs={{0,8},{4,12},{8,16},{12,20},{16,24},{20,28},{24,32},{28,36},{32,40... | collective-permute-start | bytes 43016 | tf_op jit(solution)/shard_map/ppermute | solution.py:16
  6.7 33.8 %collective-permute-start.2 = (bf16[56,128]{1,0:T(8,128)(2,1)S(1)}, bf16[56,128]{1,0:T(8,128)(2,1)S(1)}, u32[]{:S(2)}, u32[]{:S(2)}) collective-permute-start(bf16[56,128]{1,0:T(8,128)(2,1)S(1)} %get-tuple-element.27), channel_id=1, source_target_pairs={{0,4},{4,8},{8,12},{12,16},{16,20},{20,24},{24,28},{28,32},{32,36}... | collective-permute-start | bytes 43016 | tf_op jit(solution)/shard_map/ppermute | solution.py:16
  10.8 29.8 %collective-permute-start.1 = (bf16[56,128]{1,0:T(8,128)(2,1)S(1)}, bf16[56,128]{1,0:T(8,128)(2,1)S(1)}, u32[]{:S(2)}, u32[]{:S(2)}) collective-permute-start(bf16[56,128]{1,0:T(8,128)(2,1)S(1)} %get-tuple-element.28), channel_id=1, source_target_pairs={{0,508},{4,0},{8,4},{12,8},{16,12},{20,16},{24,20},{28,24},{32,28}... | collective-permute-start | bytes 43016 | tf_op jit(solution)/shard_map/ppermute | solution.py:16
  15.3 25.2 %collective-permute-start = (bf16[56,128]{1,0:T(8,128)(2,1)S(1)}, bf16[56,128]{1,0:T(8,128)(2,1)S(1)}, u32[]{:S(2)}, u32[]{:S(2)}) collective-permute-start(bf16[56,128]{1,0:T(8,128)(2,1)S(1)} %get-tuple-element.29), channel_id=1, source_target_pairs={{0,504},{4,508},{8,0},{12,4},{16,8},{20,12},{24,16},{28,20},{32,24... | collective-permute-start | bytes 43016 | tf_op jit(solution)/shard_map/ppermute | solution.py:16
  30.1 21.6 %all-to-all-start = ((bf16[128,2,128]{2,1,0:T(2,128)(2,1)}), bf16[128,2,128]{2,1,0:T(2,128)(2,1)S(1)}, u32[]{:S(2)}, u32[]{:S(2)}) async-start(bf16[128,2,128]{2,1,0:T(2,128)(2,1)} %broadcast_in_dim.4), calls=%async_computation | async-start | bytes 131072 | tf_op jit(solution)/shard_map/all_to_all | solution.py:32
  40.3 11.8 %copy-start.14 = (bf16[128,256]{1,0:T(8,128)(2,1)S(1)}, bf16[128,256]{1,0:T(8,128)(2,1)}, u32[]{:S(2)}) copy-start(bf16[128,256]{1,0:T(8,128)(2,1)} %param.12) | copy-start | bytes 196612
  40.3 11.8 %copy-start.16 = (f32[256]{0:T(256)S(1)}, f32[256]{0:T(256)}, u32[]{:S(2)}) copy-start(f32[256]{0:T(256)} %param.13) | copy-start | bytes 3076
  54.4 19.2 %collective-permute-start.5 = (bf16[704,256]{1,0:T(8,128)(2,1)}, bf16[704,256]{1,0:T(8,128)(2,1)S(1)}, u32[]{:S(2)}, u32[]{:S(2)}) collective-permute-start(bf16[704,256]{1,0:T(8,128)(2,1)} %get-tuple-element.25), channel_id=1, source_target_pairs={{0,2},{1,3},{2,0},{3,1},{4,6},{5,7},{6,4},{7,5},{8,10},{9,11},{10,... | collective-permute-start | bytes 1081352 | tf_op jit(solution)/shard_map/ppermute | solution.py:16
  59.0 17.0 %collective-permute-start.4 = (bf16[704,256]{1,0:T(8,128)(2,1)}, bf16[704,256]{1,0:T(8,128)(2,1)S(1)}, u32[]{:S(2)}, u32[]{:S(2)}) collective-permute-start(bf16[704,256]{1,0:T(8,128)(2,1)} %get-tuple-element.25), channel_id=1, source_target_pairs={{0,1},{1,2},{2,3},{3,0},{4,5},{5,6},{6,7},{7,4},{8,9},{9,10},{10,1... | collective-permute-start | bytes 1081352 | tf_op jit(solution)/shard_map/ppermute | solution.py:16
  61.2 14.8 %collective-permute-start.6 = (bf16[704,256]{1,0:T(8,128)(2,1)}, bf16[704,256]{1,0:T(8,128)(2,1)S(1)}, u32[]{:S(2)}, u32[]{:S(2)}) collective-permute-start(bf16[704,256]{1,0:T(8,128)(2,1)} %get-tuple-element.25), channel_id=1, source_target_pairs={{0,3},{1,0},{2,1},{3,2},{4,7},{5,4},{6,5},{7,6},{8,11},{9,8},{10,9... | collective-permute-start | bytes 1081352 | tf_op jit(solution)/shard_map/ppermute | solution.py:16
  67.0 21.9 %all-to-all-start.1 = ((f32[128,1,512]{2,1,0:T(1,128)}), f32[128,1,512]{2,1,0:T(1,128)S(1)}, u32[]{:S(2)}, u32[]{:S(2)}) async-start(f32[128,1,512]{2,1,0:T(1,128)} %all_to_all.22), calls=%async_computation.1 | async-start | bytes 524288 | tf_op jit(solution)/shard_map/all_to_all | solution.py:84
  73.6 2.5 %copy-start.2 = (bf16[704,256]{1,0:T(8,128)(2,1)}, bf16[704,256]{1,0:T(8,128)(2,1)S(1)}, u32[]{:S(2)}) copy-start(bf16[704,256]{1,0:T(8,128)(2,1)S(1)} %collective-permute-done.5) | copy-start | bytes 1081348
  76.0 0.8 copy-start.5
  76.0 0.9 copy-start.8
  76.9 1.6 %copy-start = (bf16[1,704,256]{2,1,0:T(8,128)(2,1)S(1)}, bf16[1,704,256]{2,1,0:T(8,128)(2,1)}, u32[]{:S(2)}) copy-start(bf16[1,704,256]{2,1,0:T(8,128)(2,1)} %get-tuple-element.24) | copy-start | bytes 1081348
  76.9 1.6 %copy-start.3 = (bf16[704,256]{1,0:T(8,128)(2,1)S(1)}, bf16[704,256]{1,0:T(8,128)(2,1)}, u32[]{:S(2)}) copy-start(bf16[704,256]{1,0:T(8,128)(2,1)} %copy-done.2) | copy-start | bytes 1081348
  76.9 1.6 %copy-start.6 = (bf16[704,256]{1,0:T(8,128)(2,1)S(1)}, bf16[704,256]{1,0:T(8,128)(2,1)}, u32[]{:S(2)}) copy-start(bf16[704,256]{1,0:T(8,128)(2,1)} %copy-done.5) | copy-start | bytes 1081348
  76.9 1.7 %copy-start.9 = (bf16[704,256]{1,0:T(8,128)(2,1)S(1)}, bf16[704,256]{1,0:T(8,128)(2,1)}, u32[]{:S(2)}) copy-start(bf16[704,256]{1,0:T(8,128)(2,1)} %copy-done.8) | copy-start | bytes 1081348
  82.4 0.8 copy-start.11
  83.2 30.7 %copy-start.1 = (bf16[1,704,256]{2,1,0:T(8,128)(2,1)S(1)}, bf16[1,704,256]{2,1,0:T(8,128)(2,1)}, u32[]{:S(2)}) copy-start(bf16[1,704,256]{2,1,0:T(8,128)(2,1)} %get-tuple-element.24) | copy-start | bytes 1081348
  83.3 30.7 %copy-start.4 = (bf16[704,256]{1,0:T(8,128)(2,1)S(1)}, bf16[704,256]{1,0:T(8,128)(2,1)}, u32[]{:S(2)}) copy-start(bf16[704,256]{1,0:T(8,128)(2,1)} %copy-done.2) | copy-start | bytes 1081348
  83.3 30.7 %copy-start.7 = (bf16[704,256]{1,0:T(8,128)(2,1)S(1)}, bf16[704,256]{1,0:T(8,128)(2,1)}, u32[]{:S(2)}) copy-start(bf16[704,256]{1,0:T(8,128)(2,1)} %copy-done.5) | copy-start | bytes 1081348
  83.3 30.7 %copy-start.10 = (bf16[704,256]{1,0:T(8,128)(2,1)S(1)}, bf16[704,256]{1,0:T(8,128)(2,1)}, u32[]{:S(2)}) copy-start(bf16[704,256]{1,0:T(8,128)(2,1)} %copy-done.8) | copy-start | bytes 1081348
  91.1 24.7 %all-to-all-start.2 = ((f32[128,1,768]{2,1,0:T(1,128)}), f32[128,1,768]{2,1,0:T(1,128)S(1)}, u32[]{:S(2)}, u32[]{:S(2)}) async-start(f32[128,1,768]{2,1,0:T(1,128)} %all_to_all.24), calls=%async_computation.2 | async-start | bytes 786432 | tf_op jit(solution)/shard_map/all_to_all | solution.py:111
  99.1 18.6 %collective-permute-start.7 = (f32[56,128]{1,0:T(8,128)}, f32[56,128]{1,0:T(8,128)}, u32[]{:S(2)}, u32[]{:S(2)}) collective-permute-start(f32[56,128]{1,0:T(8,128)} %get-tuple-element.18), channel_id=1, source_target_pairs={{0,8},{4,12},{8,16},{12,20},{16,24},{20,28},{24,32},{28,36},{32,40... | collective-permute-start | bytes 86024 | tf_op jit(solution)/shard_map/ppermute | solution.py:16
  102.4 15.3 %collective-permute-start.10 = (f32[56,128]{1,0:T(8,128)}, f32[56,128]{1,0:T(8,128)}, u32[]{:S(2)}, u32[]{:S(2)}) collective-permute-start(f32[56,128]{1,0:T(8,128)} %get-tuple-element.19), channel_id=1, source_target_pairs={{0,504},{4,508},{8,0},{12,4},{16,8},{20,12},{24,16},{28,20},{32,24... | collective-permute-start | bytes 86024 | tf_op jit(solution)/shard_map/ppermute | solution.py:16
  108.4 9.3 %collective-permute-start.9 = (f32[56,128]{1,0:T(8,128)}, f32[56,128]{1,0:T(8,128)}, u32[]{:S(2)}, u32[]{:S(2)}) collective-permute-start(f32[56,128]{1,0:T(8,128)} %get-tuple-element.20), channel_id=1, source_target_pairs={{0,508},{4,0},{8,4},{12,8},{16,12},{20,16},{24,20},{28,24},{32,28}... | collective-permute-start | bytes 86024 | tf_op jit(solution)/shard_map/ppermute | solution.py:16
  111.1 4.8 %copy-start.15 = (s32[1,2]{1,0:T(1,128)S(1)}, s32[1,2]{1,0:T(1,128)}, u32[]{:S(2)}) copy-start(s32[1,2]{1,0:T(1,128)} %param.15) | copy-start | bytes 28
  111.1 6.6 %collective-permute-start.8 = (f32[56,128]{1,0:T(8,128)S(1)}, f32[56,128]{1,0:T(8,128)}, u32[]{:S(2)}, u32[]{:S(2)}) collective-permute-start(f32[56,128]{1,0:T(8,128)S(1)} %get-tuple-element.21), channel_id=1, source_target_pairs={{0,4},{4,8},{8,12},{12,16},{16,20},{20,24},{24,28},{28,32},{32,36}... | collective-permute-start | bytes 86024 | tf_op jit(solution)/shard_map/ppermute | solution.py:16
  115.3 3.9 %copy-start.12 = (bf16[448,128]{1,0:T(8,128)(2,1)S(1)}, bf16[448,128]{1,0:T(8,128)(2,1)}, u32[]{:S(2)}) copy-start(bf16[448,128]{1,0:T(8,128)(2,1)} %param.10) | copy-start | bytes 344068

commit v3 on v2

--- a/solution.py
+++ b/solution.py
@@ -92,17 +92,16 @@
 
     table_grad = contract_rows(counts, spread, HIGH)
 
-    returned = jnp.concatenate(
-        [
+    back = []
+    for o in range(NOFF):
+        back.append(
             from_behind(
                 table_grad[rows_here + o * slots : rows_here + (o + 1) * slots],
                 "dom",
                 -offset_of(o),
             )
-            for o in range(NOFF)
-        ],
-        0,
-    )
+        )
+    returned = jnp.concatenate(back, 0)
 
     weight_part = jnp.sum(weight_recv, axis=0)
     hub_chunks = table_grad[rows_here + halo_rows :].reshape(dom_count, hub_dev * feat_in)

time: 121 us -> 121 us (level)
  no operation moved by 1% of the time
where the time goes in v3:
time: 121 us; the launch traced here: 120 us
  starting transfers between devices  70.1 us (58%)
  waiting for transfers between devices  18.9 us (16%)
  matrix products  10.6 us (9%)
  other arithmetic  9.98 us (8%)
  local copies, waits for them, and re-layouts  9.52 us (8%)
    ppermute x11, starting transfers between devices, from_behind(): return lax.ppermute(x, axis, [(i, (i + by) % size) for i in range(size)])  46.8 us
    all_to_all x1, waiting for transfers between devices, gather_all(): out = lax.all_to_all(rep, axis, 0, 0, tiled=True)  11.1 us
    all_to_all x1, starting transfers between devices, gather_all(): out = lax.all_to_all(rep, axis, 0, 0, tiled=True)  10.2 us
    all_to_all x1, starting transfers between devices, per_device(): recv = lax.all_to_all(sent, 'dom', 0, 0, tiled=True)  6.57 us
    all_to_all x1, starting transfers between devices, per_device(): lax.all_to_all(weight_flat.reshape(dom_count, -1), 'dom', 0, 0, tiled=True)  6.56 us
    dot_general x5, matrix products, contract_rows(): lax.dot_general(left, right, (((0,), (0,)), ((), ())), preferred_element_...  5.84 us
    reduce_sum x1, other arithmetic, per_device(): counts = jnp.sum((neighbors[:, :, None] == t_iota).astype(F32), axis=1)  5.01 us
    all_to_all x1, waiting for transfers between devices, per_device(): lax.all_to_all(weight_flat.reshape(dom_count, -1), 'dom', 0, 0, tiled=True)  4.92 us
  transfers between devices with their start and end apart: 14, of which 4 were waited for; matrix products, arithmetic and copies ran while one was open for 15% of the time, Pallas kernels for 0%

profile of v3, /device:TPU:1, one launch (start us, length us, event | category | flops | bytes accessed | tf_op | source)
XLA Modules:
  0.0 120.2 jit_solution(10960296933532005678)
XLA Ops:
  0.6 0.8 eq.33
  1.4 1.0 constant_dynamic-update-slice_fusion.5
  2.4 0.3 convolution_convert_fusion
  2.7 4.0 %collective-permute-start.3 = (bf16[56,128]{1,0:T(8,128)(2,1)S(1)}, bf16[56,128]{1,0:T(8,128)(2,1)S(1)}, u32[]{:S(2)}, u32[]{:S(2)}) collective-permute-start(bf16[56,128]{1,0:T(8,128)(2,1)S(1)} %get-tuple-element.26), channel_id=1, source_target_pairs={{0,8},{4,12},{8,16},{12,20},{16,24},{20,28},{24,32},{28,36},{32,40... | collective-permute-start | bytes 43016 | tf_op jit(solution)/shard_map/ppermute | solution.py:16
  6.7 4.0 %collective-permute-start.2 = (bf16[56,128]{1,0:T(8,128)(2,1)S(1)}, bf16[56,128]{1,0:T(8,128)(2,1)S(1)}, u32[]{:S(2)}, u32[]{:S(2)}) collective-permute-start(bf16[56,128]{1,0:T(8,128)(2,1)S(1)} %get-tuple-element.27), channel_id=1, source_target_pairs={{0,4},{4,8},{8,12},{12,16},{16,20},{20,24},{24,28},{28,32},{32,36}... | collective-permute-start | bytes 43016 | tf_op jit(solution)/shard_map/ppermute | solution.py:16
  10.8 4.5 %collective-permute-start.1 = (bf16[56,128]{1,0:T(8,128)(2,1)S(1)}, bf16[56,128]{1,0:T(8,128)(2,1)S(1)}, u32[]{:S(2)}, u32[]{:S(2)}) collective-permute-start(bf16[56,128]{1,0:T(8,128)(2,1)S(1)} %get-tuple-element.28), channel_id=1, source_target_pairs={{0,508},{4,0},{8,4},{12,8},{16,12},{20,16},{24,20},{28,24},{32,28}... | collective-permute-start | bytes 43016 | tf_op jit(solution)/shard_map/ppermute | solution.py:16
  15.3 8.2 %collective-permute-start = (bf16[56,128]{1,0:T(8,128)(2,1)S(1)}, bf16[56,128]{1,0:T(8,128)(2,1)S(1)}, u32[]{:S(2)}, u32[]{:S(2)}) collective-permute-start(bf16[56,128]{1,0:T(8,128)(2,1)S(1)} %get-tuple-element.29), channel_id=1, source_target_pairs={{0,504},{4,508},{8,0},{12,4},{16,8},{20,12},{24,16},{28,20},{32,24... | collective-permute-start | bytes 43016 | tf_op jit(solution)/shard_map/ppermute | solution.py:16
  23.6 0.8 convolution_convert_fusion.1
  24.4 5.0 %convert_reduce_fusion = f32[448,928]{1,0:T(8,128)S(1)} fusion(s32[448,15]{0,1:T(8,128)} %param.17), kind=kLoop, calls=%fused_computation | loop fusion | flops 18292736 | bytes 1689856 | tf_op jit(solution)/shard_map/reduce_sum | solution.py:61
  29.4 0.7 broadcast_in_dim.4
  30.1 10.2 %all-to-all-start = ((bf16[128,2,128]{2,1,0:T(2,128)(2,1)}), bf16[128,2,128]{2,1,0:T(2,128)(2,1)S(1)}, u32[]{:S(2)}, u32[]{:S(2)}) async-start(bf16[128,2,128]{2,1,0:T(2,128)(2,1)} %broadcast_in_dim.4), calls=%async_computation | async-start | bytes 131072 | tf_op jit(solution)/shard_map/all_to_all | solution.py:32
  40.3 0.2 fusion.42
  40.6 11.1 %all-to-all-done = bf16[128,2,128]{2,1,0:T(2,128)(2,1)S(1)} async-done(((bf16[128,2,128]{2,1,0:T(2,128)(2,1)}), bf16[128,2,128]{2,1,0:T(2,128)(2,1)S(1)}, u32[]{:S(2)}, u32[]{:S(2)}) %all-to-all-start) | async-done | bytes 65568 | tf_op jit(solution)/shard_map/all_to_all | solution.py:32
  51.7 0.4 fusion.4
  52.2 1.3 %multiply_convert_fusion = bf16[448,256]{1,0:T(8,128)(2,1)S(1)} fusion(f32[448,256]{1,0:T(8,128)S(1)} %fusion.42, bf16[448,128]{1,0:T(8,128)(2,1)S(1)} %fusion.4, bf16[128,256]{1,0:T(8,128)(2,1)S(1)} %copy-done.14, bf16[448,256]{1,0:T(8,128)(2,1)} %param.14, f32[256]{0:T(256)S(1)} %copy-done.16), kind=kOutput, calls=%fused_computation.18 | convolution fusion | flops 30736384 | bytes 1098752 | tf_op jit(solution)/shard_map/dot_general | solution.py:70
  53.4 0.9 fusion.38
  54.4 4.6 %collective-permute-start.5 = (bf16[704,256]{1,0:T(8,128)(2,1)}, bf16[704,256]{1,0:T(8,128)(2,1)S(1)}, u32[]{:S(2)}, u32[]{:S(2)}) collective-permute-start(bf16[704,256]{1,0:T(8,128)(2,1)} %get-tuple-element.25), channel_id=1, source_target_pairs={{0,2},{1,3},{2,0},{3,1},{4,6},{5,7},{6,4},{7,5},{8,10},{9,11},{10,... | collective-permute-start | bytes 1081352 | tf_op jit(solution)/shard_map/ppermute | solution.py:16
  59.0 2.2 %collective-permute-start.4 = (bf16[704,256]{1,0:T(8,128)(2,1)}, bf16[704,256]{1,0:T(8,128)(2,1)S(1)}, u32[]{:S(2)}, u32[]{:S(2)}) collective-permute-start(bf16[704,256]{1,0:T(8,128)(2,1)} %get-tuple-element.25), channel_id=1, source_target_pairs={{0,1},{1,2},{2,3},{3,0},{4,5},{5,6},{6,7},{7,4},{8,9},{9,10},{10,1... | collective-permute-start | bytes 1081352 | tf_op jit(solution)/shard_map/ppermute | solution.py:16
  61.2 4.3 %collective-permute-start.6 = (bf16[704,256]{1,0:T(8,128)(2,1)}, bf16[704,256]{1,0:T(8,128)(2,1)S(1)}, u32[]{:S(2)}, u32[]{:S(2)}) collective-permute-start(bf16[704,256]{1,0:T(8,128)(2,1)} %get-tuple-element.25), channel_id=1, source_target_pairs={{0,3},{1,0},{2,1},{3,2},{4,7},{5,4},{6,5},{7,6},{8,11},{9,8},{10,9... | collective-permute-start | bytes 1081352 | tf_op jit(solution)/shard_map/ppermute | solution.py:16
  65.5 0.2 fusion.45
  65.8 0.2 fusion.44
  66.1 0.9 all_to_all.22
  67.0 6.6 %all-to-all-start.1 = ((f32[128,1,512]{2,1,0:T(1,128)}), f32[128,1,512]{2,1,0:T(1,128)S(1)}, u32[]{:S(2)}, u32[]{:S(2)}) async-start(f32[128,1,512]{2,1,0:T(1,128)} %all_to_all.22), calls=%async_computation.1 | async-start | bytes 524288 | tf_op jit(solution)/shard_map/all_to_all | solution.py:84
  73.6 2.4 %collective-permute-done.4 = bf16[704,256]{1,0:T(8,128)(2,1)S(1)} collective-permute-done((bf16[704,256]{1,0:T(8,128)(2,1)}, bf16[704,256]{1,0:T(8,128)(2,1)S(1)}, u32[]{:S(2)}, u32[]{:S(2)}) %collective-permute-start.4) | collective-permute-done | bytes 360480 | tf_op jit(solution)/shard_map/ppermute | solution.py:16
  76.0 0.8 copy-done.5
  76.9 1.6 %pad_maximum_fusion = bf16[4,704,256]{2,1,0:T(8,128)(2,1)S(1)} fusion(bf16[1,704,256]{2,1,0:T(8,128)(2,1)} %bitcast.40, bf16[1,704,256]{2,1,0:T(8,128)(2,1)} %bitcast.34, bf16[1,704,256]{2,1,0:T(8,128)(2,1)} %bitcast.37, bf16[1,704,256]{2,1,0:T(8,128)(2,1)} %get-tuple-element.24), kind=kLoop, calls=%fused_computation.2 | loop fusion | flops 2162688 | bytes 2883584 | tf_op jit(solution)/shard_map/stack | solution.py:77
  78.6 0.4 fusion.2
  79.0 3.4 %fusion.43 = f32[928,128]{1,0:T(8,128)S(1)} fusion(f32[448,928]{1,0:T(8,128)S(1)} %convert_reduce_fusion, f32[448,128]{1,0:T(8,128)S(1)} %fusion.2), kind=kOutput, calls=%fused_computation.71 | convolution fusion | flops 638582784 | bytes 2367488 | tf_op jit(solution)/shard_map/dot_general | solution.py:24
  82.4 0.8 copy-done.11
  83.3 0.7 reshape.46
  84.0 4.9 %all-to-all-done.1 = f32[128,1,512]{2,1,0:T(1,128)S(1)} async-done(((f32[128,1,512]{2,1,0:T(1,128)}), f32[128,1,512]{2,1,0:T(1,128)S(1)}, u32[]{:S(2)}, u32[]{:S(2)}) %all-to-all-start.1) | async-done | bytes 262176 | tf_op jit(solution)/shard_map/all_to_all | solution.py:84
  88.9 0.2 reduce_sum.37
  89.1 0.9 pad_maximum_fusion.1
  90.1 1.0 all_to_all.24
  91.1 6.6 %all-to-all-start.2 = ((f32[128,1,768]{2,1,0:T(1,128)}), f32[128,1,768]{2,1,0:T(1,128)S(1)}, u32[]{:S(2)}, u32[]{:S(2)}) async-start(f32[128,1,768]{2,1,0:T(1,128)} %all_to_all.24), calls=%async_computation.2 | async-start | bytes 786432 | tf_op jit(solution)/shard_map/all_to_all | solution.py:110
  97.7 1.4 %fusion.39 = (f32[56,128]{1,0:T(8,128)}, f32[56,128]{1,0:T(8,128)}, f32[56,128]{1,0:T(8,128)}, f32[56,128]{1,0:T(8,128)S(1)}) fusion(f32[928,128]{1,0:T(8,128)} %copy-done.11), kind=kLoop, calls=%fused_computation.67 | loop fusion | bytes 229376 | tf_op jit(solution)/shard_map/slice | solution.py:99
  99.1 3.3 %collective-permute-start.7 = (f32[56,128]{1,0:T(8,128)}, f32[56,128]{1,0:T(8,128)}, u32[]{:S(2)}, u32[]{:S(2)}) collective-permute-start(f32[56,128]{1,0:T(8,128)} %get-tuple-element.18), channel_id=1, source_target_pairs={{0,8},{4,12},{8,16},{12,20},{16,24},{20,28},{24,32},{28,36},{32,40... | collective-permute-start | bytes 86024 | tf_op jit(solution)/shard_map/ppermute | solution.py:16
  102.4 6.0 %collective-permute-start.10 = (f32[56,128]{1,0:T(8,128)}, f32[56,128]{1,0:T(8,128)}, u32[]{:S(2)}, u32[]{:S(2)}) collective-permute-start(f32[56,128]{1,0:T(8,128)} %get-tuple-element.19), channel_id=1, source_target_pairs={{0,504},{4,508},{8,0},{12,4},{16,8},{20,12},{24,16},{28,20},{32,24... | collective-permute-start | bytes 86024 | tf_op jit(solution)/shard_map/ppermute | solution.py:16
  108.4 2.7 %collective-permute-start.9 = (f32[56,128]{1,0:T(8,128)}, f32[56,128]{1,0:T(8,128)}, u32[]{:S(2)}, u32[]{:S(2)}) collective-permute-start(f32[56,128]{1,0:T(8,128)} %get-tuple-element.20), channel_id=1, source_target_pairs={{0,508},{4,0},{8,4},{12,8},{16,12},{20,16},{24,20},{28,24},{32,28}... | collective-permute-start | bytes 86024 | tf_op jit(solution)/shard_map/ppermute | solution.py:16
  111.1 2.8 %collective-permute-start.8 = (f32[56,128]{1,0:T(8,128)S(1)}, f32[56,128]{1,0:T(8,128)}, u32[]{:S(2)}, u32[]{:S(2)}) collective-permute-start(f32[56,128]{1,0:T(8,128)S(1)} %get-tuple-element.21), channel_id=1, source_target_pairs={{0,4},{4,8},{8,12},{12,16},{16,20},{20,24},{24,28},{28,32},{32,36}... | collective-permute-start | bytes 86024 | tf_op jit(solution)/shard_map/ppermute | solution.py:16
  114.0 1.3 %fusion.3 = f32[448,128]{1,0:T(8,128)S(1)} fusion(bf16[4,704,256]{2,1,0:T(8,128)(2,1)S(1)} %pad_maximum_fusion, bf16[1,704,256]{2,1,0:T(8,128)(2,1)S(1)} %bitcast.42, bf16[1,704,256]{2,1,0:T(8,128)(2,1)S(1)} %bitcast.36, bf16[1,704,256]{2,1,0:T(8,128)(2,1)S(1)} %bitcast.39, bf16[1,704,256]{2,1,0:T(8,128)(2,1)S(1)} %copy-done.1, f32[928,128]{1,0:T(8,128)} %copy-done.11), kind=kOutput, calls=%fused_computation.11 | convolution fusion | flops 118546432 | bytes 2818048 | tf_op jit(solution)/shard_map/dot_general | solution.py:90
  115.3 0.4 all-to-all-done.2
  115.9 0.4 fusion.31
  116.3 0.7 squeeze.7
  117.0 0.7 squeeze.6
  117.7 1.6 %multiply_reduce_fusion = (f32[448]{0:T(512)S(1)}, f32[448,128]{1,0:T(8,128)S(1)}) fusion(f32[448,128]{1,0:T(8,128)S(1)} %fusion.31, f32[448,128]{1,0:T(8,128)S(1)} %fusion.3, f32[56,128]{1,0:T(8,128)} %collective-permute-done.10, f32[56,128]{1,0:T(8,128)} %collective-permute-done.9, f32[56,128]{1,0:T(8,128)} %collective-permute-done.8, ...), kind=kOutput, calls=%fused_computation.39 | convolution fusion | flops 154555968 | bytes 805504 | tf_op jit(solution)/shard_map/dot_general | solution.py:24
  119.3 0.2 add_convert_fusion
  119.5 0.7 copy.16
  (57 shorter events, 0.5 us)
Async XLA Ops:
  1.4 38.9 %copy-start.13 = (bf16[128,256]{1,0:T(8,128)(2,1)S(1)}, bf16[128,256]{1,0:T(8,128)(2,1)}, u32[]{:S(2)}) copy-start(bf16[128,256]{1,0:T(8,128)(2,1)} %param.11) | copy-start | bytes 196612
  2.7 37.9 %collective-permute-start.3 = (bf16[56,128]{1,0:T(8,128)(2,1)S(1)}, bf16[56,128]{1,0:T(8,128)(2,1)S(1)}, u32[]{:S(2)}, u32[]{:S(2)}) collective-permute-start(bf16[56,128]{1,0:T(8,128)(2,1)S(1)} %get-tuple-element.26), channel_id=1, source_target_pairs={{0,8},{4,12},{8,16},{12,20},{16,24},{20,28},{24,32},{28,36},{32,40... | collective-permute-start | bytes 43016 | tf_op jit(solution)/shard_map/ppermute | solution.py:16
  6.7 33.8 %collective-permute-start.2 = (bf16[56,128]{1,0:T(8,128)(2,1)S(1)}, bf16[56,128]{1,0:T(8,128)(2,1)S(1)}, u32[]{:S(2)}, u32[]{:S(2)}) collective-permute-start(bf16[56,128]{1,0:T(8,128)(2,1)S(1)} %get-tuple-element.27), channel_id=1, source_target_pairs={{0,4},{4,8},{8,12},{12,16},{16,20},{20,24},{24,28},{28,32},{32,36}... | collective-permute-start | bytes 43016 | tf_op jit(solution)/shard_map/ppermute | solution.py:16
  10.8 29.8 %collective-permute-start.1 = (bf16[56,128]{1,0:T(8,128)(2,1)S(1)}, bf16[56,128]{1,0:T(8,128)(2,1)S(1)}, u32[]{:S(2)}, u32[]{:S(2)}) collective-permute-start(bf16[56,128]{1,0:T(8,128)(2,1)S(1)} %get-tuple-element.28), channel_id=1, source_target_pairs={{0,508},{4,0},{8,4},{12,8},{16,12},{20,16},{24,20},{28,24},{32,28}... | collective-permute-start | bytes 43016 | tf_op jit(solution)/shard_map/ppermute | solution.py:16
  15.3 25.2 %collective-permute-start = (bf16[56,128]{1,0:T(8,128)(2,1)S(1)}, bf16[56,128]{1,0:T(8,128)(2,1)S(1)}, u32[]{:S(2)}, u32[]{:S(2)}) collective-permute-start(bf16[56,128]{1,0:T(8,128)(2,1)S(1)} %get-tuple-element.29), channel_id=1, source_target_pairs={{0,504},{4,508},{8,0},{12,4},{16,8},{20,12},{24,16},{28,20},{32,24... | collective-permute-start | bytes 43016 | tf_op jit(solution)/shard_map/ppermute | solution.py:16
  30.1 21.6 %all-to-all-start = ((bf16[128,2,128]{2,1,0:T(2,128)(2,1)}), bf16[128,2,128]{2,1,0:T(2,128)(2,1)S(1)}, u32[]{:S(2)}, u32[]{:S(2)}) async-start(bf16[128,2,128]{2,1,0:T(2,128)(2,1)} %broadcast_in_dim.4), calls=%async_computation | async-start | bytes 131072 | tf_op jit(solution)/shard_map/all_to_all | solution.py:32
  40.3 11.8 %copy-start.14 = (bf16[128,256]{1,0:T(8,128)(2,1)S(1)}, bf16[128,256]{1,0:T(8,128)(2,1)}, u32[]{:S(2)}) copy-start(bf16[128,256]{1,0:T(8,128)(2,1)} %param.12) | copy-start | bytes 196612
  40.3 11.8 %copy-start.16 = (f32[256]{0:T(256)S(1)}, f32[256]{0:T(256)}, u32[]{:S(2)}) copy-start(f32[256]{0:T(256)} %param.13) | copy-start | bytes 3076
  54.4 19.2 %collective-permute-start.5 = (bf16[704,256]{1,0:T(8,128)(2,1)}, bf16[704,256]{1,0:T(8,128)(2,1)S(1)}, u32[]{:S(2)}, u32[]{:S(2)}) collective-permute-start(bf16[704,256]{1,0:T(8,128)(2,1)} %get-tuple-element.25), channel_id=1, source_target_pairs={{0,2},{1,3},{2,0},{3,1},{4,6},{5,7},{6,4},{7,5},{8,10},{9,11},{10,... | collective-permute-start | bytes 1081352 | tf_op jit(solution)/shard_map/ppermute | solution.py:16
  59.0 17.0 %collective-permute-start.4 = (bf16[704,256]{1,0:T(8,128)(2,1)}, bf16[704,256]{1,0:T(8,128)(2,1)S(1)}, u32[]{:S(2)}, u32[]{:S(2)}) collective-permute-start(bf16[704,256]{1,0:T(8,128)(2,1)} %get-tuple-element.25), channel_id=1, source_target_pairs={{0,1},{1,2},{2,3},{3,0},{4,5},{5,6},{6,7},{7,4},{8,9},{9,10},{10,1... | collective-permute-start | bytes 1081352 | tf_op jit(solution)/shard_map/ppermute | solution.py:16
  61.2 14.8 %collective-permute-start.6 = (bf16[704,256]{1,0:T(8,128)(2,1)}, bf16[704,256]{1,0:T(8,128)(2,1)S(1)}, u32[]{:S(2)}, u32[]{:S(2)}) collective-permute-start(bf16[704,256]{1,0:T(8,128)(2,1)} %get-tuple-element.25), channel_id=1, source_target_pairs={{0,3},{1,0},{2,1},{3,2},{4,7},{5,4},{6,5},{7,6},{8,11},{9,8},{10,9... | collective-permute-start | bytes 1081352 | tf_op jit(solution)/shard_map/ppermute | solution.py:16
  67.0 21.9 %all-to-all-start.1 = ((f32[128,1,512]{2,1,0:T(1,128)}), f32[128,1,512]{2,1,0:T(1,128)S(1)}, u32[]{:S(2)}, u32[]{:S(2)}) async-start(f32[128,1,512]{2,1,0:T(1,128)} %all_to_all.22), calls=%async_computation.1 | async-start | bytes 524288 | tf_op jit(solution)/shard_map/all_to_all | solution.py:84
  73.6 2.5 %copy-start.2 = (bf16[704,256]{1,0:T(8,128)(2,1)}, bf16[704,256]{1,0:T(8,128)(2,1)S(1)}, u32[]{:S(2)}) copy-start(bf16[704,256]{1,0:T(8,128)(2,1)S(1)} %collective-permute-done.5) | copy-start | bytes 1081348
  76.0 0.8 copy-start.5
  76.0 0.9 copy-start.8
  76.9 1.6 %copy-start = (bf16[1,704,256]{2,1,0:T(8,128)(2,1)S(1)}, bf16[1,704,256]{2,1,0:T(8,128)(2,1)}, u32[]{:S(2)}) copy-start(bf16[1,704,256]{2,1,0:T(8,128)(2,1)} %get-tuple-element.24) | copy-start | bytes 1081348
  76.9 1.6 %copy-start.3 = (bf16[704,256]{1,0:T(8,128)(2,1)S(1)}, bf16[704,256]{1,0:T(8,128)(2,1)}, u32[]{:S(2)}) copy-start(bf16[704,256]{1,0:T(8,128)(2,1)} %copy-done.2) | copy-start | bytes 1081348
  76.9 1.6 %copy-start.6 = (bf16[704,256]{1,0:T(8,128)(2,1)S(1)}, bf16[704,256]{1,0:T(8,128)(2,1)}, u32[]{:S(2)}) copy-start(bf16[704,256]{1,0:T(8,128)(2,1)} %copy-done.5) | copy-start | bytes 1081348
  76.9 1.7 %copy-start.9 = (bf16[704,256]{1,0:T(8,128)(2,1)S(1)}, bf16[704,256]{1,0:T(8,128)(2,1)}, u32[]{:S(2)}) copy-start(bf16[704,256]{1,0:T(8,128)(2,1)} %copy-done.8) | copy-start | bytes 1081348
  82.4 0.8 copy-start.11
  83.2 30.7 %copy-start.1 = (bf16[1,704,256]{2,1,0:T(8,128)(2,1)S(1)}, bf16[1,704,256]{2,1,0:T(8,128)(2,1)}, u32[]{:S(2)}) copy-start(bf16[1,704,256]{2,1,0:T(8,128)(2,1)} %get-tuple-element.24) | copy-start | bytes 1081348
  83.3 30.7 %copy-start.4 = (bf16[704,256]{1,0:T(8,128)(2,1)S(1)}, bf16[704,256]{1,0:T(8,128)(2,1)}, u32[]{:S(2)}) copy-start(bf16[704,256]{1,0:T(8,128)(2,1)} %copy-done.2) | copy-start | bytes 1081348
  83.3 30.7 %copy-start.7 = (bf16[704,256]{1,0:T(8,128)(2,1)S(1)}, bf16[704,256]{1,0:T(8,128)(2,1)}, u32[]{:S(2)}) copy-start(bf16[704,256]{1,0:T(8,128)(2,1)} %copy-done.5) | copy-start | bytes 1081348
  83.3 30.7 %copy-start.10 = (bf16[704,256]{1,0:T(8,128)(2,1)S(1)}, bf16[704,256]{1,0:T(8,128)(2,1)}, u32[]{:S(2)}) copy-start(bf16[704,256]{1,0:T(8,128)(2,1)} %copy-done.8) | copy-start | bytes 1081348
  91.1 24.7 %all-to-all-start.2 = ((f32[128,1,768]{2,1,0:T(1,128)}), f32[128,1,768]{2,1,0:T(1,128)S(1)}, u32[]{:S(2)}, u32[]{:S(2)}) async-start(f32[128,1,768]{2,1,0:T(1,128)} %all_to_all.24), calls=%async_computation.2 | async-start | bytes 786432 | tf_op jit(solution)/shard_map/all_to_all | solution.py:110
  99.1 18.6 %collective-permute-start.7 = (f32[56,128]{1,0:T(8,128)}, f32[56,128]{1,0:T(8,128)}, u32[]{:S(2)}, u32[]{:S(2)}) collective-permute-start(f32[56,128]{1,0:T(8,128)} %get-tuple-element.18), channel_id=1, source_target_pairs={{0,8},{4,12},{8,16},{12,20},{16,24},{20,28},{24,32},{28,36},{32,40... | collective-permute-start | bytes 86024 | tf_op jit(solution)/shard_map/ppermute | solution.py:16
  102.4 15.3 %collective-permute-start.10 = (f32[56,128]{1,0:T(8,128)}, f32[56,128]{1,0:T(8,128)}, u32[]{:S(2)}, u32[]{:S(2)}) collective-permute-start(f32[56,128]{1,0:T(8,128)} %get-tuple-element.19), channel_id=1, source_target_pairs={{0,504},{4,508},{8,0},{12,4},{16,8},{20,12},{24,16},{28,20},{32,24... | collective-permute-start | bytes 86024 | tf_op jit(solution)/shard_map/ppermute | solution.py:16
  108.4 9.3 %collective-permute-start.9 = (f32[56,128]{1,0:T(8,128)}, f32[56,128]{1,0:T(8,128)}, u32[]{:S(2)}, u32[]{:S(2)}) collective-permute-start(f32[56,128]{1,0:T(8,128)} %get-tuple-element.20), channel_id=1, source_target_pairs={{0,508},{4,0},{8,4},{12,8},{16,12},{20,16},{24,20},{28,24},{32,28}... | collective-permute-start | bytes 86024 | tf_op jit(solution)/shard_map/ppermute | solution.py:16
  111.1 4.8 %copy-start.15 = (s32[1,2]{1,0:T(1,128)S(1)}, s32[1,2]{1,0:T(1,128)}, u32[]{:S(2)}) copy-start(s32[1,2]{1,0:T(1,128)} %param.15) | copy-start | bytes 28
  111.1 6.6 %collective-permute-start.8 = (f32[56,128]{1,0:T(8,128)S(1)}, f32[56,128]{1,0:T(8,128)}, u32[]{:S(2)}, u32[]{:S(2)}) collective-permute-start(f32[56,128]{1,0:T(8,128)S(1)} %get-tuple-element.21), channel_id=1, source_target_pairs={{0,4},{4,8},{8,12},{12,16},{16,20},{20,24},{24,28},{28,32},{32,36}... | collective-permute-start | bytes 86024 | tf_op jit(solution)/shard_map/ppermute | solution.py:16
  115.3 3.9 %copy-start.12 = (bf16[448,128]{1,0:T(8,128)(2,1)S(1)}, bf16[448,128]{1,0:T(8,128)(2,1)}, u32[]{:S(2)}) copy-start(bf16[448,128]{1,0:T(8,128)(2,1)} %param.10) | copy-start | bytes 344068

commit v4 on v2

--- a/solution.py
+++ b/solution.py
@@ -57,12 +57,11 @@
         from_behind(halo_out[o * slots : (o + 1) * slots], "dom", offset_of(o))
         for o in range(NOFF)
     ]
+    hubs = gather_all(hub_out, "dom").reshape(dom_count * hub_dev, feat_in)
+    table = jnp.concatenate([perturbed] + pieces + [hubs], 0)
+
     t_iota = lax.broadcasted_iota(jnp.int32, (rows_here, K, table_rows), 2)
     counts = jnp.sum((neighbors[:, :, None] == t_iota).astype(F32), axis=1)
-    hub_out, counts = lax.optimization_barrier((hub_out, counts))
-
-    hubs = gather_all(hub_out, "dom").reshape(dom_count * hub_dev, feat_in)
-    table = jnp.concatenate([perturbed] + pieces + [hubs], 0)
     gathered_sum = jnp.dot(counts.astype(BF16), table, preferred_element_type=F32)
     neighbor_mean = (gathered_sum / K).astype(BF16)
 
@@ -81,7 +80,7 @@
     part_self = contract_rows(perturbed, grad_pre)
     part_neigh = contract_rows(neighbor_mean, grad_pre)
     weight_flat = jnp.concatenate([part_self.reshape(-1), part_neigh.reshape(-1)])
-    weight_recv = lax.all_to_all(weight_flat.reshape(dom_count, -1), "dom", 0, 0, tiled=True)
+    weight_recv = lax.all_to_all(weight_flat.reshape(dom_count, -1, 128), "dom", 0, 0, tiled=True)
 
     gp_all = got[:, :rows_here]
     ws_all = got[:, rows_here : rows_here + feat_in]
@@ -104,11 +103,11 @@
         0,
     )
 
-    weight_part = jnp.sum(weight_recv, axis=0)
-    hub_chunks = table_grad[rows_here + halo_rows :].reshape(dom_count, hub_dev * feat_in)
-    weight_rep = jnp.broadcast_to(weight_part[None], (dom_count, weight_part.shape[0]))
+    weight_part = jnp.sum(weight_recv.reshape(dom_count, -1, 128), axis=0)
+    hub_chunks = table_grad[rows_here + halo_rows :].reshape(dom_count, hub_dev, feat_in)
+    weight_rep = jnp.broadcast_to(weight_part[None], (dom_count,) + weight_part.shape)
     sent = jnp.concatenate([hub_chunks, weight_rep], 1)
-    recv = lax.all_to_all(sent, "dom", 0, 0, tiled=True)
+    recv = lax.all_to_all(sent, "dom", 0, 0, tiled=True).reshape(dom_count, -1)
     hub_total = jnp.sum(recv[:, : hub_dev * feat_in], axis=0).reshape(hub_dev, feat_in)
     weights = recv[:, hub_dev * feat_in :].reshape(2, feat_in, hidden_here)
 

time: 121 us -> 118 us (0.975)
  local copies, waits for them, and re-layouts: 9.52 us -> 7.77 us
  waiting for transfers between devices: 18.9 us -> 17.5 us
    all_to_all x1, waiting for transfers between devices: 11.1 us -> 6.07 us  [gather_all(): out = lax.all_to_all(rep, axis, 0, 0, tiled=True)]
    ppermute x11, waiting for transfers between devices: 2.47 us -> 6.74 us  [from_behind(): return lax.ppermute(x, axis, [(i, (i + by) % size) for i in range(size)])]
    all_to_all x2, starting transfers between devices: 13.1 us -> 15.5 us  [the longest x1 8.57 us: per_device(): lax.all_to_all(weight_flat.reshape(dom_count, -1, 128), 'dom', 0, 0, tile...]
    all_to_all x1, starting transfers between devices: 10.2 us -> 8.57 us  [gather_all(): out = lax.all_to_all(rep, axis, 0, 0, tiled=True)]
    unnamed x40 -> x39, local copies, waits for them, and re-layouts: 2.58 us -> 2.43 us
where the time goes in v4:
time: 118 us; the launch traced here: 117 us
  starting transfers between devices  70.1 us (59%)
  waiting for transfers between devices  17.5 us (15%)
  other arithmetic  10.7 us (9%)
  matrix products  9.77 us (8%)
  local copies, waits for them, and re-layouts  7.77 us (7%)
    ppermute x11, starting transfers between devices, from_behind(): return lax.ppermute(x, axis, [(i, (i + by) % size) for i in range(size)])  46 us
    all_to_all x1, starting transfers between devices, per_device(): lax.all_to_all(weight_flat.reshape(dom_count, -1, 128), 'dom', 0, 0, tile...  8.57 us
    all_to_all x1, starting transfers between devices, gather_all(): out = lax.all_to_all(rep, axis, 0, 0, tiled=True)  8.57 us
    all_to_all x1, starting transfers between devices, per_device(): recv = lax.all_to_all(sent, 'dom', 0, 0, tiled=True).reshape(dom_count, -1)  6.94 us
    ppermute x11, waiting for transfers between devices, from_behind(): return lax.ppermute(x, axis, [(i, (i + by) % size) for i in range(size)])  6.74 us
    all_to_all x1, waiting for transfers between devices, gather_all(): out = lax.all_to_all(rep, axis, 0, 0, tiled=True)  6.07 us
    dot_general x5, matrix products, contract_rows(): lax.dot_general(left, right, (((0,), (0,)), ((), ())), preferred_element_...  5.04 us
    reduce_sum x1, other arithmetic, per_device(): counts = jnp.sum((neighbors[:, :, None] == t_iota).astype(F32), axis=1)  5.01 us
  transfers between devices with their start and end apart: 14, of which 4 were waited for; matrix products, arithmetic and copies ran while one was open for 15% of the time, Pallas kernels for 0%

profile of v4, /device:TPU:1, one launch (start us, length us, event | category | flops | bytes accessed | tf_op | source)
XLA Modules:
  0.0 117.0 jit_solution(2012042410345878216)
XLA Ops:
  0.6 0.8 eq.30
  1.4 1.0 constant_dynamic-update-slice_fusion.5
  2.4 0.3 convolution_convert_fusion
  2.7 14.4 %collective-permute-start = (bf16[56,128]{1,0:T(8,128)(2,1)S(1)}, bf16[56,128]{1,0:T(8,128)(2,1)S(1)}, u32[]{:S(2)}, u32[]{:S(2)}) collective-permute-start(bf16[56,128]{1,0:T(8,128)(2,1)S(1)} %get-tuple-element.31), channel_id=1, source_target_pairs={{0,504},{4,508},{8,0},{12,4},{16,8},{20,12},{24,16},{28,20},{32,24... | collective-permute-start | bytes 43016 | tf_op jit(solution)/shard_map/ppermute | solution.py:16
  17.1 2.9 %collective-permute-start.1 = (bf16[56,128]{1,0:T(8,128)(2,1)S(1)}, bf16[56,128]{1,0:T(8,128)(2,1)S(1)}, u32[]{:S(2)}, u32[]{:S(2)}) collective-permute-start(bf16[56,128]{1,0:T(8,128)(2,1)S(1)} %get-tuple-element.30), channel_id=1, source_target_pairs={{0,508},{4,0},{8,4},{12,8},{16,12},{20,16},{24,20},{28,24},{32,28}... | collective-permute-start | bytes 43016 | tf_op jit(solution)/shard_map/ppermute | solution.py:16
  20.0 2.7 %collective-permute-start.2 = (bf16[56,128]{1,0:T(8,128)(2,1)S(1)}, bf16[56,128]{1,0:T(8,128)(2,1)S(1)}, u32[]{:S(2)}, u32[]{:S(2)}) collective-permute-start(bf16[56,128]{1,0:T(8,128)(2,1)S(1)} %get-tuple-element.29), channel_id=1, source_target_pairs={{0,4},{4,8},{8,12},{12,16},{16,20},{20,24},{24,28},{28,32},{32,36}... | collective-permute-start | bytes 43016 | tf_op jit(solution)/shard_map/ppermute | solution.py:16
  22.7 1.9 %collective-permute-start.3 = (bf16[56,128]{1,0:T(8,128)(2,1)S(1)}, bf16[56,128]{1,0:T(8,128)(2,1)S(1)}, u32[]{:S(2)}, u32[]{:S(2)}) collective-permute-start(bf16[56,128]{1,0:T(8,128)(2,1)S(1)} %get-tuple-element.28), channel_id=1, source_target_pairs={{0,8},{4,12},{8,16},{12,20},{16,24},{20,28},{24,32},{28,36},{32,40... | collective-permute-start | bytes 43016 | tf_op jit(solution)/shard_map/ppermute | solution.py:16
  24.6 0.8 convolution_convert_fusion.1
  25.5 0.7 broadcast_in_dim.4
  26.1 8.6 %all-to-all-start = ((bf16[128,2,128]{2,1,0:T(2,128)(2,1)}), bf16[128,2,128]{2,1,0:T(2,128)(2,1)S(1)}, u32[]{:S(2)}, u32[]{:S(2)}) async-start(bf16[128,2,128]{2,1,0:T(2,128)(2,1)} %broadcast_in_dim.4), calls=%async_computation | async-start | bytes 131072 | tf_op jit(solution)/shard_map/all_to_all | solution.py:32
  34.7 5.0 %convert_reduce_fusion = f32[448,928]{1,0:T(8,128)S(1)} fusion(s32[448,15]{0,1:T(8,128)} %param.17), kind=kLoop, calls=%fused_computation | loop fusion | flops 18292736 | bytes 1689856 | tf_op jit(solution)/shard_map/reduce_sum | solution.py:64
  39.8 0.2 fusion.42
  40.0 6.1 %all-to-all-done = bf16[128,2,128]{2,1,0:T(2,128)(2,1)S(1)} async-done(((bf16[128,2,128]{2,1,0:T(2,128)(2,1)}), bf16[128,2,128]{2,1,0:T(2,128)(2,1)S(1)}, u32[]{:S(2)}, u32[]{:S(2)}) %all-to-all-start) | async-done | bytes 65568 | tf_op jit(solution)/shard_map/all_to_all | solution.py:32
  46.1 0.4 fusion.4
  46.6 1.3 %multiply_convert_fusion = bf16[448,256]{1,0:T(8,128)(2,1)S(1)} fusion(f32[448,256]{1,0:T(8,128)S(1)} %fusion.42, bf16[448,128]{1,0:T(8,128)(2,1)S(1)} %fusion.4, bf16[128,256]{1,0:T(8,128)(2,1)S(1)} %copy-done.14, bf16[448,256]{1,0:T(8,128)(2,1)} %param.14, f32[256]{0:T(256)S(1)} %copy-done.16), kind=kOutput, calls=%fused_computation.19 | convolution fusion | flops 30736384 | bytes 1098752 | tf_op jit(solution)/shard_map/dot_general | solution.py:69
  47.9 0.9 fusion.38
  48.8 4.4 %collective-permute-start.6 = (bf16[704,256]{1,0:T(8,128)(2,1)}, bf16[704,256]{1,0:T(8,128)(2,1)S(1)}, u32[]{:S(2)}, u32[]{:S(2)}) collective-permute-start(bf16[704,256]{1,0:T(8,128)(2,1)} %get-tuple-element.27), channel_id=1, source_target_pairs={{0,3},{1,0},{2,1},{3,2},{4,7},{5,4},{6,5},{7,6},{8,11},{9,8},{10,9... | collective-permute-start | bytes 1081352 | tf_op jit(solution)/shard_map/ppermute | solution.py:16
  53.2 2.4 %collective-permute-start.5 = (bf16[704,256]{1,0:T(8,128)(2,1)}, bf16[704,256]{1,0:T(8,128)(2,1)S(1)}, u32[]{:S(2)}, u32[]{:S(2)}) collective-permute-start(bf16[704,256]{1,0:T(8,128)(2,1)} %get-tuple-element.27), channel_id=1, source_target_pairs={{0,2},{1,3},{2,0},{3,1},{4,6},{5,7},{6,4},{7,5},{8,10},{9,11},{10,... | collective-permute-start | bytes 1081352 | tf_op jit(solution)/shard_map/ppermute | solution.py:16
  55.6 2.5 %collective-permute-start.4 = (bf16[704,256]{1,0:T(8,128)(2,1)}, bf16[704,256]{1,0:T(8,128)(2,1)S(1)}, u32[]{:S(2)}, u32[]{:S(2)}) collective-permute-start(bf16[704,256]{1,0:T(8,128)(2,1)} %get-tuple-element.27), channel_id=1, source_target_pairs={{0,1},{1,2},{2,3},{3,0},{4,5},{5,6},{6,7},{7,4},{8,9},{9,10},{10,1... | collective-permute-start | bytes 1081352 | tf_op jit(solution)/shard_map/ppermute | solution.py:16
  58.1 0.2 fusion.45
  58.4 0.2 fusion.44
  58.7 0.8 pad_maximum_fusion.3
  59.5 8.6 %all-to-all-start.1 = ((f32[128,4,128]{2,1,0:T(4,128)}), f32[128,4,128]{2,1,0:T(4,128)S(1)}, u32[]{:S(2)}, u32[]{:S(2)}) async-start(f32[128,4,128]{2,1,0:T(4,128)} %pad_maximum_fusion.3), calls=%async_computation.1 | async-start | bytes 524288 | tf_op jit(solution)/shard_map/all_to_all | solution.py:83
  68.1 6.7 %collective-permute-done.4 = bf16[704,256]{1,0:T(8,128)(2,1)S(1)} collective-permute-done((bf16[704,256]{1,0:T(8,128)(2,1)}, bf16[704,256]{1,0:T(8,128)(2,1)S(1)}, u32[]{:S(2)}, u32[]{:S(2)}) %collective-permute-start.4) | collective-permute-done | bytes 360480 | tf_op jit(solution)/shard_map/ppermute | solution.py:16
  74.8 0.7 copy-done.8
  75.6 1.6 %pad_maximum_fusion = bf16[4,704,256]{2,1,0:T(8,128)(2,1)S(1)} fusion(bf16[1,704,256]{2,1,0:T(8,128)(2,1)} %bitcast.33, bf16[1,704,256]{2,1,0:T(8,128)(2,1)} %bitcast.36, bf16[1,704,256]{2,1,0:T(8,128)(2,1)} %bitcast.39, bf16[1,704,256]{2,1,0:T(8,128)(2,1)} %get-tuple-element.26), kind=kLoop, calls=%fused_computation.2 | loop fusion | flops 2162688 | bytes 2883584 | tf_op jit(solution)/shard_map/stack | solution.py:76
  77.3 0.4 fusion.2
  77.7 3.4 %fusion.43 = f32[928,128]{1,0:T(8,128)S(1)} fusion(f32[448,928]{1,0:T(8,128)S(1)} %convert_reduce_fusion, f32[448,128]{1,0:T(8,128)S(1)} %fusion.2), kind=kOutput, calls=%fused_computation.70 | convolution fusion | flops 638582784 | bytes 2367488 | tf_op jit(solution)/shard_map/dot_general | solution.py:24
  81.1 0.8 copy-done.11
  81.9 1.4 %all-to-all-done.1 = f32[128,4,128]{2,1,0:T(4,128)S(1)} async-done(((f32[128,4,128]{2,1,0:T(4,128)}), f32[128,4,128]{2,1,0:T(4,128)S(1)}, u32[]{:S(2)}, u32[]{:S(2)}) %all-to-all-start.1) | async-done | bytes 262176 | tf_op jit(solution)/shard_map/all_to_all | solution.py:83
  83.3 0.1 reduce_sum.37
  83.5 0.9 pad_maximum_fusion.1
  84.4 6.9 %all-to-all-start.2 = ((f32[128,6,128]{2,1,0:T(8,128)}), f32[128,6,128]{2,1,0:T(8,128)}, u32[]{:S(2)}, u32[]{:S(2)}) async-start(f32[128,6,128]{2,1,0:T(8,128)} %pad_maximum_fusion.1), calls=%async_computation.2 | async-start | bytes 1048576 | tf_op jit(solution)/shard_map/all_to_all | solution.py:110
  91.4 0.8 fusion.39
  92.2 7.3 %collective-permute-start.10 = (f32[56,128]{1,0:T(8,128)S(1)}, f32[56,128]{1,0:T(8,128)S(1)}, u32[]{:S(2)}, u32[]{:S(2)}) collective-permute-start(f32[56,128]{1,0:T(8,128)S(1)} %get-tuple-element.21), channel_id=1, source_target_pairs={{0,504},{4,508},{8,0},{12,4},{16,8},{20,12},{24,16},{28,20},{32,24... | collective-permute-start | bytes 86024 | tf_op jit(solution)/shard_map/ppermute | solution.py:16
  99.5 2.6 %collective-permute-start.9 = (f32[56,128]{1,0:T(8,128)S(1)}, f32[56,128]{1,0:T(8,128)S(1)}, u32[]{:S(2)}, u32[]{:S(2)}) collective-permute-start(f32[56,128]{1,0:T(8,128)S(1)} %get-tuple-element.22), channel_id=1, source_target_pairs={{0,508},{4,0},{8,4},{12,8},{16,12},{20,16},{24,20},{28,24},{32,28}... | collective-permute-start | bytes 86024 | tf_op jit(solution)/shard_map/ppermute | solution.py:16
  102.1 3.0 %collective-permute-start.8 = (f32[56,128]{1,0:T(8,128)S(1)}, f32[56,128]{1,0:T(8,128)S(1)}, u32[]{:S(2)}, u32[]{:S(2)}) collective-permute-start(f32[56,128]{1,0:T(8,128)S(1)} %get-tuple-element.23), channel_id=1, source_target_pairs={{0,4},{4,8},{8,12},{12,16},{16,20},{20,24},{24,28},{28,32},{32,36}... | collective-permute-start | bytes 86024 | tf_op jit(solution)/shard_map/ppermute | solution.py:16
  105.1 1.9 %collective-permute-start.7 = (f32[56,128]{1,0:T(8,128)S(1)}, f32[56,128]{1,0:T(8,128)S(1)}, u32[]{:S(2)}, u32[]{:S(2)}) collective-permute-start(f32[56,128]{1,0:T(8,128)S(1)} %get-tuple-element.20), channel_id=1, source_target_pairs={{0,8},{4,12},{8,16},{12,20},{16,24},{20,28},{24,32},{28,36},{32,40... | collective-permute-start | bytes 86024 | tf_op jit(solution)/shard_map/ppermute | solution.py:16
  107.1 1.3 %fusion.3 = f32[448,128]{1,0:T(8,128)S(1)} fusion(bf16[4,704,256]{2,1,0:T(8,128)(2,1)S(1)} %pad_maximum_fusion, bf16[1,704,256]{2,1,0:T(8,128)(2,1)S(1)} %bitcast.35, bf16[1,704,256]{2,1,0:T(8,128)(2,1)S(1)} %bitcast.38, bf16[1,704,256]{2,1,0:T(8,128)(2,1)S(1)} %bitcast.41, bf16[1,704,256]{2,1,0:T(8,128)(2,1)S(1)} %copy-done.1, f32[928,128]{1,0:T(8,128)} %copy-done.11), kind=kOutput, calls=%fused_computation.11 | convolution fusion | flops 118546432 | bytes 2818048 | tf_op jit(solution)/shard_map/dot_general | solution.py:89
  108.4 3.3 %all-to-all-done.2 = f32[128,6,128]{2,1,0:T(8,128)} async-done(((f32[128,6,128]{2,1,0:T(8,128)}), f32[128,6,128]{2,1,0:T(8,128)}, u32[]{:S(2)}, u32[]{:S(2)}) %all-to-all-start.2) | async-done | bytes 393248 | tf_op jit(solution)/shard_map/all_to_all | solution.py:110
  111.7 1.2 %copy.27 = f32[128,6,128]{0,2,1:T(8,128)S(1)} copy(f32[128,6,128]{2,1,0:T(8,128)} %all-to-all-done.2) | data formatting | bytes 786432 | tf_op jit(solution)/shard_map/all_to_all | solution.py:110
  113.0 0.1 fusion.40
  113.2 0.4 fusion.31
  113.7 0.8 multiply_reduce_fusion
  114.5 0.2 add_convert_fusion
  114.7 0.7 copy.30
  115.5 0.7 squeeze.6
  116.3 0.7 squeeze.7
  (56 shorter events, 0.8 us)
Async XLA Ops:
  1.4 38.3 %copy-start.13 = (bf16[128,256]{1,0:T(8,128)(2,1)S(1)}, bf16[128,256]{1,0:T(8,128)(2,1)}, u32[]{:S(2)}) copy-start(bf16[128,256]{1,0:T(8,128)(2,1)} %param.11) | copy-start | bytes 196612
  2.7 37.2 %collective-permute-start = (bf16[56,128]{1,0:T(8,128)(2,1)S(1)}, bf16[56,128]{1,0:T(8,128)(2,1)S(1)}, u32[]{:S(2)}, u32[]{:S(2)}) collective-permute-start(bf16[56,128]{1,0:T(8,128)(2,1)S(1)} %get-tuple-element.31), channel_id=1, source_target_pairs={{0,504},{4,508},{8,0},{12,4},{16,8},{20,12},{24,16},{28,20},{32,24... | collective-permute-start | bytes 43016 | tf_op jit(solution)/shard_map/ppermute | solution.py:16
  17.1 22.9 %collective-permute-start.1 = (bf16[56,128]{1,0:T(8,128)(2,1)S(1)}, bf16[56,128]{1,0:T(8,128)(2,1)S(1)}, u32[]{:S(2)}, u32[]{:S(2)}) collective-permute-start(bf16[56,128]{1,0:T(8,128)(2,1)S(1)} %get-tuple-element.30), channel_id=1, source_target_pairs={{0,508},{4,0},{8,4},{12,8},{16,12},{20,16},{24,20},{28,24},{32,28}... | collective-permute-start | bytes 43016 | tf_op jit(solution)/shard_map/ppermute | solution.py:16
  20.0 20.0 %collective-permute-start.2 = (bf16[56,128]{1,0:T(8,128)(2,1)S(1)}, bf16[56,128]{1,0:T(8,128)(2,1)S(1)}, u32[]{:S(2)}, u32[]{:S(2)}) collective-permute-start(bf16[56,128]{1,0:T(8,128)(2,1)S(1)} %get-tuple-element.29), channel_id=1, source_target_pairs={{0,4},{4,8},{8,12},{12,16},{16,20},{20,24},{24,28},{28,32},{32,36}... | collective-permute-start | bytes 43016 | tf_op jit(solution)/shard_map/ppermute | solution.py:16
  22.7 17.3 %collective-permute-start.3 = (bf16[56,128]{1,0:T(8,128)(2,1)S(1)}, bf16[56,128]{1,0:T(8,128)(2,1)S(1)}, u32[]{:S(2)}, u32[]{:S(2)}) collective-permute-start(bf16[56,128]{1,0:T(8,128)(2,1)S(1)} %get-tuple-element.28), channel_id=1, source_target_pairs={{0,8},{4,12},{8,16},{12,20},{16,24},{20,28},{24,32},{28,36},{32,40... | collective-permute-start | bytes 43016 | tf_op jit(solution)/shard_map/ppermute | solution.py:16
  26.1 20.0 %all-to-all-start = ((bf16[128,2,128]{2,1,0:T(2,128)(2,1)}), bf16[128,2,128]{2,1,0:T(2,128)(2,1)S(1)}, u32[]{:S(2)}, u32[]{:S(2)}) async-start(bf16[128,2,128]{2,1,0:T(2,128)(2,1)} %broadcast_in_dim.4), calls=%async_computation | async-start | bytes 131072 | tf_op jit(solution)/shard_map/all_to_all | solution.py:32
  39.7 6.8 %copy-start.14 = (bf16[128,256]{1,0:T(8,128)(2,1)S(1)}, bf16[128,256]{1,0:T(8,128)(2,1)}, u32[]{:S(2)}) copy-start(bf16[128,256]{1,0:T(8,128)(2,1)} %param.12) | copy-start | bytes 196612
  39.7 6.8 %copy-start.16 = (f32[256]{0:T(256)S(1)}, f32[256]{0:T(256)}, u32[]{:S(2)}) copy-start(f32[256]{0:T(256)} %param.13) | copy-start | bytes 3076
  48.8 19.3 %collective-permute-start.6 = (bf16[704,256]{1,0:T(8,128)(2,1)}, bf16[704,256]{1,0:T(8,128)(2,1)S(1)}, u32[]{:S(2)}, u32[]{:S(2)}) collective-permute-start(bf16[704,256]{1,0:T(8,128)(2,1)} %get-tuple-element.27), channel_id=1, source_target_pairs={{0,3},{1,0},{2,1},{3,2},{4,7},{5,4},{6,5},{7,6},{8,11},{9,8},{10,9... | collective-permute-start | bytes 1081352 | tf_op jit(solution)/shard_map/ppermute | solution.py:16
  53.2 14.9 %collective-permute-start.5 = (bf16[704,256]{1,0:T(8,128)(2,1)}, bf16[704,256]{1,0:T(8,128)(2,1)S(1)}, u32[]{:S(2)}, u32[]{:S(2)}) collective-permute-start(bf16[704,256]{1,0:T(8,128)(2,1)} %get-tuple-element.27), channel_id=1, source_target_pairs={{0,2},{1,3},{2,0},{3,1},{4,6},{5,7},{6,4},{7,5},{8,10},{9,11},{10,... | collective-permute-start | bytes 1081352 | tf_op jit(solution)/shard_map/ppermute | solution.py:16
  55.6 19.2 %collective-permute-start.4 = (bf16[704,256]{1,0:T(8,128)(2,1)}, bf16[704,256]{1,0:T(8,128)(2,1)S(1)}, u32[]{:S(2)}, u32[]{:S(2)}) collective-permute-start(bf16[704,256]{1,0:T(8,128)(2,1)} %get-tuple-element.27), channel_id=1, source_target_pairs={{0,1},{1,2},{2,3},{3,0},{4,5},{5,6},{6,7},{7,4},{8,9},{9,10},{10,1... | collective-permute-start | bytes 1081352 | tf_op jit(solution)/shard_map/ppermute | solution.py:16
  59.5 23.8 %all-to-all-start.1 = ((f32[128,4,128]{2,1,0:T(4,128)}), f32[128,4,128]{2,1,0:T(4,128)S(1)}, u32[]{:S(2)}, u32[]{:S(2)}) async-start(f32[128,4,128]{2,1,0:T(4,128)} %pad_maximum_fusion.3), calls=%async_computation.1 | async-start | bytes 524288 | tf_op jit(solution)/shard_map/all_to_all | solution.py:83
  68.1 6.7 %copy-start.2 = (bf16[704,256]{1,0:T(8,128)(2,1)}, bf16[704,256]{1,0:T(8,128)(2,1)S(1)}, u32[]{:S(2)}) copy-start(bf16[704,256]{1,0:T(8,128)(2,1)S(1)} %collective-permute-done.6) | copy-start | bytes 1081348
  68.1 6.7 %copy-start.5 = (bf16[704,256]{1,0:T(8,128)(2,1)}, bf16[704,256]{1,0:T(8,128)(2,1)S(1)}, u32[]{:S(2)}) copy-start(bf16[704,256]{1,0:T(8,128)(2,1)S(1)} %collective-permute-done.5) | copy-start | bytes 1081348
  74.8 0.8 copy-start.8
  75.6 1.6 %copy-start = (bf16[1,704,256]{2,1,0:T(8,128)(2,1)S(1)}, bf16[1,704,256]{2,1,0:T(8,128)(2,1)}, u32[]{:S(2)}) copy-start(bf16[1,704,256]{2,1,0:T(8,128)(2,1)} %get-tuple-element.26) | copy-start | bytes 1081348
  75.6 1.6 %copy-start.3 = (bf16[704,256]{1,0:T(8,128)(2,1)S(1)}, bf16[704,256]{1,0:T(8,128)(2,1)}, u32[]{:S(2)}) copy-start(bf16[704,256]{1,0:T(8,128)(2,1)} %copy-done.2) | copy-start | bytes 1081348
  75.6 1.6 %copy-start.6 = (bf16[704,256]{1,0:T(8,128)(2,1)S(1)}, bf16[704,256]{1,0:T(8,128)(2,1)}, u32[]{:S(2)}) copy-start(bf16[704,256]{1,0:T(8,128)(2,1)} %copy-done.5) | copy-start | bytes 1081348
  75.6 1.7 %copy-start.9 = (bf16[704,256]{1,0:T(8,128)(2,1)S(1)}, bf16[704,256]{1,0:T(8,128)(2,1)}, u32[]{:S(2)}) copy-start(bf16[704,256]{1,0:T(8,128)(2,1)} %copy-done.8) | copy-start | bytes 1081348
  81.1 0.8 copy-start.11
  81.9 25.1 %copy-start.1 = (bf16[1,704,256]{2,1,0:T(8,128)(2,1)S(1)}, bf16[1,704,256]{2,1,0:T(8,128)(2,1)}, u32[]{:S(2)}) copy-start(bf16[1,704,256]{2,1,0:T(8,128)(2,1)} %get-tuple-element.26) | copy-start | bytes 1081348
  81.9 25.1 %copy-start.4 = (bf16[704,256]{1,0:T(8,128)(2,1)S(1)}, bf16[704,256]{1,0:T(8,128)(2,1)}, u32[]{:S(2)}) copy-start(bf16[704,256]{1,0:T(8,128)(2,1)} %copy-done.2) | copy-start | bytes 1081348
  81.9 25.1 %copy-start.7 = (bf16[704,256]{1,0:T(8,128)(2,1)S(1)}, bf16[704,256]{1,0:T(8,128)(2,1)}, u32[]{:S(2)}) copy-start(bf16[704,256]{1,0:T(8,128)(2,1)} %copy-done.5) | copy-start | bytes 1081348
  81.9 25.1 %copy-start.10 = (bf16[704,256]{1,0:T(8,128)(2,1)S(1)}, bf16[704,256]{1,0:T(8,128)(2,1)}, u32[]{:S(2)}) copy-start(bf16[704,256]{1,0:T(8,128)(2,1)} %copy-done.8) | copy-start | bytes 1081348
  84.4 27.3 %all-to-all-start.2 = ((f32[128,6,128]{2,1,0:T(8,128)}), f32[128,6,128]{2,1,0:T(8,128)}, u32[]{:S(2)}, u32[]{:S(2)}) async-start(f32[128,6,128]{2,1,0:T(8,128)} %pad_maximum_fusion.1), calls=%async_computation.2 | async-start | bytes 1048576 | tf_op jit(solution)/shard_map/all_to_all | solution.py:110
  92.2 21.5 %collective-permute-start.10 = (f32[56,128]{1,0:T(8,128)S(1)}, f32[56,128]{1,0:T(8,128)S(1)}, u32[]{:S(2)}, u32[]{:S(2)}) collective-permute-start(f32[56,128]{1,0:T(8,128)S(1)} %get-tuple-element.21), channel_id=1, source_target_pairs={{0,504},{4,508},{8,0},{12,4},{16,8},{20,12},{24,16},{28,20},{32,24... | collective-permute-start | bytes 86024 | tf_op jit(solution)/shard_map/ppermute | solution.py:16
  99.5 14.1 %collective-permute-start.9 = (f32[56,128]{1,0:T(8,128)S(1)}, f32[56,128]{1,0:T(8,128)S(1)}, u32[]{:S(2)}, u32[]{:S(2)}) collective-permute-start(f32[56,128]{1,0:T(8,128)S(1)} %get-tuple-element.22), channel_id=1, source_target_pairs={{0,508},{4,0},{8,4},{12,8},{16,12},{20,16},{24,20},{28,24},{32,28}... | collective-permute-start | bytes 86024 | tf_op jit(solution)/shard_map/ppermute | solution.py:16
  102.1 11.6 %collective-permute-start.8 = (f32[56,128]{1,0:T(8,128)S(1)}, f32[56,128]{1,0:T(8,128)S(1)}, u32[]{:S(2)}, u32[]{:S(2)}) collective-permute-start(f32[56,128]{1,0:T(8,128)S(1)} %get-tuple-element.23), channel_id=1, source_target_pairs={{0,4},{4,8},{8,12},{12,16},{16,20},{20,24},{24,28},{28,32},{32,36}... | collective-permute-start | bytes 86024 | tf_op jit(solution)/shard_map/ppermute | solution.py:16
  105.1 8.6 %collective-permute-start.7 = (f32[56,128]{1,0:T(8,128)S(1)}, f32[56,128]{1,0:T(8,128)S(1)}, u32[]{:S(2)}, u32[]{:S(2)}) collective-permute-start(f32[56,128]{1,0:T(8,128)S(1)} %get-tuple-element.20), channel_id=1, source_target_pairs={{0,8},{4,12},{8,16},{12,20},{16,24},{20,28},{24,32},{28,36},{32,40... | collective-permute-start | bytes 86024 | tf_op jit(solution)/shard_map/ppermute | solution.py:16
  108.4 4.8 %copy-start.15 = (s32[1,2]{1,0:T(1,128)S(1)}, s32[1,2]{1,0:T(1,128)}, u32[]{:S(2)}) copy-start(s32[1,2]{1,0:T(1,128)} %param.15) | copy-start | bytes 28
  108.4 6.0 %copy-start.12 = (bf16[448,128]{1,0:T(8,128)(2,1)S(1)}, bf16[448,128]{1,0:T(8,128)(2,1)}, u32[]{:S(2)}) copy-start(bf16[448,128]{1,0:T(8,128)(2,1)} %param.10) | copy-start | bytes 344068

commit v5 on v4

--- a/solution.py
+++ b/solution.py
@@ -57,7 +57,9 @@
         from_behind(halo_out[o * slots : (o + 1) * slots], "dom", offset_of(o))
         for o in range(NOFF)
     ]
-    hubs = gather_all(hub_out, "dom").reshape(dom_count * hub_dev, feat_in)
+    pad_rows = 8 - hub_dev % 8 if hub_dev % 8 else 0
+    hub_tile = jnp.pad(hub_out, ((0, pad_rows), (0, 0)))
+    hubs = gather_all(hub_tile, "dom")[:, :hub_dev].reshape(dom_count * hub_dev, feat_in)
     table = jnp.concatenate([perturbed] + pieces + [hubs], 0)
 
     t_iota = lax.broadcasted_iota(jnp.int32, (rows_here, K, table_rows), 2)
@@ -107,9 +109,9 @@
     hub_chunks = table_grad[rows_here + halo_rows :].reshape(dom_count, hub_dev, feat_in)
     weight_rep = jnp.broadcast_to(weight_part[None], (dom_count,) + weight_part.shape)
     sent = jnp.concatenate([hub_chunks, weight_rep], 1)
-    recv = lax.all_to_all(sent, "dom", 0, 0, tiled=True).reshape(dom_count, -1)
-    hub_total = jnp.sum(recv[:, : hub_dev * feat_in], axis=0).reshape(hub_dev, feat_in)
-    weights = recv[:, hub_dev * feat_in :].reshape(2, feat_in, hidden_here)
+    recv = lax.all_to_all(sent, "dom", 0, 0, tiled=True)
+    hub_total = jnp.sum(recv[:, :hub_dev], axis=0)
+    weights = recv[:, hub_dev:].reshape(2, feat_in, hidden_here)
 
     grad_in = own_grad + table_grad[:rows_here]
     grad_in = grad_in + contract_rows(pick.astype(F32), returned, HIGH)

time: 118 us -> 121 us (1.025)
  waiting for transfers between devices: 17.5 us -> 23.5 us
  starting transfers between devices: 70.1 us -> 68.1 us
    all_to_all x1, waiting for transfers between devices: 6.07 us -> 11.2 us  [gather_all(): out = lax.all_to_all(rep, axis, 0, 0, tiled=True)]
    ppermute x11, waiting for transfers between devices: 6.74 us -> 9.06 us  [from_behind(): return lax.ppermute(x, axis, [(i, (i + by) % size) for i in range(size)])]
    all_to_all x1, starting transfers between devices: 8.57 us -> 6.37 us  [per_device(): lax.all_to_all(weight_flat.reshape(dom_count, -1, 128), 'dom', 0, 0, tile...]
    all_to_all x1, waiting for transfers between devices: 1.37 us -> 0.01 us  [per_device(): lax.all_to_all(weight_flat.reshape(dom_count, -1, 128), 'dom', 0, 0, tile...]
    reduce_sum x1, other arithmetic: 5.01 us -> 3.65 us  [per_device(): counts = jnp.sum((neighbors[:, :, None] == t_iota).astype(F32), axis=1)]
    unnamed x39 -> x41, local copies, waits for them, and re-layouts: 2.43 us -> 2.45 us
  transfers between devices with their start and end apart: 14 -> 14, of which waited for: 4 -> 5; matrix products, arithmetic and copies ran while one was open for 15% -> 13% of each run, Pallas kernels for 0% -> 0%
where the time goes in v5:
time: 121 us; the launch traced here: 120 us
  starting transfers between devices  68.1 us (56%)
  waiting for transfers between devices  23.5 us (19%)
  other arithmetic  10.4 us (9%)
  matrix products  9.76 us (8%)
  local copies, waits for them, and re-layouts  7.55 us (6%)
    ppermute x11, starting transfers between devices, from_behind(): return lax.ppermute(x, axis, [(i, (i + by) % size) for i in range(size)])  46.3 us
    all_to_all x1, waiting for transfers between devices, gather_all(): out = lax.all_to_all(rep, axis, 0, 0, tiled=True)  11.2 us
    ppermute x11, waiting for transfers between devices, from_behind(): return lax.ppermute(x, axis, [(i, (i + by) % size) for i in range(size)])  9.06 us
    all_to_all x1, starting transfers between devices, gather_all(): out = lax.all_to_all(rep, axis, 0, 0, tiled=True)  8.57 us
    all_to_all x1, starting transfers between devices, per_device(): recv = lax.all_to_all(sent, 'dom', 0, 0, tiled=True)  6.9 us
    all_to_all x1, starting transfers between devices, per_device(): lax.all_to_all(weight_flat.reshape(dom_count, -1, 128), 'dom', 0, 0, tile...  6.37 us
    dot_general x5, matrix products, contract_rows(): lax.dot_general(left, right, (((0,), (0,)), ((), ())), preferred_element_...  5.04 us
    reduce_sum x1, other arithmetic, per_device(): counts = jnp.sum((neighbors[:, :, None] == t_iota).astype(F32), axis=1)  3.65 us
  transfers between devices with their start and end apart: 14, of which 5 were waited for; matrix products, arithmetic and copies ran while one was open for 13% of the time, Pallas kernels for 0%

profile of v5, /device:TPU:1, one launch (start us, length us, event | category | flops | bytes accessed | tf_op | source)
XLA Modules:
  0.0 120.4 jit_solution(6114552086365579004)
XLA Ops:
  0.6 0.8 eq.30
  1.4 1.0 constant_dynamic-update-slice_fusion.5
  2.4 0.3 convolution_convert_fusion
  2.7 14.4 %collective-permute-start = (bf16[56,128]{1,0:T(8,128)(2,1)S(1)}, bf16[56,128]{1,0:T(8,128)(2,1)S(1)}, u32[]{:S(2)}, u32[]{:S(2)}) collective-permute-start(bf16[56,128]{1,0:T(8,128)(2,1)S(1)} %get-tuple-element.22), channel_id=1, source_target_pairs={{0,504},{4,508},{8,0},{12,4},{16,8},{20,12},{24,16},{28,20},{32,24... | collective-permute-start | bytes 43016 | tf_op jit(solution)/shard_map/ppermute | solution.py:16
  17.1 2.9 %collective-permute-start.1 = (bf16[56,128]{1,0:T(8,128)(2,1)S(1)}, bf16[56,128]{1,0:T(8,128)(2,1)S(1)}, u32[]{:S(2)}, u32[]{:S(2)}) collective-permute-start(bf16[56,128]{1,0:T(8,128)(2,1)S(1)} %get-tuple-element.21), channel_id=1, source_target_pairs={{0,508},{4,0},{8,4},{12,8},{16,12},{20,16},{24,20},{28,24},{32,28}... | collective-permute-start | bytes 43016 | tf_op jit(solution)/shard_map/ppermute | solution.py:16
  20.0 2.7 %collective-permute-start.2 = (bf16[56,128]{1,0:T(8,128)(2,1)S(1)}, bf16[56,128]{1,0:T(8,128)(2,1)S(1)}, u32[]{:S(2)}, u32[]{:S(2)}) collective-permute-start(bf16[56,128]{1,0:T(8,128)(2,1)S(1)} %get-tuple-element.20), channel_id=1, source_target_pairs={{0,4},{4,8},{8,12},{12,16},{16,20},{20,24},{24,28},{28,32},{32,36}... | collective-permute-start | bytes 43016 | tf_op jit(solution)/shard_map/ppermute | solution.py:16
  22.7 1.9 %collective-permute-start.3 = (bf16[56,128]{1,0:T(8,128)(2,1)S(1)}, bf16[56,128]{1,0:T(8,128)(2,1)S(1)}, u32[]{:S(2)}, u32[]{:S(2)}) collective-permute-start(bf16[56,128]{1,0:T(8,128)(2,1)S(1)} %get-tuple-element.19), channel_id=1, source_target_pairs={{0,8},{4,12},{8,16},{12,20},{16,24},{20,28},{24,32},{28,36},{32,40... | collective-permute-start | bytes 43016 | tf_op jit(solution)/shard_map/ppermute | solution.py:16
  24.6 0.8 convolution_convert_fusion.1
  25.5 0.7 broadcast_in_dim.4
  26.2 8.6 %all-to-all-start = ((bf16[128,8,128]{2,1,0:T(8,128)(2,1)}), bf16[128,8,128]{2,1,0:T(8,128)(2,1)S(1)}, u32[]{:S(2)}, u32[]{:S(2)}) async-start(bf16[128,8,128]{2,1,0:T(8,128)(2,1)} %broadcast_in_dim.4), calls=%async_computation | async-start | bytes 524288 | tf_op jit(solution)/shard_map/all_to_all | solution.py:32
  34.8 3.6 %convert_reduce_fusion = f32[448,928]{1,0:T(8,128)S(1)} fusion(s32[448,15]{0,1:T(8,128)S(1)} %copy-done.15), kind=kLoop, calls=%fused_computation | loop fusion | flops 18292736 | bytes 1689856 | tf_op jit(solution)/shard_map/reduce_sum | solution.py:66
  38.4 0.2 fusion.41
  38.8 11.2 %all-to-all-done = bf16[128,8,128]{2,1,0:T(8,128)(2,1)S(1)} async-done(((bf16[128,8,128]{2,1,0:T(8,128)(2,1)}), bf16[128,8,128]{2,1,0:T(8,128)(2,1)S(1)}, u32[]{:S(2)}, u32[]{:S(2)}) %all-to-all-start) | async-done | bytes 262176 | tf_op jit(solution)/shard_map/all_to_all | solution.py:32
  50.1 0.4 fusion.4
  50.5 1.3 %multiply_convert_fusion = bf16[448,256]{1,0:T(8,128)(2,1)S(1)} fusion(f32[448,256]{1,0:T(8,128)S(1)} %fusion.41, bf16[448,128]{1,0:T(8,128)(2,1)S(1)} %fusion.4, bf16[128,256]{1,0:T(8,128)(2,1)S(1)} %copy-done.14, bf16[448,256]{1,0:T(8,128)(2,1)} %param.14, f32[256]{0:T(256)S(1)} %copy-done.17), kind=kOutput, calls=%fused_computation.19 | convolution fusion | flops 30736384 | bytes 1098752 | tf_op jit(solution)/shard_map/dot_general | solution.py:71
  51.8 0.9 fusion.37
  52.7 4.4 %collective-permute-start.6 = (bf16[704,256]{1,0:T(8,128)(2,1)}, bf16[704,256]{1,0:T(8,128)(2,1)S(1)}, u32[]{:S(2)}, u32[]{:S(2)}) collective-permute-start(bf16[704,256]{1,0:T(8,128)(2,1)} %get-tuple-element.18), channel_id=1, source_target_pairs={{0,3},{1,0},{2,1},{3,2},{4,7},{5,4},{6,5},{7,6},{8,11},{9,8},{10,9... | collective-permute-start | bytes 1081352 | tf_op jit(solution)/shard_map/ppermute | solution.py:16
  57.1 2.4 %collective-permute-start.5 = (bf16[704,256]{1,0:T(8,128)(2,1)}, bf16[704,256]{1,0:T(8,128)(2,1)S(1)}, u32[]{:S(2)}, u32[]{:S(2)}) collective-permute-start(bf16[704,256]{1,0:T(8,128)(2,1)} %get-tuple-element.18), channel_id=1, source_target_pairs={{0,2},{1,3},{2,0},{3,1},{4,6},{5,7},{6,4},{7,5},{8,10},{9,11},{10,... | collective-permute-start | bytes 1081352 | tf_op jit(solution)/shard_map/ppermute | solution.py:16
  59.5 2.5 %collective-permute-start.4 = (bf16[704,256]{1,0:T(8,128)(2,1)}, bf16[704,256]{1,0:T(8,128)(2,1)S(1)}, u32[]{:S(2)}, u32[]{:S(2)}) collective-permute-start(bf16[704,256]{1,0:T(8,128)(2,1)} %get-tuple-element.18), channel_id=1, source_target_pairs={{0,1},{1,2},{2,3},{3,0},{4,5},{5,6},{6,7},{7,4},{8,9},{9,10},{10,1... | collective-permute-start | bytes 1081352 | tf_op jit(solution)/shard_map/ppermute | solution.py:16
  62.1 0.2 fusion.44
  62.4 0.2 fusion.43
  62.7 0.8 pad_maximum_fusion.3
  63.4 6.4 %all-to-all-start.1 = ((f32[128,4,128]{2,1,0:T(4,128)}), f32[128,4,128]{2,1,0:T(4,128)S(1)}, u32[]{:S(2)}, u32[]{:S(2)}) async-start(f32[128,4,128]{2,1,0:T(4,128)} %pad_maximum_fusion.3), calls=%async_computation.1 | async-start | bytes 524288 | tf_op jit(solution)/shard_map/all_to_all | solution.py:85
  69.8 0.2 collective-permute-done.5
  70.1 8.7 %collective-permute-done.4 = bf16[704,256]{1,0:T(8,128)(2,1)S(1)} collective-permute-done((bf16[704,256]{1,0:T(8,128)(2,1)}, bf16[704,256]{1,0:T(8,128)(2,1)S(1)}, u32[]{:S(2)}, u32[]{:S(2)}) %collective-permute-start.4) | collective-permute-done | bytes 360480 | tf_op jit(solution)/shard_map/ppermute | solution.py:16
  78.8 0.7 copy-done.8
  79.5 1.6 %pad_maximum_fusion = bf16[4,704,256]{2,1,0:T(8,128)(2,1)S(1)} fusion(bf16[1,704,256]{2,1,0:T(8,128)(2,1)} %bitcast.30, bf16[1,704,256]{2,1,0:T(8,128)(2,1)} %bitcast.33, bf16[1,704,256]{2,1,0:T(8,128)(2,1)} %bitcast.36, bf16[1,704,256]{2,1,0:T(8,128)(2,1)} %get-tuple-element.17), kind=kLoop, calls=%fused_computation.2 | loop fusion | flops 2162688 | bytes 2883584 | tf_op jit(solution)/shard_map/stack | solution.py:78
  81.3 0.4 fusion.2
  81.7 3.4 %fusion.42 = f32[928,128]{1,0:T(8,128)S(1)} fusion(f32[448,928]{1,0:T(8,128)S(1)} %convert_reduce_fusion, f32[448,128]{1,0:T(8,128)S(1)} %fusion.2), kind=kOutput, calls=%fused_computation.69 | convolution fusion | flops 638582784 | bytes 2367488 | tf_op jit(solution)/shard_map/dot_general | solution.py:24
  85.1 0.8 copy-done.11
  85.9 0.1 reduce_sum.37
  86.1 0.9 pad_maximum_fusion.1
  87.0 6.9 %all-to-all-start.2 = ((f32[128,6,128]{2,1,0:T(8,128)}), f32[128,6,128]{2,1,0:T(8,128)}, u32[]{:S(2)}, u32[]{:S(2)}) async-start(f32[128,6,128]{2,1,0:T(8,128)} %pad_maximum_fusion.1), calls=%async_computation.2 | async-start | bytes 1048576 | tf_op jit(solution)/shard_map/all_to_all | solution.py:112
  93.9 0.8 fusion.39
  94.7 7.4 %collective-permute-start.10 = (f32[56,128]{1,0:T(8,128)S(1)}, f32[56,128]{1,0:T(8,128)S(1)}, u32[]{:S(2)}, u32[]{:S(2)}) collective-permute-start(f32[56,128]{1,0:T(8,128)S(1)} %get-tuple-element.14), channel_id=1, source_target_pairs={{0,504},{4,508},{8,0},{12,4},{16,8},{20,12},{24,16},{28,20},{32,24... | collective-permute-start | bytes 86024 | tf_op jit(solution)/shard_map/ppermute | solution.py:16
  102.2 2.6 %collective-permute-start.9 = (f32[56,128]{1,0:T(8,128)S(1)}, f32[56,128]{1,0:T(8,128)S(1)}, u32[]{:S(2)}, u32[]{:S(2)}) collective-permute-start(f32[56,128]{1,0:T(8,128)S(1)} %get-tuple-element.15), channel_id=1, source_target_pairs={{0,508},{4,0},{8,4},{12,8},{16,12},{20,16},{24,20},{28,24},{32,28}... | collective-permute-start | bytes 86024 | tf_op jit(solution)/shard_map/ppermute | solution.py:16
  104.8 3.0 %collective-permute-start.8 = (f32[56,128]{1,0:T(8,128)S(1)}, f32[56,128]{1,0:T(8,128)S(1)}, u32[]{:S(2)}, u32[]{:S(2)}) collective-permute-start(f32[56,128]{1,0:T(8,128)S(1)} %get-tuple-element.16), channel_id=1, source_target_pairs={{0,4},{4,8},{8,12},{12,16},{16,20},{20,24},{24,28},{28,32},{32,36}... | collective-permute-start | bytes 86024 | tf_op jit(solution)/shard_map/ppermute | solution.py:16
  107.8 2.1 %collective-permute-start.7 = (f32[56,128]{1,0:T(8,128)S(1)}, f32[56,128]{1,0:T(8,128)S(1)}, u32[]{:S(2)}, u32[]{:S(2)}) collective-permute-start(f32[56,128]{1,0:T(8,128)S(1)} %get-tuple-element.13), channel_id=1, source_target_pairs={{0,8},{4,12},{8,16},{12,20},{16,24},{20,28},{24,32},{28,36},{32,40... | collective-permute-start | bytes 86024 | tf_op jit(solution)/shard_map/ppermute | solution.py:16
  109.9 1.3 %fusion.3 = f32[448,128]{1,0:T(8,128)S(1)} fusion(bf16[4,704,256]{2,1,0:T(8,128)(2,1)S(1)} %pad_maximum_fusion, bf16[1,704,256]{2,1,0:T(8,128)(2,1)S(1)} %bitcast.32, bf16[1,704,256]{2,1,0:T(8,128)(2,1)S(1)} %bitcast.35, bf16[1,704,256]{2,1,0:T(8,128)(2,1)S(1)} %bitcast.38, bf16[1,704,256]{2,1,0:T(8,128)(2,1)S(1)} %copy-done.1, f32[928,128]{1,0:T(8,128)} %copy-done.11), kind=kOutput, calls=%fused_computation.11 | convolution fusion | flops 118546432 | bytes 2818048 | tf_op jit(solution)/shard_map/dot_general | solution.py:91
  111.2 3.2 %all-to-all-done.2 = f32[128,6,128]{2,1,0:T(8,128)} async-done(((f32[128,6,128]{2,1,0:T(8,128)}), f32[128,6,128]{2,1,0:T(8,128)}, u32[]{:S(2)}, u32[]{:S(2)}) %all-to-all-start.2) | async-done | bytes 393248 | tf_op jit(solution)/shard_map/all_to_all | solution.py:112
  114.4 1.2 slice_reduce_fusion
  115.6 0.4 fusion.31
  116.2 0.8 multiply_reduce_fusion
  116.9 0.2 add_convert_fusion
  117.2 0.7 copy.14
  117.9 1.1 fusion.38
  119.0 0.7 squeeze.6
  119.7 0.7 squeeze.7
  (57 shorter events, 0.6 us)
Async XLA Ops:
  0.6 34.1 %copy-start.15 = (s32[448,15]{0,1:T(8,128)S(1)}, s32[448,15]{0,1:T(8,128)}, u32[]{:S(2)}) copy-start(s32[448,15]{0,1:T(8,128)} %param.17) | copy-start | bytes 80644
  2.7 35.8 %copy-start.13 = (bf16[128,256]{1,0:T(8,128)(2,1)S(1)}, bf16[128,256]{1,0:T(8,128)(2,1)}, u32[]{:S(2)}) copy-start(bf16[128,256]{1,0:T(8,128)(2,1)} %param.11) | copy-start | bytes 196612
  2.7 36.0 %collective-permute-start = (bf16[56,128]{1,0:T(8,128)(2,1)S(1)}, bf16[56,128]{1,0:T(8,128)(2,1)S(1)}, u32[]{:S(2)}, u32[]{:S(2)}) collective-permute-start(bf16[56,128]{1,0:T(8,128)(2,1)S(1)} %get-tuple-element.22), channel_id=1, source_target_pairs={{0,504},{4,508},{8,0},{12,4},{16,8},{20,12},{24,16},{28,20},{32,24... | collective-permute-start | bytes 43016 | tf_op jit(solution)/shard_map/ppermute | solution.py:16
  17.1 21.6 %collective-permute-start.1 = (bf16[56,128]{1,0:T(8,128)(2,1)S(1)}, bf16[56,128]{1,0:T(8,128)(2,1)S(1)}, u32[]{:S(2)}, u32[]{:S(2)}) collective-permute-start(bf16[56,128]{1,0:T(8,128)(2,1)S(1)} %get-tuple-element.21), channel_id=1, source_target_pairs={{0,508},{4,0},{8,4},{12,8},{16,12},{20,16},{24,20},{28,24},{32,28}... | collective-permute-start | bytes 43016 | tf_op jit(solution)/shard_map/ppermute | solution.py:16
  20.0 18.7 %collective-permute-start.2 = (bf16[56,128]{1,0:T(8,128)(2,1)S(1)}, bf16[56,128]{1,0:T(8,128)(2,1)S(1)}, u32[]{:S(2)}, u32[]{:S(2)}) collective-permute-start(bf16[56,128]{1,0:T(8,128)(2,1)S(1)} %get-tuple-element.20), channel_id=1, source_target_pairs={{0,4},{4,8},{8,12},{12,16},{16,20},{20,24},{24,28},{28,32},{32,36}... | collective-permute-start | bytes 43016 | tf_op jit(solution)/shard_map/ppermute | solution.py:16
  22.7 16.1 %collective-permute-start.3 = (bf16[56,128]{1,0:T(8,128)(2,1)S(1)}, bf16[56,128]{1,0:T(8,128)(2,1)S(1)}, u32[]{:S(2)}, u32[]{:S(2)}) collective-permute-start(bf16[56,128]{1,0:T(8,128)(2,1)S(1)} %get-tuple-element.19), channel_id=1, source_target_pairs={{0,8},{4,12},{8,16},{12,20},{16,24},{20,28},{24,32},{28,36},{32,40... | collective-permute-start | bytes 43016 | tf_op jit(solution)/shard_map/ppermute | solution.py:16
  26.2 23.8 %all-to-all-start = ((bf16[128,8,128]{2,1,0:T(8,128)(2,1)}), bf16[128,8,128]{2,1,0:T(8,128)(2,1)S(1)}, u32[]{:S(2)}, u32[]{:S(2)}) async-start(bf16[128,8,128]{2,1,0:T(8,128)(2,1)} %broadcast_in_dim.4), calls=%async_computation | async-start | bytes 524288 | tf_op jit(solution)/shard_map/all_to_all | solution.py:32
  38.6 11.8 %copy-start.14 = (bf16[128,256]{1,0:T(8,128)(2,1)S(1)}, bf16[128,256]{1,0:T(8,128)(2,1)}, u32[]{:S(2)}) copy-start(bf16[128,256]{1,0:T(8,128)(2,1)} %param.12) | copy-start | bytes 196612
  38.7 11.8 %copy-start.17 = (f32[256]{0:T(256)S(1)}, f32[256]{0:T(256)}, u32[]{:S(2)}) copy-start(f32[256]{0:T(256)} %param.13) | copy-start | bytes 3076
  52.7 17.1 %collective-permute-start.6 = (bf16[704,256]{1,0:T(8,128)(2,1)}, bf16[704,256]{1,0:T(8,128)(2,1)S(1)}, u32[]{:S(2)}, u32[]{:S(2)}) collective-permute-start(bf16[704,256]{1,0:T(8,128)(2,1)} %get-tuple-element.18), channel_id=1, source_target_pairs={{0,3},{1,0},{2,1},{3,2},{4,7},{5,4},{6,5},{7,6},{8,11},{9,8},{10,9... | collective-permute-start | bytes 1081352 | tf_op jit(solution)/shard_map/ppermute | solution.py:16
  57.1 13.0 %collective-permute-start.5 = (bf16[704,256]{1,0:T(8,128)(2,1)}, bf16[704,256]{1,0:T(8,128)(2,1)S(1)}, u32[]{:S(2)}, u32[]{:S(2)}) collective-permute-start(bf16[704,256]{1,0:T(8,128)(2,1)} %get-tuple-element.18), channel_id=1, source_target_pairs={{0,2},{1,3},{2,0},{3,1},{4,6},{5,7},{6,4},{7,5},{8,10},{9,11},{10,... | collective-permute-start | bytes 1081352 | tf_op jit(solution)/shard_map/ppermute | solution.py:16
  59.5 19.2 %collective-permute-start.4 = (bf16[704,256]{1,0:T(8,128)(2,1)}, bf16[704,256]{1,0:T(8,128)(2,1)S(1)}, u32[]{:S(2)}, u32[]{:S(2)}) collective-permute-start(bf16[704,256]{1,0:T(8,128)(2,1)} %get-tuple-element.18), channel_id=1, source_target_pairs={{0,1},{1,2},{2,3},{3,0},{4,5},{5,6},{6,7},{7,4},{8,9},{9,10},{10,1... | collective-permute-start | bytes 1081352 | tf_op jit(solution)/shard_map/ppermute | solution.py:16
  63.4 22.5 %all-to-all-start.1 = ((f32[128,4,128]{2,1,0:T(4,128)}), f32[128,4,128]{2,1,0:T(4,128)S(1)}, u32[]{:S(2)}, u32[]{:S(2)}) async-start(f32[128,4,128]{2,1,0:T(4,128)} %pad_maximum_fusion.3), calls=%async_computation.1 | async-start | bytes 524288 | tf_op jit(solution)/shard_map/all_to_all | solution.py:85
  69.8 9.0 %copy-start.2 = (bf16[704,256]{1,0:T(8,128)(2,1)}, bf16[704,256]{1,0:T(8,128)(2,1)S(1)}, u32[]{:S(2)}) copy-start(bf16[704,256]{1,0:T(8,128)(2,1)S(1)} %collective-permute-done.6) | copy-start | bytes 1081348
  70.1 8.7 %copy-start.5 = (bf16[704,256]{1,0:T(8,128)(2,1)}, bf16[704,256]{1,0:T(8,128)(2,1)S(1)}, u32[]{:S(2)}) copy-start(bf16[704,256]{1,0:T(8,128)(2,1)S(1)} %collective-permute-done.5) | copy-start | bytes 1081348
  78.8 0.8 copy-start.8
  79.5 1.6 %copy-start = (bf16[1,704,256]{2,1,0:T(8,128)(2,1)S(1)}, bf16[1,704,256]{2,1,0:T(8,128)(2,1)}, u32[]{:S(2)}) copy-start(bf16[1,704,256]{2,1,0:T(8,128)(2,1)} %get-tuple-element.17) | copy-start | bytes 1081348
  79.5 1.6 %copy-start.3 = (bf16[704,256]{1,0:T(8,128)(2,1)S(1)}, bf16[704,256]{1,0:T(8,128)(2,1)}, u32[]{:S(2)}) copy-start(bf16[704,256]{1,0:T(8,128)(2,1)} %copy-done.2) | copy-start | bytes 1081348
  79.5 1.6 %copy-start.6 = (bf16[704,256]{1,0:T(8,128)(2,1)S(1)}, bf16[704,256]{1,0:T(8,128)(2,1)}, u32[]{:S(2)}) copy-start(bf16[704,256]{1,0:T(8,128)(2,1)} %copy-done.5) | copy-start | bytes 1081348
  79.5 1.7 %copy-start.9 = (bf16[704,256]{1,0:T(8,128)(2,1)S(1)}, bf16[704,256]{1,0:T(8,128)(2,1)}, u32[]{:S(2)}) copy-start(bf16[704,256]{1,0:T(8,128)(2,1)} %copy-done.8) | copy-start | bytes 1081348
  85.1 0.8 copy-start.11
  85.9 24.0 %copy-start.1 = (bf16[1,704,256]{2,1,0:T(8,128)(2,1)S(1)}, bf16[1,704,256]{2,1,0:T(8,128)(2,1)}, u32[]{:S(2)}) copy-start(bf16[1,704,256]{2,1,0:T(8,128)(2,1)} %get-tuple-element.17) | copy-start | bytes 1081348
  85.9 24.0 %copy-start.4 = (bf16[704,256]{1,0:T(8,128)(2,1)S(1)}, bf16[704,256]{1,0:T(8,128)(2,1)}, u32[]{:S(2)}) copy-start(bf16[704,256]{1,0:T(8,128)(2,1)} %copy-done.2) | copy-start | bytes 1081348
  85.9 24.0 %copy-start.7 = (bf16[704,256]{1,0:T(8,128)(2,1)S(1)}, bf16[704,256]{1,0:T(8,128)(2,1)}, u32[]{:S(2)}) copy-start(bf16[704,256]{1,0:T(8,128)(2,1)} %copy-done.5) | copy-start | bytes 1081348
  85.9 24.0 %copy-start.10 = (bf16[704,256]{1,0:T(8,128)(2,1)S(1)}, bf16[704,256]{1,0:T(8,128)(2,1)}, u32[]{:S(2)}) copy-start(bf16[704,256]{1,0:T(8,128)(2,1)} %copy-done.8) | copy-start | bytes 1081348
  87.0 27.4 %all-to-all-start.2 = ((f32[128,6,128]{2,1,0:T(8,128)}), f32[128,6,128]{2,1,0:T(8,128)}, u32[]{:S(2)}, u32[]{:S(2)}) async-start(f32[128,6,128]{2,1,0:T(8,128)} %pad_maximum_fusion.1), calls=%async_computation.2 | async-start | bytes 1048576 | tf_op jit(solution)/shard_map/all_to_all | solution.py:112
  94.7 21.3 %collective-permute-start.10 = (f32[56,128]{1,0:T(8,128)S(1)}, f32[56,128]{1,0:T(8,128)S(1)}, u32[]{:S(2)}, u32[]{:S(2)}) collective-permute-start(f32[56,128]{1,0:T(8,128)S(1)} %get-tuple-element.14), channel_id=1, source_target_pairs={{0,504},{4,508},{8,0},{12,4},{16,8},{20,12},{24,16},{28,20},{32,24... | collective-permute-start | bytes 86024 | tf_op jit(solution)/shard_map/ppermute | solution.py:16
  102.2 13.9 %collective-permute-start.9 = (f32[56,128]{1,0:T(8,128)S(1)}, f32[56,128]{1,0:T(8,128)S(1)}, u32[]{:S(2)}, u32[]{:S(2)}) collective-permute-start(f32[56,128]{1,0:T(8,128)S(1)} %get-tuple-element.15), channel_id=1, source_target_pairs={{0,508},{4,0},{8,4},{12,8},{16,12},{20,16},{24,20},{28,24},{32,28}... | collective-permute-start | bytes 86024 | tf_op jit(solution)/shard_map/ppermute | solution.py:16
  104.8 11.3 %collective-permute-start.8 = (f32[56,128]{1,0:T(8,128)S(1)}, f32[56,128]{1,0:T(8,128)S(1)}, u32[]{:S(2)}, u32[]{:S(2)}) collective-permute-start(f32[56,128]{1,0:T(8,128)S(1)} %get-tuple-element.16), channel_id=1, source_target_pairs={{0,4},{4,8},{8,12},{12,16},{16,20},{20,24},{24,28},{28,32},{32,36}... | collective-permute-start | bytes 86024 | tf_op jit(solution)/shard_map/ppermute | solution.py:16
  107.8 7.8 %copy-start.16 = (s32[1,2]{1,0:T(1,128)S(1)}, s32[1,2]{1,0:T(1,128)}, u32[]{:S(2)}) copy-start(s32[1,2]{1,0:T(1,128)} %param.15) | copy-start | bytes 28
  107.8 9.2 %copy-start.12 = (bf16[448,128]{1,0:T(8,128)(2,1)S(1)}, bf16[448,128]{1,0:T(8,128)(2,1)}, u32[]{:S(2)}) copy-start(bf16[448,128]{1,0:T(8,128)(2,1)} %param.10) | copy-start | bytes 344068
  107.8 8.4 %collective-permute-start.7 = (f32[56,128]{1,0:T(8,128)S(1)}, f32[56,128]{1,0:T(8,128)S(1)}, u32[]{:S(2)}, u32[]{:S(2)}) collective-permute-start(f32[56,128]{1,0:T(8,128)S(1)} %get-tuple-element.13), channel_id=1, source_target_pairs={{0,8},{4,12},{8,16},{12,20},{16,24},{20,28},{24,32},{28,36},{32,40... | collective-permute-start | bytes 86024 | tf_op jit(solution)/shard_map/ppermute | solution.py:16

commit v6 on v4

--- a/solution.py
+++ b/solution.py
@@ -53,11 +53,18 @@
     halo_out = jnp.dot(pick.astype(BF16), perturbed, preferred_element_type=F32).astype(BF16)
     hub_out = jnp.dot(hub_pick.astype(BF16), perturbed, preferred_element_type=F32).astype(BF16)
 
+    halo_pad = -slots % 16
     pieces = [
-        from_behind(halo_out[o * slots : (o + 1) * slots], "dom", offset_of(o))
+        from_behind(
+            jnp.pad(halo_out[o * slots : (o + 1) * slots], ((0, halo_pad), (0, 0))),
+            "dom",
+            offset_of(o),
+        )[:slots]
         for o in range(NOFF)
     ]
-    hubs = gather_all(hub_out, "dom").reshape(dom_count * hub_dev, feat_in)
+    pad_rows = 8 - hub_dev % 8 if hub_dev % 8 else 0
+    hub_tile = jnp.pad(hub_out, ((0, pad_rows), (0, 0)))
+    hubs = gather_all(hub_tile, "dom")[:, :hub_dev].reshape(dom_count * hub_dev, feat_in)
     table = jnp.concatenate([perturbed] + pieces + [hubs], 0)
 
     t_iota = lax.broadcasted_iota(jnp.int32, (rows_here, K, table_rows), 2)

time: 118 us -> 121 us (1.025)
  waiting for transfers between devices: 17.5 us -> 23.5 us
  starting transfers between devices: 70.1 us -> 67.9 us
    all_to_all x1, waiting for transfers between devices: 6.07 us -> 11.2 us  [gather_all(): out = lax.all_to_all(rep, axis, 0, 0, tiled=True)]
    ppermute x11, waiting for transfers between devices: 6.74 us -> 8.98 us  [from_behind(): return lax.ppermute(x, axis, [(i, (i + by) % size) for i in range(size)])]
    all_to_all x1, starting transfers between devices: 8.57 us -> 6.37 us  [per_device(): lax.all_to_all(weight_flat.reshape(dom_count, -1, 128), 'dom', 0, 0, tile...]
    all_to_all x1, waiting for transfers between devices: 1.37 us -> 0.01 us  [per_device(): lax.all_to_all(weight_flat.reshape(dom_count, -1, 128), 'dom', 0, 0, tile...]
    reduce_sum x1, other arithmetic: 5.01 us -> 3.65 us  [per_device(): counts = jnp.sum((neighbors[:, :, None] == t_iota).astype(F32), axis=1)]
    unnamed x39 -> x41, local copies, waits for them, and re-layouts: 2.43 us -> 2.45 us
  transfers between devices with their start and end apart: 14 -> 14, of which waited for: 4 -> 4; matrix products, arithmetic and copies ran while one was open for 15% -> 14% of each run, Pallas kernels for 0% -> 0%
where the time goes in v6:
time: 121 us; the launch traced here: 120 us
  starting transfers between devices  67.9 us (56%)
  waiting for transfers between devices  23.5 us (19%)
  other arithmetic  10.1 us (8%)
  matrix products  9.77 us (8%)
  local copies, waits for them, and re-layouts  7.92 us (7%)
    ppermute x11, starting transfers between devices, from_behind(): return lax.ppermute(x, axis, [(i, (i + by) % size) for i in range(size)])  46.1 us
    all_to_all x1, waiting for transfers between devices, gather_all(): out = lax.all_to_all(rep, axis, 0, 0, tiled=True)  11.2 us
    ppermute x11, waiting for transfers between devices, from_behind(): return lax.ppermute(x, axis, [(i, (i + by) % size) for i in range(size)])  8.98 us
    all_to_all x1, starting transfers between devices, gather_all(): out = lax.all_to_all(rep, axis, 0, 0, tiled=True)  8.57 us
    all_to_all x1, starting transfers between devices, per_device(): recv = lax.all_to_all(sent, 'dom', 0, 0, tiled=True).reshape(dom_count, -1)  6.9 us
    all_to_all x1, starting transfers between devices, per_device(): lax.all_to_all(weight_flat.reshape(dom_count, -1, 128), 'dom', 0, 0, tile...  6.37 us
    dot_general x5, matrix products, contract_rows(): lax.dot_general(left, right, (((0,), (0,)), ((), ())), preferred_element_...  5.04 us
    reduce_sum x1, other arithmetic, per_device(): counts = jnp.sum((neighbors[:, :, None] == t_iota).astype(F32), axis=1)  3.65 us
  transfers between devices with their start and end apart: 14, of which 4 were waited for; matrix products, arithmetic and copies ran while one was open for 14% of the time, Pallas kernels for 0%

profile of v6, /device:TPU:1, one launch (start us, length us, event | category | flops | bytes accessed | tf_op | source)
XLA Modules:
  0.0 120.4 jit_solution(10901926654700803391)
XLA Ops:
  0.6 0.8 eq.30
  1.4 1.0 constant_dynamic-update-slice_fusion.1
  2.4 0.3 convolution_convert_fusion
  2.7 0.7 slice_select_fusion
  3.4 14.4 %collective-permute-start = (bf16[64,128]{1,0:T(8,128)(2,1)S(1)}, bf16[64,128]{1,0:T(8,128)(2,1)S(1)}, u32[]{:S(2)}, u32[]{:S(2)}) collective-permute-start(bf16[64,128]{1,0:T(8,128)(2,1)S(1)} %slice_select_fusion), channel_id=1, source_target_pairs={{0,504},{4,508},{8,0},{12,4},{16,8},{20,12},{24,16},{28,20},{32,24... | collective-permute-start | bytes 49160 | tf_op jit(solution)/shard_map/ppermute | solution.py:16
  17.8 2.9 %collective-permute-start.1 = (bf16[64,128]{1,0:T(8,128)(2,1)S(1)}, bf16[64,128]{1,0:T(8,128)(2,1)S(1)}, u32[]{:S(2)}, u32[]{:S(2)}) collective-permute-start(bf16[64,128]{1,0:T(8,128)(2,1)S(1)} %pad.18), channel_id=1, source_target_pairs={{0,508},{4,0},{8,4},{12,8},{16,12},{20,16},{24,20},{28,24},{32,28}... | collective-permute-start | bytes 49160 | tf_op jit(solution)/shard_map/ppermute | solution.py:16
  20.7 2.7 %collective-permute-start.2 = (bf16[64,128]{1,0:T(8,128)(2,1)S(1)}, bf16[64,128]{1,0:T(8,128)(2,1)S(1)}, u32[]{:S(2)}, u32[]{:S(2)}) collective-permute-start(bf16[64,128]{1,0:T(8,128)(2,1)S(1)} %pad.19), channel_id=1, source_target_pairs={{0,4},{4,8},{8,12},{12,16},{16,20},{20,24},{24,28},{28,32},{32,36}... | collective-permute-start | bytes 49160 | tf_op jit(solution)/shard_map/ppermute | solution.py:16
  23.4 1.9 %collective-permute-start.3 = (bf16[64,128]{1,0:T(8,128)(2,1)S(1)}, bf16[64,128]{1,0:T(8,128)(2,1)S(1)}, u32[]{:S(2)}, u32[]{:S(2)}) collective-permute-start(bf16[64,128]{1,0:T(8,128)(2,1)S(1)} %pad.20), channel_id=1, source_target_pairs={{0,8},{4,12},{8,16},{12,20},{16,24},{20,28},{24,32},{28,36},{32,40... | collective-permute-start | bytes 49160 | tf_op jit(solution)/shard_map/ppermute | solution.py:16
  25.4 0.8 convolution_convert_fusion.1
  26.2 0.7 broadcast_in_dim.4
  27.0 8.6 %all-to-all-start = ((bf16[128,8,128]{2,1,0:T(8,128)(2,1)}), bf16[128,8,128]{2,1,0:T(8,128)(2,1)S(1)}, u32[]{:S(2)}, u32[]{:S(2)}) async-start(bf16[128,8,128]{2,1,0:T(8,128)(2,1)} %broadcast_in_dim.4), calls=%async_computation | async-start | bytes 524288 | tf_op jit(solution)/shard_map/all_to_all | solution.py:32
  35.5 3.6 %convert_reduce_fusion = f32[448,928]{1,0:T(8,128)S(1)} fusion(s32[448,15]{0,1:T(8,128)S(1)} %copy-done.15), kind=kLoop, calls=%fused_computation | loop fusion | flops 18292736 | bytes 1689856 | tf_op jit(solution)/shard_map/reduce_sum | solution.py:71
  39.2 0.2 fusion.42
  39.5 11.2 %all-to-all-done = bf16[128,8,128]{2,1,0:T(8,128)(2,1)S(1)} async-done(((bf16[128,8,128]{2,1,0:T(8,128)(2,1)}), bf16[128,8,128]{2,1,0:T(8,128)(2,1)S(1)}, u32[]{:S(2)}, u32[]{:S(2)}) %all-to-all-start) | async-done | bytes 262176 | tf_op jit(solution)/shard_map/all_to_all | solution.py:32
  50.8 0.4 fusion.4
  51.3 1.3 %multiply_convert_fusion = bf16[448,256]{1,0:T(8,128)(2,1)S(1)} fusion(f32[448,256]{1,0:T(8,128)S(1)} %fusion.42, bf16[448,128]{1,0:T(8,128)(2,1)S(1)} %fusion.4, bf16[128,256]{1,0:T(8,128)(2,1)S(1)} %copy-done.14, bf16[448,256]{1,0:T(8,128)(2,1)} %param.14, f32[256]{0:T(256)S(1)} %copy-done.17), kind=kOutput, calls=%fused_computation.19 | convolution fusion | flops 30736384 | bytes 1098752 | tf_op jit(solution)/shard_map/dot_general | solution.py:76
  52.5 0.9 fusion.38
  53.5 4.4 %collective-permute-start.6 = (bf16[704,256]{1,0:T(8,128)(2,1)}, bf16[704,256]{1,0:T(8,128)(2,1)S(1)}, u32[]{:S(2)}, u32[]{:S(2)}) collective-permute-start(bf16[704,256]{1,0:T(8,128)(2,1)} %get-tuple-element.27), channel_id=1, source_target_pairs={{0,3},{1,0},{2,1},{3,2},{4,7},{5,4},{6,5},{7,6},{8,11},{9,8},{10,9... | collective-permute-start | bytes 1081352 | tf_op jit(solution)/shard_map/ppermute | solution.py:16
  57.9 2.4 %collective-permute-start.5 = (bf16[704,256]{1,0:T(8,128)(2,1)}, bf16[704,256]{1,0:T(8,128)(2,1)S(1)}, u32[]{:S(2)}, u32[]{:S(2)}) collective-permute-start(bf16[704,256]{1,0:T(8,128)(2,1)} %get-tuple-element.27), channel_id=1, source_target_pairs={{0,2},{1,3},{2,0},{3,1},{4,6},{5,7},{6,4},{7,5},{8,10},{9,11},{10,... | collective-permute-start | bytes 1081352 | tf_op jit(solution)/shard_map/ppermute | solution.py:16
  60.3 2.5 %collective-permute-start.4 = (bf16[704,256]{1,0:T(8,128)(2,1)}, bf16[704,256]{1,0:T(8,128)(2,1)S(1)}, u32[]{:S(2)}, u32[]{:S(2)}) collective-permute-start(bf16[704,256]{1,0:T(8,128)(2,1)} %get-tuple-element.27), channel_id=1, source_target_pairs={{0,1},{1,2},{2,3},{3,0},{4,5},{5,6},{6,7},{7,4},{8,9},{9,10},{10,1... | collective-permute-start | bytes 1081352 | tf_op jit(solution)/shard_map/ppermute | solution.py:16
  62.8 0.2 fusion.45
  63.1 0.2 fusion.44
  63.4 0.8 pad_maximum_fusion.3
  64.2 6.4 %all-to-all-start.1 = ((f32[128,4,128]{2,1,0:T(4,128)}), f32[128,4,128]{2,1,0:T(4,128)S(1)}, u32[]{:S(2)}, u32[]{:S(2)}) async-start(f32[128,4,128]{2,1,0:T(4,128)} %pad_maximum_fusion.3), calls=%async_computation.1 | async-start | bytes 524288 | tf_op jit(solution)/shard_map/all_to_all | solution.py:90
  70.6 2.6 %collective-permute-done.6 = bf16[704,256]{1,0:T(8,128)(2,1)S(1)} collective-permute-done((bf16[704,256]{1,0:T(8,128)(2,1)}, bf16[704,256]{1,0:T(8,128)(2,1)S(1)}, u32[]{:S(2)}, u32[]{:S(2)}) %collective-permute-start.6) | collective-permute-done | bytes 360480 | tf_op jit(solution)/shard_map/ppermute | solution.py:16
  73.1 6.4 %collective-permute-done.4 = bf16[704,256]{1,0:T(8,128)(2,1)S(1)} collective-permute-done((bf16[704,256]{1,0:T(8,128)(2,1)}, bf16[704,256]{1,0:T(8,128)(2,1)S(1)}, u32[]{:S(2)}, u32[]{:S(2)}) %collective-permute-start.4) | collective-permute-done | bytes 360480 | tf_op jit(solution)/shard_map/ppermute | solution.py:16
  79.5 0.7 copy-done.8
  80.3 1.6 %pad_maximum_fusion = bf16[4,704,256]{2,1,0:T(8,128)(2,1)S(1)} fusion(bf16[1,704,256]{2,1,0:T(8,128)(2,1)} %bitcast.33, bf16[1,704,256]{2,1,0:T(8,128)(2,1)} %bitcast.36, bf16[1,704,256]{2,1,0:T(8,128)(2,1)} %bitcast.39, bf16[1,704,256]{2,1,0:T(8,128)(2,1)} %get-tuple-element.26), kind=kLoop, calls=%fused_computation.2 | loop fusion | flops 2162688 | bytes 2883584 | tf_op jit(solution)/shard_map/stack | solution.py:83
  82.0 0.4 fusion.2
  82.4 3.4 %fusion.43 = f32[928,128]{1,0:T(8,128)S(1)} fusion(f32[448,928]{1,0:T(8,128)S(1)} %convert_reduce_fusion, f32[448,128]{1,0:T(8,128)S(1)} %fusion.2), kind=kOutput, calls=%fused_computation.71 | convolution fusion | flops 638582784 | bytes 2367488 | tf_op jit(solution)/shard_map/dot_general | solution.py:24
  85.8 0.8 copy-done.11
  86.7 0.1 reduce_sum.37
  86.8 0.9 pad_maximum_fusion.1
  87.8 6.9 %all-to-all-start.2 = ((f32[128,6,128]{2,1,0:T(8,128)}), f32[128,6,128]{2,1,0:T(8,128)}, u32[]{:S(2)}, u32[]{:S(2)}) async-start(f32[128,6,128]{2,1,0:T(8,128)} %pad_maximum_fusion.1), calls=%async_computation.2 | async-start | bytes 1048576 | tf_op jit(solution)/shard_map/all_to_all | solution.py:117
  94.7 0.8 fusion.39
  95.5 7.4 %collective-permute-start.10 = (f32[56,128]{1,0:T(8,128)S(1)}, f32[56,128]{1,0:T(8,128)S(1)}, u32[]{:S(2)}, u32[]{:S(2)}) collective-permute-start(f32[56,128]{1,0:T(8,128)S(1)} %get-tuple-element.21), channel_id=1, source_target_pairs={{0,504},{4,508},{8,0},{12,4},{16,8},{20,12},{24,16},{28,20},{32,24... | collective-permute-start | bytes 86024 | tf_op jit(solution)/shard_map/ppermute | solution.py:16
  102.9 2.6 %collective-permute-start.9 = (f32[56,128]{1,0:T(8,128)S(1)}, f32[56,128]{1,0:T(8,128)S(1)}, u32[]{:S(2)}, u32[]{:S(2)}) collective-permute-start(f32[56,128]{1,0:T(8,128)S(1)} %get-tuple-element.22), channel_id=1, source_target_pairs={{0,508},{4,0},{8,4},{12,8},{16,12},{20,16},{24,20},{28,24},{32,28}... | collective-permute-start | bytes 86024 | tf_op jit(solution)/shard_map/ppermute | solution.py:16
  105.5 3.0 %collective-permute-start.8 = (f32[56,128]{1,0:T(8,128)S(1)}, f32[56,128]{1,0:T(8,128)S(1)}, u32[]{:S(2)}, u32[]{:S(2)}) collective-permute-start(f32[56,128]{1,0:T(8,128)S(1)} %get-tuple-element.23), channel_id=1, source_target_pairs={{0,4},{4,8},{8,12},{12,16},{16,20},{20,24},{24,28},{28,32},{32,36}... | collective-permute-start | bytes 86024 | tf_op jit(solution)/shard_map/ppermute | solution.py:16
  108.5 1.9 %collective-permute-start.7 = (f32[56,128]{1,0:T(8,128)S(1)}, f32[56,128]{1,0:T(8,128)S(1)}, u32[]{:S(2)}, u32[]{:S(2)}) collective-permute-start(f32[56,128]{1,0:T(8,128)S(1)} %get-tuple-element.20), channel_id=1, source_target_pairs={{0,8},{4,12},{8,16},{12,20},{16,24},{20,28},{24,32},{28,36},{32,40... | collective-permute-start | bytes 86024 | tf_op jit(solution)/shard_map/ppermute | solution.py:16
  110.5 1.3 %fusion.3 = f32[448,128]{1,0:T(8,128)S(1)} fusion(bf16[4,704,256]{2,1,0:T(8,128)(2,1)S(1)} %pad_maximum_fusion, bf16[1,704,256]{2,1,0:T(8,128)(2,1)S(1)} %bitcast.35, bf16[1,704,256]{2,1,0:T(8,128)(2,1)S(1)} %bitcast.38, bf16[1,704,256]{2,1,0:T(8,128)(2,1)S(1)} %bitcast.41, bf16[1,704,256]{2,1,0:T(8,128)(2,1)S(1)} %copy-done.1, f32[928,128]{1,0:T(8,128)} %copy-done.11), kind=kOutput, calls=%fused_computation.11 | convolution fusion | flops 118546432 | bytes 2818048 | tf_op jit(solution)/shard_map/dot_general | solution.py:96
  111.9 3.3 %all-to-all-done.2 = f32[128,6,128]{2,1,0:T(8,128)} async-done(((f32[128,6,128]{2,1,0:T(8,128)}), f32[128,6,128]{2,1,0:T(8,128)}, u32[]{:S(2)}, u32[]{:S(2)}) %all-to-all-start.2) | async-done | bytes 393248 | tf_op jit(solution)/shard_map/all_to_all | solution.py:117
  115.2 1.2 copy.27
  116.6 0.4 fusion.31
  117.1 0.8 multiply_reduce_fusion
  117.9 0.2 add_convert_fusion
  118.1 0.7 copy.30
  118.9 0.7 squeeze.6
  119.7 0.7 squeeze.7
  (64 shorter events, 1.0 us)
Async XLA Ops:
  0.6 34.9 %copy-start.15 = (s32[448,15]{0,1:T(8,128)S(1)}, s32[448,15]{0,1:T(8,128)}, u32[]{:S(2)}) copy-start(s32[448,15]{0,1:T(8,128)} %param.17) | copy-start | bytes 80644
  3.4 36.0 %collective-permute-start = (bf16[64,128]{1,0:T(8,128)(2,1)S(1)}, bf16[64,128]{1,0:T(8,128)(2,1)S(1)}, u32[]{:S(2)}, u32[]{:S(2)}) collective-permute-start(bf16[64,128]{1,0:T(8,128)(2,1)S(1)} %slice_select_fusion), channel_id=1, source_target_pairs={{0,504},{4,508},{8,0},{12,4},{16,8},{20,12},{24,16},{28,20},{32,24... | collective-permute-start | bytes 49160 | tf_op jit(solution)/shard_map/ppermute | solution.py:16
  17.8 21.4 %copy-start.13 = (bf16[128,256]{1,0:T(8,128)(2,1)S(1)}, bf16[128,256]{1,0:T(8,128)(2,1)}, u32[]{:S(2)}) copy-start(bf16[128,256]{1,0:T(8,128)(2,1)} %param.11) | copy-start | bytes 196612
  17.8 21.6 %collective-permute-start.1 = (bf16[64,128]{1,0:T(8,128)(2,1)S(1)}, bf16[64,128]{1,0:T(8,128)(2,1)S(1)}, u32[]{:S(2)}, u32[]{:S(2)}) collective-permute-start(bf16[64,128]{1,0:T(8,128)(2,1)S(1)} %pad.18), channel_id=1, source_target_pairs={{0,508},{4,0},{8,4},{12,8},{16,12},{20,16},{24,20},{28,24},{32,28}... | collective-permute-start | bytes 49160 | tf_op jit(solution)/shard_map/ppermute | solution.py:16
  20.7 18.8 %collective-permute-start.2 = (bf16[64,128]{1,0:T(8,128)(2,1)S(1)}, bf16[64,128]{1,0:T(8,128)(2,1)S(1)}, u32[]{:S(2)}, u32[]{:S(2)}) collective-permute-start(bf16[64,128]{1,0:T(8,128)(2,1)S(1)} %pad.19), channel_id=1, source_target_pairs={{0,4},{4,8},{8,12},{12,16},{16,20},{20,24},{24,28},{28,32},{32,36}... | collective-permute-start | bytes 49160 | tf_op jit(solution)/shard_map/ppermute | solution.py:16
  23.4 16.1 %collective-permute-start.3 = (bf16[64,128]{1,0:T(8,128)(2,1)S(1)}, bf16[64,128]{1,0:T(8,128)(2,1)S(1)}, u32[]{:S(2)}, u32[]{:S(2)}) collective-permute-start(bf16[64,128]{1,0:T(8,128)(2,1)S(1)} %pad.20), channel_id=1, source_target_pairs={{0,8},{4,12},{8,16},{12,20},{16,24},{20,28},{24,32},{28,36},{32,40... | collective-permute-start | bytes 49160 | tf_op jit(solution)/shard_map/ppermute | solution.py:16
  27.0 23.8 %all-to-all-start = ((bf16[128,8,128]{2,1,0:T(8,128)(2,1)}), bf16[128,8,128]{2,1,0:T(8,128)(2,1)S(1)}, u32[]{:S(2)}, u32[]{:S(2)}) async-start(bf16[128,8,128]{2,1,0:T(8,128)(2,1)} %broadcast_in_dim.4), calls=%async_computation | async-start | bytes 524288 | tf_op jit(solution)/shard_map/all_to_all | solution.py:32
  39.4 11.8 %copy-start.14 = (bf16[128,256]{1,0:T(8,128)(2,1)S(1)}, bf16[128,256]{1,0:T(8,128)(2,1)}, u32[]{:S(2)}) copy-start(bf16[128,256]{1,0:T(8,128)(2,1)} %param.12) | copy-start | bytes 196612
  39.4 11.8 %copy-start.17 = (f32[256]{0:T(256)S(1)}, f32[256]{0:T(256)}, u32[]{:S(2)}) copy-start(f32[256]{0:T(256)} %param.13) | copy-start | bytes 3076
  53.5 19.7 %collective-permute-start.6 = (bf16[704,256]{1,0:T(8,128)(2,1)}, bf16[704,256]{1,0:T(8,128)(2,1)S(1)}, u32[]{:S(2)}, u32[]{:S(2)}) collective-permute-start(bf16[704,256]{1,0:T(8,128)(2,1)} %get-tuple-element.27), channel_id=1, source_target_pairs={{0,3},{1,0},{2,1},{3,2},{4,7},{5,4},{6,5},{7,6},{8,11},{9,8},{10,9... | collective-permute-start | bytes 1081352 | tf_op jit(solution)/shard_map/ppermute | solution.py:16
  57.9 15.3 %collective-permute-start.5 = (bf16[704,256]{1,0:T(8,128)(2,1)}, bf16[704,256]{1,0:T(8,128)(2,1)S(1)}, u32[]{:S(2)}, u32[]{:S(2)}) collective-permute-start(bf16[704,256]{1,0:T(8,128)(2,1)} %get-tuple-element.27), channel_id=1, source_target_pairs={{0,2},{1,3},{2,0},{3,1},{4,6},{5,7},{6,4},{7,5},{8,10},{9,11},{10,... | collective-permute-start | bytes 1081352 | tf_op jit(solution)/shard_map/ppermute | solution.py:16
  60.3 19.2 %collective-permute-start.4 = (bf16[704,256]{1,0:T(8,128)(2,1)}, bf16[704,256]{1,0:T(8,128)(2,1)S(1)}, u32[]{:S(2)}, u32[]{:S(2)}) collective-permute-start(bf16[704,256]{1,0:T(8,128)(2,1)} %get-tuple-element.27), channel_id=1, source_target_pairs={{0,1},{1,2},{2,3},{3,0},{4,5},{5,6},{6,7},{7,4},{8,9},{9,10},{10,1... | collective-permute-start | bytes 1081352 | tf_op jit(solution)/shard_map/ppermute | solution.py:16
  64.2 22.5 %all-to-all-start.1 = ((f32[128,4,128]{2,1,0:T(4,128)}), f32[128,4,128]{2,1,0:T(4,128)S(1)}, u32[]{:S(2)}, u32[]{:S(2)}) async-start(f32[128,4,128]{2,1,0:T(4,128)} %pad_maximum_fusion.3), calls=%async_computation.1 | async-start | bytes 524288 | tf_op jit(solution)/shard_map/all_to_all | solution.py:90
  73.1 6.4 %copy-start.2 = (bf16[704,256]{1,0:T(8,128)(2,1)}, bf16[704,256]{1,0:T(8,128)(2,1)S(1)}, u32[]{:S(2)}) copy-start(bf16[704,256]{1,0:T(8,128)(2,1)S(1)} %collective-permute-done.6) | copy-start | bytes 1081348
  73.1 6.4 %copy-start.5 = (bf16[704,256]{1,0:T(8,128)(2,1)}, bf16[704,256]{1,0:T(8,128)(2,1)S(1)}, u32[]{:S(2)}) copy-start(bf16[704,256]{1,0:T(8,128)(2,1)S(1)} %collective-permute-done.5) | copy-start | bytes 1081348
  79.5 0.8 copy-start.8
  80.3 1.6 %copy-start = (bf16[1,704,256]{2,1,0:T(8,128)(2,1)S(1)}, bf16[1,704,256]{2,1,0:T(8,128)(2,1)}, u32[]{:S(2)}) copy-start(bf16[1,704,256]{2,1,0:T(8,128)(2,1)} %get-tuple-element.26) | copy-start | bytes 1081348
  80.3 1.6 %copy-start.3 = (bf16[704,256]{1,0:T(8,128)(2,1)S(1)}, bf16[704,256]{1,0:T(8,128)(2,1)}, u32[]{:S(2)}) copy-start(bf16[704,256]{1,0:T(8,128)(2,1)} %copy-done.2) | copy-start | bytes 1081348
  80.3 1.6 %copy-start.6 = (bf16[704,256]{1,0:T(8,128)(2,1)S(1)}, bf16[704,256]{1,0:T(8,128)(2,1)}, u32[]{:S(2)}) copy-start(bf16[704,256]{1,0:T(8,128)(2,1)} %copy-done.5) | copy-start | bytes 1081348
  80.3 1.7 %copy-start.9 = (bf16[704,256]{1,0:T(8,128)(2,1)S(1)}, bf16[704,256]{1,0:T(8,128)(2,1)}, u32[]{:S(2)}) copy-start(bf16[704,256]{1,0:T(8,128)(2,1)} %copy-done.8) | copy-start | bytes 1081348
  85.8 0.8 copy-start.11
  86.6 23.8 %copy-start.1 = (bf16[1,704,256]{2,1,0:T(8,128)(2,1)S(1)}, bf16[1,704,256]{2,1,0:T(8,128)(2,1)}, u32[]{:S(2)}) copy-start(bf16[1,704,256]{2,1,0:T(8,128)(2,1)} %get-tuple-element.26) | copy-start | bytes 1081348
  86.6 23.8 %copy-start.4 = (bf16[704,256]{1,0:T(8,128)(2,1)S(1)}, bf16[704,256]{1,0:T(8,128)(2,1)}, u32[]{:S(2)}) copy-start(bf16[704,256]{1,0:T(8,128)(2,1)} %copy-done.2) | copy-start | bytes 1081348
  86.6 23.8 %copy-start.7 = (bf16[704,256]{1,0:T(8,128)(2,1)S(1)}, bf16[704,256]{1,0:T(8,128)(2,1)}, u32[]{:S(2)}) copy-start(bf16[704,256]{1,0:T(8,128)(2,1)} %copy-done.5) | copy-start | bytes 1081348
  86.6 23.9 %copy-start.10 = (bf16[704,256]{1,0:T(8,128)(2,1)S(1)}, bf16[704,256]{1,0:T(8,128)(2,1)}, u32[]{:S(2)}) copy-start(bf16[704,256]{1,0:T(8,128)(2,1)} %copy-done.8) | copy-start | bytes 1081348
  87.8 27.4 %all-to-all-start.2 = ((f32[128,6,128]{2,1,0:T(8,128)}), f32[128,6,128]{2,1,0:T(8,128)}, u32[]{:S(2)}, u32[]{:S(2)}) async-start(f32[128,6,128]{2,1,0:T(8,128)} %pad_maximum_fusion.1), calls=%async_computation.2 | async-start | bytes 1048576 | tf_op jit(solution)/shard_map/all_to_all | solution.py:117
  95.5 21.6 %collective-permute-start.10 = (f32[56,128]{1,0:T(8,128)S(1)}, f32[56,128]{1,0:T(8,128)S(1)}, u32[]{:S(2)}, u32[]{:S(2)}) collective-permute-start(f32[56,128]{1,0:T(8,128)S(1)} %get-tuple-element.21), channel_id=1, source_target_pairs={{0,504},{4,508},{8,0},{12,4},{16,8},{20,12},{24,16},{28,20},{32,24... | collective-permute-start | bytes 86024 | tf_op jit(solution)/shard_map/ppermute | solution.py:16
  102.9 14.1 %collective-permute-start.9 = (f32[56,128]{1,0:T(8,128)S(1)}, f32[56,128]{1,0:T(8,128)S(1)}, u32[]{:S(2)}, u32[]{:S(2)}) collective-permute-start(f32[56,128]{1,0:T(8,128)S(1)} %get-tuple-element.22), channel_id=1, source_target_pairs={{0,508},{4,0},{8,4},{12,8},{16,12},{20,16},{24,20},{28,24},{32,28}... | collective-permute-start | bytes 86024 | tf_op jit(solution)/shard_map/ppermute | solution.py:16
  105.5 11.6 %collective-permute-start.8 = (f32[56,128]{1,0:T(8,128)S(1)}, f32[56,128]{1,0:T(8,128)S(1)}, u32[]{:S(2)}, u32[]{:S(2)}) collective-permute-start(f32[56,128]{1,0:T(8,128)S(1)} %get-tuple-element.23), channel_id=1, source_target_pairs={{0,4},{4,8},{8,12},{12,16},{16,20},{20,24},{24,28},{28,32},{32,36}... | collective-permute-start | bytes 86024 | tf_op jit(solution)/shard_map/ppermute | solution.py:16
  108.5 8.6 %collective-permute-start.7 = (f32[56,128]{1,0:T(8,128)S(1)}, f32[56,128]{1,0:T(8,128)S(1)}, u32[]{:S(2)}, u32[]{:S(2)}) collective-permute-start(f32[56,128]{1,0:T(8,128)S(1)} %get-tuple-element.20), channel_id=1, source_target_pairs={{0,8},{4,12},{8,16},{12,20},{16,24},{20,28},{24,32},{28,36},{32,40... | collective-permute-start | bytes 86024 | tf_op jit(solution)/shard_map/ppermute | solution.py:16
  111.8 4.8 %copy-start.16 = (s32[1,2]{1,0:T(1,128)S(1)}, s32[1,2]{1,0:T(1,128)}, u32[]{:S(2)}) copy-start(s32[1,2]{1,0:T(1,128)} %param.15) | copy-start | bytes 28
  111.8 6.0 %copy-start.12 = (bf16[448,128]{1,0:T(8,128)(2,1)S(1)}, bf16[448,128]{1,0:T(8,128)(2,1)}, u32[]{:S(2)}) copy-start(bf16[448,128]{1,0:T(8,128)(2,1)} %param.10) | copy-start | bytes 344068

commit v7 on v4

--- a/solution.py
+++ b/solution.py
@@ -53,15 +53,19 @@
     halo_out = jnp.dot(pick.astype(BF16), perturbed, preferred_element_type=F32).astype(BF16)
     hub_out = jnp.dot(hub_pick.astype(BF16), perturbed, preferred_element_type=F32).astype(BF16)
 
+    t_iota = lax.broadcasted_iota(jnp.int32, (rows_here, K, table_rows), 2)
+    counts = jnp.sum((neighbors[:, :, None] == t_iota).astype(F32), axis=1)
+    halo_out, counts = lax.optimization_barrier((halo_out, counts))
+
     pieces = [
         from_behind(halo_out[o * slots : (o + 1) * slots], "dom", offset_of(o))
         for o in range(NOFF)
     ]
-    hubs = gather_all(hub_out, "dom").reshape(dom_count * hub_dev, feat_in)
+    pad_rows = 8 - hub_dev % 8 if hub_dev % 8 else 0
+    hub_tile = jnp.pad(hub_out, ((0, pad_rows), (0, 0)))
+    hubs = gather_all(hub_tile, "dom")[:, :hub_dev].reshape(dom_count * hub_dev, feat_in)
     table = jnp.concatenate([perturbed] + pieces + [hubs], 0)
 
-    t_iota = lax.broadcasted_iota(jnp.int32, (rows_here, K, table_rows), 2)
-    counts = jnp.sum((neighbors[:, :, None] == t_iota).astype(F32), axis=1)
     gathered_sum = jnp.dot(counts.astype(BF16), table, preferred_element_type=F32)
     neighbor_mean = (gathered_sum / K).astype(BF16)
 

time: 118 us -> 124 us (1.051)
  waiting for transfers between devices: 17.5 us -> 27.2 us
  starting transfers between devices: 70.1 us -> 67.9 us
    all_to_all x1, waiting for transfers between devices: 6.07 us -> 14.9 us  [gather_all(): out = lax.all_to_all(rep, axis, 0, 0, tiled=True)]
    ppermute x11, waiting for transfers between devices: 6.74 us -> 8.97 us  [from_behind(): return lax.ppermute(x, axis, [(i, (i + by) % size) for i in range(size)])]
    all_to_all x1, starting transfers between devices: 8.57 us -> 6.37 us  [per_device(): lax.all_to_all(weight_flat.reshape(dom_count, -1, 128), 'dom', 0, 0, tile...]
    all_to_all x1, waiting for transfers between devices: 1.37 us -> 0.01 us  [per_device(): lax.all_to_all(weight_flat.reshape(dom_count, -1, 128), 'dom', 0, 0, tile...]
  transfers between devices with their start and end apart: 14 -> 14, of which waited for: 4 -> 4; matrix products, arithmetic and copies ran while one was open for 15% -> 10% of each run, Pallas kernels for 0% -> 0%
where the time goes in v7:
time: 124 us; the launch traced here: 123 us
  starting transfers between devices  67.9 us (55%)
  waiting for transfers between devices  27.2 us (22%)
  other arithmetic  9.73 us (8%)
  matrix products  9.12 us (7%)
  local copies, waits for them, and re-layouts  7.94 us (6%)
    ppermute x11, starting transfers between devices, from_behind(): return lax.ppermute(x, axis, [(i, (i + by) % size) for i in range(size)])  46.1 us
    all_to_all x1, waiting for transfers between devices, gather_all(): out = lax.all_to_all(rep, axis, 0, 0, tiled=True)  14.9 us
    ppermute x11, waiting for transfers between devices, from_behind(): return lax.ppermute(x, axis, [(i, (i + by) % size) for i in range(size)])  8.97 us
    all_to_all x1, starting transfers between devices, gather_all(): out = lax.all_to_all(rep, axis, 0, 0, tiled=True)  8.57 us
    all_to_all x1, starting transfers between devices, per_device(): recv = lax.all_to_all(sent, 'dom', 0, 0, tiled=True).reshape(dom_count, -1)  6.88 us
    all_to_all x1, starting transfers between devices, per_device(): lax.all_to_all(weight_flat.reshape(dom_count, -1, 128), 'dom', 0, 0, tile...  6.37 us
    dot_general x5, matrix products, contract_rows(): lax.dot_general(left, right, (((0,), (0,)), ((), ())), preferred_element_...  5.05 us
    reduce_sum x1, other arithmetic, per_device(): counts = jnp.sum((neighbors[:, :, None] == t_iota).astype(F32), axis=1)  5.01 us
  transfers between devices with their start and end apart: 14, of which 4 were waited for; matrix products, arithmetic and copies ran while one was open for 10% of the time, Pallas kernels for 0%

profile of v7, /device:TPU:1, one launch (start us, length us, event | category | flops | bytes accessed | tf_op | source)
XLA Modules:
  0.0 123.1 jit_solution(770398008959498689)
XLA Ops:
  0.7 0.8 eq.28
  1.5 5.0 %convert_reduce_fusion = f32[448,928]{1,0:T(8,128)S(1)} fusion(s32[448,15]{0,1:T(8,128)} %param.17), kind=kLoop, calls=%fused_computation | loop fusion | flops 18292736 | bytes 1689856 | tf_op jit(solution)/shard_map/reduce_sum | solution.py:57
  6.5 0.3 convolution_convert_fusion
  6.8 14.4 %collective-permute-start = (bf16[56,128]{1,0:T(8,128)(2,1)S(1)}, bf16[56,128]{1,0:T(8,128)(2,1)S(1)}, u32[]{:S(2)}, u32[]{:S(2)}) collective-permute-start(bf16[56,128]{1,0:T(8,128)(2,1)S(1)} %get-tuple-element.35), channel_id=1, source_target_pairs={{0,504},{4,508},{8,0},{12,4},{16,8},{20,12},{24,16},{28,20},{32,24... | collective-permute-start | bytes 43016 | tf_op jit(solution)/shard_map/ppermute | solution.py:16
  21.2 2.9 %collective-permute-start.1 = (bf16[56,128]{1,0:T(8,128)(2,1)S(1)}, bf16[56,128]{1,0:T(8,128)(2,1)S(1)}, u32[]{:S(2)}, u32[]{:S(2)}) collective-permute-start(bf16[56,128]{1,0:T(8,128)(2,1)S(1)} %get-tuple-element.34), channel_id=1, source_target_pairs={{0,508},{4,0},{8,4},{12,8},{16,12},{20,16},{24,20},{28,24},{32,28}... | collective-permute-start | bytes 43016 | tf_op jit(solution)/shard_map/ppermute | solution.py:16
  24.1 2.7 %collective-permute-start.2 = (bf16[56,128]{1,0:T(8,128)(2,1)S(1)}, bf16[56,128]{1,0:T(8,128)(2,1)S(1)}, u32[]{:S(2)}, u32[]{:S(2)}) collective-permute-start(bf16[56,128]{1,0:T(8,128)(2,1)S(1)} %get-tuple-element.33), channel_id=1, source_target_pairs={{0,4},{4,8},{8,12},{12,16},{16,20},{20,24},{24,28},{28,32},{32,36}... | collective-permute-start | bytes 43016 | tf_op jit(solution)/shard_map/ppermute | solution.py:16
  26.8 1.9 %collective-permute-start.3 = (bf16[56,128]{1,0:T(8,128)(2,1)S(1)}, bf16[56,128]{1,0:T(8,128)(2,1)S(1)}, u32[]{:S(2)}, u32[]{:S(2)}) collective-permute-start(bf16[56,128]{1,0:T(8,128)(2,1)S(1)} %get-tuple-element.32), channel_id=1, source_target_pairs={{0,8},{4,12},{8,16},{12,20},{16,24},{20,28},{24,32},{28,36},{32,40... | collective-permute-start | bytes 43016 | tf_op jit(solution)/shard_map/ppermute | solution.py:16
  28.7 0.2 convolution_convert_fusion.1
  28.9 0.7 broadcast_in_dim.4
  29.7 8.6 %all-to-all-start = ((bf16[128,8,128]{2,1,0:T(8,128)(2,1)}), bf16[128,8,128]{2,1,0:T(8,128)(2,1)S(1)}, u32[]{:S(2)}, u32[]{:S(2)}) async-start(bf16[128,8,128]{2,1,0:T(8,128)(2,1)} %broadcast_in_dim.4), calls=%async_computation | async-start | bytes 524288 | tf_op jit(solution)/shard_map/all_to_all | solution.py:32
  38.3 0.2 fusion.42
  38.6 14.9 %all-to-all-done = bf16[128,8,128]{2,1,0:T(8,128)(2,1)S(1)} async-done(((bf16[128,8,128]{2,1,0:T(8,128)(2,1)}), bf16[128,8,128]{2,1,0:T(8,128)(2,1)S(1)}, u32[]{:S(2)}, u32[]{:S(2)}) %all-to-all-start) | async-done | bytes 262176 | tf_op jit(solution)/shard_map/all_to_all | solution.py:32
  53.6 0.4 fusion.4
  54.0 1.3 %multiply_convert_fusion = bf16[448,256]{1,0:T(8,128)(2,1)S(1)} fusion(f32[448,256]{1,0:T(8,128)S(1)} %fusion.42, bf16[448,128]{1,0:T(8,128)(2,1)S(1)} %fusion.4, bf16[128,256]{1,0:T(8,128)(2,1)S(1)} %copy-done.16, bf16[448,256]{1,0:T(8,128)(2,1)} %param.14, f32[256]{0:T(256)S(1)} %copy-done.18), kind=kOutput, calls=%fused_computation.19 | convolution fusion | flops 30736384 | bytes 1098752 | tf_op jit(solution)/shard_map/dot_general | solution.py:73
  55.3 0.9 fusion.38
  56.2 4.4 %collective-permute-start.6 = (bf16[704,256]{1,0:T(8,128)(2,1)}, bf16[704,256]{1,0:T(8,128)(2,1)S(1)}, u32[]{:S(2)}, u32[]{:S(2)}) collective-permute-start(bf16[704,256]{1,0:T(8,128)(2,1)} %get-tuple-element.31), channel_id=1, source_target_pairs={{0,3},{1,0},{2,1},{3,2},{4,7},{5,4},{6,5},{7,6},{8,11},{9,8},{10,9... | collective-permute-start | bytes 1081352 | tf_op jit(solution)/shard_map/ppermute | solution.py:16
  60.6 2.4 %collective-permute-start.5 = (bf16[704,256]{1,0:T(8,128)(2,1)}, bf16[704,256]{1,0:T(8,128)(2,1)S(1)}, u32[]{:S(2)}, u32[]{:S(2)}) collective-permute-start(bf16[704,256]{1,0:T(8,128)(2,1)} %get-tuple-element.31), channel_id=1, source_target_pairs={{0,2},{1,3},{2,0},{3,1},{4,6},{5,7},{6,4},{7,5},{8,10},{9,11},{10,... | collective-permute-start | bytes 1081352 | tf_op jit(solution)/shard_map/ppermute | solution.py:16
  63.0 2.5 %collective-permute-start.4 = (bf16[704,256]{1,0:T(8,128)(2,1)}, bf16[704,256]{1,0:T(8,128)(2,1)S(1)}, u32[]{:S(2)}, u32[]{:S(2)}) collective-permute-start(bf16[704,256]{1,0:T(8,128)(2,1)} %get-tuple-element.31), channel_id=1, source_target_pairs={{0,1},{1,2},{2,3},{3,0},{4,5},{5,6},{6,7},{7,4},{8,9},{9,10},{10,1... | collective-permute-start | bytes 1081352 | tf_op jit(solution)/shard_map/ppermute | solution.py:16
  65.5 0.2 fusion.45
  65.9 0.2 fusion.44
  66.2 0.8 pad_maximum_fusion.3
  66.9 6.4 %all-to-all-start.1 = ((f32[128,4,128]{2,1,0:T(4,128)}), f32[128,4,128]{2,1,0:T(4,128)S(1)}, u32[]{:S(2)}, u32[]{:S(2)}) async-start(f32[128,4,128]{2,1,0:T(4,128)} %pad_maximum_fusion.3), calls=%async_computation.1 | async-start | bytes 524288 | tf_op jit(solution)/shard_map/all_to_all | solution.py:87
  73.3 2.6 %collective-permute-done.6 = bf16[704,256]{1,0:T(8,128)(2,1)S(1)} collective-permute-done((bf16[704,256]{1,0:T(8,128)(2,1)}, bf16[704,256]{1,0:T(8,128)(2,1)S(1)}, u32[]{:S(2)}, u32[]{:S(2)}) %collective-permute-start.6) | collective-permute-done | bytes 360480 | tf_op jit(solution)/shard_map/ppermute | solution.py:16
  75.9 6.4 %collective-permute-done.4 = bf16[704,256]{1,0:T(8,128)(2,1)S(1)} collective-permute-done((bf16[704,256]{1,0:T(8,128)(2,1)}, bf16[704,256]{1,0:T(8,128)(2,1)S(1)}, u32[]{:S(2)}, u32[]{:S(2)}) %collective-permute-start.4) | collective-permute-done | bytes 360480 | tf_op jit(solution)/shard_map/ppermute | solution.py:16
  82.3 0.7 copy-done.8
  83.0 1.6 %pad_maximum_fusion = bf16[4,704,256]{2,1,0:T(8,128)(2,1)S(1)} fusion(bf16[1,704,256]{2,1,0:T(8,128)(2,1)} %bitcast.33, bf16[1,704,256]{2,1,0:T(8,128)(2,1)} %bitcast.36, bf16[1,704,256]{2,1,0:T(8,128)(2,1)} %bitcast.39, bf16[1,704,256]{2,1,0:T(8,128)(2,1)} %get-tuple-element.30), kind=kLoop, calls=%fused_computation.2 | loop fusion | flops 2162688 | bytes 2883584 | tf_op jit(solution)/shard_map/stack | solution.py:80
  84.7 0.4 fusion.2
  85.1 3.4 %fusion.43 = f32[928,128]{1,0:T(8,128)S(1)} fusion(f32[448,928]{1,0:T(8,128)S(1)} %convert_reduce_fusion, f32[448,128]{1,0:T(8,128)S(1)} %fusion.2), kind=kOutput, calls=%fused_computation.70 | convolution fusion | flops 638582784 | bytes 2367488 | tf_op jit(solution)/shard_map/dot_general | solution.py:24
  88.5 0.8 copy-done.11
  89.4 0.1 reduce_sum.37
  89.6 0.9 pad_maximum_fusion.1
  90.5 6.9 %all-to-all-start.2 = ((f32[128,6,128]{2,1,0:T(8,128)}), f32[128,6,128]{2,1,0:T(8,128)}, u32[]{:S(2)}, u32[]{:S(2)}) async-start(f32[128,6,128]{2,1,0:T(8,128)} %pad_maximum_fusion.1), calls=%async_computation.2 | async-start | bytes 1048576 | tf_op jit(solution)/shard_map/all_to_all | solution.py:114
  97.4 0.8 fusion.39
  98.2 7.4 %collective-permute-start.10 = (f32[56,128]{1,0:T(8,128)S(1)}, f32[56,128]{1,0:T(8,128)S(1)}, u32[]{:S(2)}, u32[]{:S(2)}) collective-permute-start(f32[56,128]{1,0:T(8,128)S(1)} %get-tuple-element.25), channel_id=1, source_target_pairs={{0,504},{4,508},{8,0},{12,4},{16,8},{20,12},{24,16},{28,20},{32,24... | collective-permute-start | bytes 86024 | tf_op jit(solution)/shard_map/ppermute | solution.py:16
  105.6 2.6 %collective-permute-start.9 = (f32[56,128]{1,0:T(8,128)S(1)}, f32[56,128]{1,0:T(8,128)S(1)}, u32[]{:S(2)}, u32[]{:S(2)}) collective-permute-start(f32[56,128]{1,0:T(8,128)S(1)} %get-tuple-element.26), channel_id=1, source_target_pairs={{0,508},{4,0},{8,4},{12,8},{16,12},{20,16},{24,20},{28,24},{32,28}... | collective-permute-start | bytes 86024 | tf_op jit(solution)/shard_map/ppermute | solution.py:16
  108.2 3.0 %collective-permute-start.8 = (f32[56,128]{1,0:T(8,128)S(1)}, f32[56,128]{1,0:T(8,128)S(1)}, u32[]{:S(2)}, u32[]{:S(2)}) collective-permute-start(f32[56,128]{1,0:T(8,128)S(1)} %get-tuple-element.27), channel_id=1, source_target_pairs={{0,4},{4,8},{8,12},{12,16},{16,20},{20,24},{24,28},{28,32},{32,36}... | collective-permute-start | bytes 86024 | tf_op jit(solution)/shard_map/ppermute | solution.py:16
  111.2 1.9 %collective-permute-start.7 = (f32[56,128]{1,0:T(8,128)S(1)}, f32[56,128]{1,0:T(8,128)S(1)}, u32[]{:S(2)}, u32[]{:S(2)}) collective-permute-start(f32[56,128]{1,0:T(8,128)S(1)} %get-tuple-element.24), channel_id=1, source_target_pairs={{0,8},{4,12},{8,16},{12,20},{16,24},{20,28},{24,32},{28,36},{32,40... | collective-permute-start | bytes 86024 | tf_op jit(solution)/shard_map/ppermute | solution.py:16
  113.2 1.3 %fusion.3 = f32[448,128]{1,0:T(8,128)S(1)} fusion(bf16[4,704,256]{2,1,0:T(8,128)(2,1)S(1)} %pad_maximum_fusion, bf16[1,704,256]{2,1,0:T(8,128)(2,1)S(1)} %bitcast.35, bf16[1,704,256]{2,1,0:T(8,128)(2,1)S(1)} %bitcast.38, bf16[1,704,256]{2,1,0:T(8,128)(2,1)S(1)} %bitcast.41, bf16[1,704,256]{2,1,0:T(8,128)(2,1)S(1)} %copy-done.1, f32[928,128]{1,0:T(8,128)} %copy-done.11), kind=kOutput, calls=%fused_computation.11 | convolution fusion | flops 118546432 | bytes 2818048 | tf_op jit(solution)/shard_map/dot_general | solution.py:93
  114.5 3.3 %all-to-all-done.2 = f32[128,6,128]{2,1,0:T(8,128)} async-done(((f32[128,6,128]{2,1,0:T(8,128)}), f32[128,6,128]{2,1,0:T(8,128)}, u32[]{:S(2)}, u32[]{:S(2)}) %all-to-all-start.2) | async-done | bytes 393248 | tf_op jit(solution)/shard_map/all_to_all | solution.py:114
  117.8 1.2 copy.27
  119.0 0.1 slice_reduce_fusion
  119.2 0.1 fusion.40
  119.3 0.4 fusion.31
  119.8 0.8 multiply_reduce_fusion
  120.6 0.2 add_convert_fusion
  120.8 0.7 copy.30
  121.6 0.7 squeeze.6
  122.4 0.7 squeeze.7
  (62 shorter events, 0.7 us)
Async XLA Ops:
  0.6 5.9 %copy-start.12 = (bf16[448,128]{1,0:T(8,128)(2,1)S(1)}, bf16[448,128]{1,0:T(8,128)(2,1)}, u32[]{:S(2)}) copy-start(bf16[448,128]{1,0:T(8,128)(2,1)} %param.10) | copy-start | bytes 344068
  0.6 5.9 %copy-start.15 = (bf16[448,128]{1,0:T(8,128)(2,1)S(1)}, bf16[448,128]{1,0:T(8,128)(2,1)}, u32[]{:S(2)}) copy-start(bf16[448,128]{1,0:T(8,128)(2,1)} %param.9) | copy-start | bytes 344068
  0.7 28.1 %copy-start.17 = (s32[1,2]{1,0:T(1,128)S(1)}, s32[1,2]{1,0:T(1,128)}, u32[]{:S(2)}) copy-start(s32[1,2]{1,0:T(1,128)} %param.15) | copy-start | bytes 28
  1.5 36.8 %copy-start.14 = (bf16[128,256]{1,0:T(8,128)(2,1)S(1)}, bf16[128,256]{1,0:T(8,128)(2,1)}, u32[]{:S(2)}) copy-start(bf16[128,256]{1,0:T(8,128)(2,1)} %param.11) | copy-start | bytes 196612
  6.8 31.7 %collective-permute-start = (bf16[56,128]{1,0:T(8,128)(2,1)S(1)}, bf16[56,128]{1,0:T(8,128)(2,1)S(1)}, u32[]{:S(2)}, u32[]{:S(2)}) collective-permute-start(bf16[56,128]{1,0:T(8,128)(2,1)S(1)} %get-tuple-element.35), channel_id=1, source_target_pairs={{0,504},{4,508},{8,0},{12,4},{16,8},{20,12},{24,16},{28,20},{32,24... | collective-permute-start | bytes 43016 | tf_op jit(solution)/shard_map/ppermute | solution.py:16
  21.2 17.3 %collective-permute-start.1 = (bf16[56,128]{1,0:T(8,128)(2,1)S(1)}, bf16[56,128]{1,0:T(8,128)(2,1)S(1)}, u32[]{:S(2)}, u32[]{:S(2)}) collective-permute-start(bf16[56,128]{1,0:T(8,128)(2,1)S(1)} %get-tuple-element.34), channel_id=1, source_target_pairs={{0,508},{4,0},{8,4},{12,8},{16,12},{20,16},{24,20},{28,24},{32,28}... | collective-permute-start | bytes 43016 | tf_op jit(solution)/shard_map/ppermute | solution.py:16
  24.1 14.4 %collective-permute-start.2 = (bf16[56,128]{1,0:T(8,128)(2,1)S(1)}, bf16[56,128]{1,0:T(8,128)(2,1)S(1)}, u32[]{:S(2)}, u32[]{:S(2)}) collective-permute-start(bf16[56,128]{1,0:T(8,128)(2,1)S(1)} %get-tuple-element.33), channel_id=1, source_target_pairs={{0,4},{4,8},{8,12},{12,16},{16,20},{20,24},{24,28},{28,32},{32,36}... | collective-permute-start | bytes 43016 | tf_op jit(solution)/shard_map/ppermute | solution.py:16
  26.8 11.8 %collective-permute-start.3 = (bf16[56,128]{1,0:T(8,128)(2,1)S(1)}, bf16[56,128]{1,0:T(8,128)(2,1)S(1)}, u32[]{:S(2)}, u32[]{:S(2)}) collective-permute-start(bf16[56,128]{1,0:T(8,128)(2,1)S(1)} %get-tuple-element.32), channel_id=1, source_target_pairs={{0,8},{4,12},{8,16},{12,20},{16,24},{20,28},{24,32},{28,36},{32,40... | collective-permute-start | bytes 43016 | tf_op jit(solution)/shard_map/ppermute | solution.py:16
  29.7 23.8 %all-to-all-start = ((bf16[128,8,128]{2,1,0:T(8,128)(2,1)}), bf16[128,8,128]{2,1,0:T(8,128)(2,1)S(1)}, u32[]{:S(2)}, u32[]{:S(2)}) async-start(bf16[128,8,128]{2,1,0:T(8,128)(2,1)} %broadcast_in_dim.4), calls=%async_computation | async-start | bytes 524288 | tf_op jit(solution)/shard_map/all_to_all | solution.py:32
  38.5 15.5 %copy-start.16 = (bf16[128,256]{1,0:T(8,128)(2,1)S(1)}, bf16[128,256]{1,0:T(8,128)(2,1)}, u32[]{:S(2)}) copy-start(bf16[128,256]{1,0:T(8,128)(2,1)} %param.12) | copy-start | bytes 196612
  38.5 15.5 %copy-start.18 = (f32[256]{0:T(256)S(1)}, f32[256]{0:T(256)}, u32[]{:S(2)}) copy-start(f32[256]{0:T(256)} %param.13) | copy-start | bytes 3076
  56.2 19.7 %collective-permute-start.6 = (bf16[704,256]{1,0:T(8,128)(2,1)}, bf16[704,256]{1,0:T(8,128)(2,1)S(1)}, u32[]{:S(2)}, u32[]{:S(2)}) collective-permute-start(bf16[704,256]{1,0:T(8,128)(2,1)} %get-tuple-element.31), channel_id=1, source_target_pairs={{0,3},{1,0},{2,1},{3,2},{4,7},{5,4},{6,5},{7,6},{8,11},{9,8},{10,9... | collective-permute-start | bytes 1081352 | tf_op jit(solution)/shard_map/ppermute | solution.py:16
  60.6 15.3 %collective-permute-start.5 = (bf16[704,256]{1,0:T(8,128)(2,1)}, bf16[704,256]{1,0:T(8,128)(2,1)S(1)}, u32[]{:S(2)}, u32[]{:S(2)}) collective-permute-start(bf16[704,256]{1,0:T(8,128)(2,1)} %get-tuple-element.31), channel_id=1, source_target_pairs={{0,2},{1,3},{2,0},{3,1},{4,6},{5,7},{6,4},{7,5},{8,10},{9,11},{10,... | collective-permute-start | bytes 1081352 | tf_op jit(solution)/shard_map/ppermute | solution.py:16
  63.0 19.2 %collective-permute-start.4 = (bf16[704,256]{1,0:T(8,128)(2,1)}, bf16[704,256]{1,0:T(8,128)(2,1)S(1)}, u32[]{:S(2)}, u32[]{:S(2)}) collective-permute-start(bf16[704,256]{1,0:T(8,128)(2,1)} %get-tuple-element.31), channel_id=1, source_target_pairs={{0,1},{1,2},{2,3},{3,0},{4,5},{5,6},{6,7},{7,4},{8,9},{9,10},{10,1... | collective-permute-start | bytes 1081352 | tf_op jit(solution)/shard_map/ppermute | solution.py:16
  66.9 22.4 %all-to-all-start.1 = ((f32[128,4,128]{2,1,0:T(4,128)}), f32[128,4,128]{2,1,0:T(4,128)S(1)}, u32[]{:S(2)}, u32[]{:S(2)}) async-start(f32[128,4,128]{2,1,0:T(4,128)} %pad_maximum_fusion.3), calls=%async_computation.1 | async-start | bytes 524288 | tf_op jit(solution)/shard_map/all_to_all | solution.py:87
  75.9 6.4 %copy-start.2 = (bf16[704,256]{1,0:T(8,128)(2,1)}, bf16[704,256]{1,0:T(8,128)(2,1)S(1)}, u32[]{:S(2)}) copy-start(bf16[704,256]{1,0:T(8,128)(2,1)S(1)} %collective-permute-done.6) | copy-start | bytes 1081348
  75.9 6.4 %copy-start.5 = (bf16[704,256]{1,0:T(8,128)(2,1)}, bf16[704,256]{1,0:T(8,128)(2,1)S(1)}, u32[]{:S(2)}) copy-start(bf16[704,256]{1,0:T(8,128)(2,1)S(1)} %collective-permute-done.5) | copy-start | bytes 1081348
  82.3 0.7 copy-start.8
  83.0 1.6 %copy-start = (bf16[1,704,256]{2,1,0:T(8,128)(2,1)S(1)}, bf16[1,704,256]{2,1,0:T(8,128)(2,1)}, u32[]{:S(2)}) copy-start(bf16[1,704,256]{2,1,0:T(8,128)(2,1)} %get-tuple-element.30) | copy-start | bytes 1081348
  83.0 1.6 %copy-start.3 = (bf16[704,256]{1,0:T(8,128)(2,1)S(1)}, bf16[704,256]{1,0:T(8,128)(2,1)}, u32[]{:S(2)}) copy-start(bf16[704,256]{1,0:T(8,128)(2,1)} %copy-done.2) | copy-start | bytes 1081348
  83.0 1.6 %copy-start.6 = (bf16[704,256]{1,0:T(8,128)(2,1)S(1)}, bf16[704,256]{1,0:T(8,128)(2,1)}, u32[]{:S(2)}) copy-start(bf16[704,256]{1,0:T(8,128)(2,1)} %copy-done.5) | copy-start | bytes 1081348
  83.0 1.7 %copy-start.9 = (bf16[704,256]{1,0:T(8,128)(2,1)S(1)}, bf16[704,256]{1,0:T(8,128)(2,1)}, u32[]{:S(2)}) copy-start(bf16[704,256]{1,0:T(8,128)(2,1)} %copy-done.8) | copy-start | bytes 1081348
  88.5 0.8 copy-start.11
  89.3 23.8 %copy-start.1 = (bf16[1,704,256]{2,1,0:T(8,128)(2,1)S(1)}, bf16[1,704,256]{2,1,0:T(8,128)(2,1)}, u32[]{:S(2)}) copy-start(bf16[1,704,256]{2,1,0:T(8,128)(2,1)} %get-tuple-element.30) | copy-start | bytes 1081348
  89.3 23.8 %copy-start.4 = (bf16[704,256]{1,0:T(8,128)(2,1)S(1)}, bf16[704,256]{1,0:T(8,128)(2,1)}, u32[]{:S(2)}) copy-start(bf16[704,256]{1,0:T(8,128)(2,1)} %copy-done.2) | copy-start | bytes 1081348
  89.3 23.8 %copy-start.7 = (bf16[704,256]{1,0:T(8,128)(2,1)S(1)}, bf16[704,256]{1,0:T(8,128)(2,1)}, u32[]{:S(2)}) copy-start(bf16[704,256]{1,0:T(8,128)(2,1)} %copy-done.5) | copy-start | bytes 1081348
  89.3 23.8 %copy-start.10 = (bf16[704,256]{1,0:T(8,128)(2,1)S(1)}, bf16[704,256]{1,0:T(8,128)(2,1)}, u32[]{:S(2)}) copy-start(bf16[704,256]{1,0:T(8,128)(2,1)} %copy-done.8) | copy-start | bytes 1081348
  90.5 27.4 %all-to-all-start.2 = ((f32[128,6,128]{2,1,0:T(8,128)}), f32[128,6,128]{2,1,0:T(8,128)}, u32[]{:S(2)}, u32[]{:S(2)}) async-start(f32[128,6,128]{2,1,0:T(8,128)} %pad_maximum_fusion.1), calls=%async_computation.2 | async-start | bytes 1048576 | tf_op jit(solution)/shard_map/all_to_all | solution.py:114
  98.2 21.6 %collective-permute-start.10 = (f32[56,128]{1,0:T(8,128)S(1)}, f32[56,128]{1,0:T(8,128)S(1)}, u32[]{:S(2)}, u32[]{:S(2)}) collective-permute-start(f32[56,128]{1,0:T(8,128)S(1)} %get-tuple-element.25), channel_id=1, source_target_pairs={{0,504},{4,508},{8,0},{12,4},{16,8},{20,12},{24,16},{28,20},{32,24... | collective-permute-start | bytes 86024 | tf_op jit(solution)/shard_map/ppermute | solution.py:16
  105.6 14.1 %collective-permute-start.9 = (f32[56,128]{1,0:T(8,128)S(1)}, f32[56,128]{1,0:T(8,128)S(1)}, u32[]{:S(2)}, u32[]{:S(2)}) collective-permute-start(f32[56,128]{1,0:T(8,128)S(1)} %get-tuple-element.26), channel_id=1, source_target_pairs={{0,508},{4,0},{8,4},{12,8},{16,12},{20,16},{24,20},{28,24},{32,28}... | collective-permute-start | bytes 86024 | tf_op jit(solution)/shard_map/ppermute | solution.py:16
  108.2 11.6 %collective-permute-start.8 = (f32[56,128]{1,0:T(8,128)S(1)}, f32[56,128]{1,0:T(8,128)S(1)}, u32[]{:S(2)}, u32[]{:S(2)}) collective-permute-start(f32[56,128]{1,0:T(8,128)S(1)} %get-tuple-element.27), channel_id=1, source_target_pairs={{0,4},{4,8},{8,12},{12,16},{16,20},{20,24},{24,28},{28,32},{32,36}... | collective-permute-start | bytes 86024 | tf_op jit(solution)/shard_map/ppermute | solution.py:16
  111.2 8.6 %collective-permute-start.7 = (f32[56,128]{1,0:T(8,128)S(1)}, f32[56,128]{1,0:T(8,128)S(1)}, u32[]{:S(2)}, u32[]{:S(2)}) collective-permute-start(f32[56,128]{1,0:T(8,128)S(1)} %get-tuple-element.24), channel_id=1, source_target_pairs={{0,8},{4,12},{8,16},{12,20},{16,24},{20,28},{24,32},{28,36},{32,40... | collective-permute-start | bytes 86024 | tf_op jit(solution)/shard_map/ppermute | solution.py:16
  114.5 6.0 %copy-start.13 = (bf16[448,128]{1,0:T(8,128)(2,1)S(1)}, bf16[448,128]{1,0:T(8,128)(2,1)}, u32[]{:S(2)}) copy-start(bf16[448,128]{1,0:T(8,128)(2,1)} %param.10) | copy-start | bytes 344068

commit v8 on v5

--- a/solution.py
+++ b/solution.py
@@ -109,9 +109,10 @@
     hub_chunks = table_grad[rows_here + halo_rows :].reshape(dom_count, hub_dev, feat_in)
     weight_rep = jnp.broadcast_to(weight_part[None], (dom_count,) + weight_part.shape)
     sent = jnp.concatenate([hub_chunks, weight_rep], 1)
-    recv = lax.all_to_all(sent, "dom", 0, 0, tiled=True)
-    hub_total = jnp.sum(recv[:, :hub_dev], axis=0)
-    weights = recv[:, hub_dev:].reshape(2, feat_in, hidden_here)
+    recv3 = lax.all_to_all(sent, "dom", 0, 0, tiled=True)
+    recv = recv3.reshape(dom_count, -1)
+    hub_total = jnp.sum(recv[:, : hub_dev * feat_in], axis=0).reshape(hub_dev, feat_in)
+    weights = recv3[:, hub_dev:].reshape(2, feat_in, hidden_here)
 
     grad_in = own_grad + table_grad[:rows_here]
     grad_in = grad_in + contract_rows(pick.astype(F32), returned, HIGH)

time: 121 us -> 119 us (0.983)
    unnamed x41 -> x39, local copies, waits for them, and re-layouts: 2.45 us -> 2.46 us
where the time goes in v8:
time: 119 us; the launch traced here: 118 us
  starting transfers between devices  66.9 us (56%)
  waiting for transfers between devices  24.3 us (20%)
  matrix products  9.82 us (8%)
  other arithmetic  9.35 us (8%)
  local copies, waits for them, and re-layouts  6.74 us (6%)
    ppermute x11, starting transfers between devices, from_behind(): return lax.ppermute(x, axis, [(i, (i + by) % size) for i in range(size)])  46.1 us
    all_to_all x1, waiting for transfers between devices, gather_all(): out = lax.all_to_all(rep, axis, 0, 0, tiled=True)  11.2 us
    ppermute x11, waiting for transfers between devices, from_behind(): return lax.ppermute(x, axis, [(i, (i + by) % size) for i in range(size)])  9.43 us
    all_to_all x1, starting transfers between devices, gather_all(): out = lax.all_to_all(rep, axis, 0, 0, tiled=True)  8.57 us
    all_to_all x1, starting transfers between devices, per_device(): lax.all_to_all(weight_flat.reshape(dom_count, -1, 128), 'dom', 0, 0, tile...  6.38 us
    all_to_all x1, starting transfers between devices, per_device(): recv3 = lax.all_to_all(sent, 'dom', 0, 0, tiled=True)  5.84 us
    dot_general x5, matrix products, contract_rows(): lax.dot_general(left, right, (((0,), (0,)), ((), ())), preferred_element_...  5.04 us
    reduce_sum x1, other arithmetic, per_device(): counts = jnp.sum((neighbors[:, :, None] == t_iota).astype(F32), axis=1)  3.65 us
  transfers between devices with their start and end apart: 14, of which 5 were waited for; matrix products, arithmetic and copies ran while one was open for 13% of the time, Pallas kernels for 0%

profile of v8, /device:TPU:1, one launch (start us, length us, event | category | flops | bytes accessed | tf_op | source)
XLA Modules:
  0.0 118.2 jit_solution(9697361618187803980)
XLA Ops:
  0.6 0.8 eq.30
  1.4 1.0 constant_dynamic-update-slice_fusion.5
  2.4 0.3 convolution_convert_fusion
  2.7 14.4 %collective-permute-start = (bf16[56,128]{1,0:T(8,128)(2,1)S(1)}, bf16[56,128]{1,0:T(8,128)(2,1)S(1)}, u32[]{:S(2)}, u32[]{:S(2)}) collective-permute-start(bf16[56,128]{1,0:T(8,128)(2,1)S(1)} %get-tuple-element.31), channel_id=1, source_target_pairs={{0,504},{4,508},{8,0},{12,4},{16,8},{20,12},{24,16},{28,20},{32,24... | collective-permute-start | bytes 43016 | tf_op jit(solution)/shard_map/ppermute | solution.py:16
  17.1 2.9 %collective-permute-start.1 = (bf16[56,128]{1,0:T(8,128)(2,1)S(1)}, bf16[56,128]{1,0:T(8,128)(2,1)S(1)}, u32[]{:S(2)}, u32[]{:S(2)}) collective-permute-start(bf16[56,128]{1,0:T(8,128)(2,1)S(1)} %get-tuple-element.30), channel_id=1, source_target_pairs={{0,508},{4,0},{8,4},{12,8},{16,12},{20,16},{24,20},{28,24},{32,28}... | collective-permute-start | bytes 43016 | tf_op jit(solution)/shard_map/ppermute | solution.py:16
  20.0 2.7 %collective-permute-start.2 = (bf16[56,128]{1,0:T(8,128)(2,1)S(1)}, bf16[56,128]{1,0:T(8,128)(2,1)S(1)}, u32[]{:S(2)}, u32[]{:S(2)}) collective-permute-start(bf16[56,128]{1,0:T(8,128)(2,1)S(1)} %get-tuple-element.29), channel_id=1, source_target_pairs={{0,4},{4,8},{8,12},{12,16},{16,20},{20,24},{24,28},{28,32},{32,36}... | collective-permute-start | bytes 43016 | tf_op jit(solution)/shard_map/ppermute | solution.py:16
  22.7 1.9 %collective-permute-start.3 = (bf16[56,128]{1,0:T(8,128)(2,1)S(1)}, bf16[56,128]{1,0:T(8,128)(2,1)S(1)}, u32[]{:S(2)}, u32[]{:S(2)}) collective-permute-start(bf16[56,128]{1,0:T(8,128)(2,1)S(1)} %get-tuple-element.28), channel_id=1, source_target_pairs={{0,8},{4,12},{8,16},{12,20},{16,24},{20,28},{24,32},{28,36},{32,40... | collective-permute-start | bytes 43016 | tf_op jit(solution)/shard_map/ppermute | solution.py:16
  24.6 0.8 convolution_convert_fusion.1
  25.5 0.8 broadcast_in_dim.4
  26.2 8.6 %all-to-all-start = ((bf16[128,8,128]{2,1,0:T(8,128)(2,1)}), bf16[128,8,128]{2,1,0:T(8,128)(2,1)S(1)}, u32[]{:S(2)}, u32[]{:S(2)}) async-start(bf16[128,8,128]{2,1,0:T(8,128)(2,1)} %broadcast_in_dim.4), calls=%async_computation | async-start | bytes 524288 | tf_op jit(solution)/shard_map/all_to_all | solution.py:32
  34.8 3.6 %convert_reduce_fusion = f32[448,928]{1,0:T(8,128)S(1)} fusion(s32[448,15]{0,1:T(8,128)S(1)} %copy-done.14), kind=kLoop, calls=%fused_computation | loop fusion | flops 18292736 | bytes 1689856 | tf_op jit(solution)/shard_map/reduce_sum | solution.py:66
  38.5 0.2 fusion.42
  38.8 11.2 %all-to-all-done = bf16[128,8,128]{2,1,0:T(8,128)(2,1)S(1)} async-done(((bf16[128,8,128]{2,1,0:T(8,128)(2,1)}), bf16[128,8,128]{2,1,0:T(8,128)(2,1)S(1)}, u32[]{:S(2)}, u32[]{:S(2)}) %all-to-all-start) | async-done | bytes 262176 | tf_op jit(solution)/shard_map/all_to_all | solution.py:32
  50.1 0.4 fusion.4
  50.5 1.3 %multiply_convert_fusion = bf16[448,256]{1,0:T(8,128)(2,1)S(1)} fusion(f32[448,256]{1,0:T(8,128)S(1)} %fusion.42, bf16[448,128]{1,0:T(8,128)(2,1)S(1)} %fusion.4, bf16[128,256]{1,0:T(8,128)(2,1)S(1)} %copy-done.13, bf16[448,256]{1,0:T(8,128)(2,1)} %param.14, f32[256]{0:T(256)S(1)} %copy-done.16), kind=kOutput, calls=%fused_computation.19 | convolution fusion | flops 30736384 | bytes 1098752 | tf_op jit(solution)/shard_map/dot_general | solution.py:71
  51.8 0.9 fusion.38
  52.7 4.4 %collective-permute-start.6 = (bf16[704,256]{1,0:T(8,128)(2,1)}, bf16[704,256]{1,0:T(8,128)(2,1)S(1)}, u32[]{:S(2)}, u32[]{:S(2)}) collective-permute-start(bf16[704,256]{1,0:T(8,128)(2,1)} %get-tuple-element.27), channel_id=1, source_target_pairs={{0,3},{1,0},{2,1},{3,2},{4,7},{5,4},{6,5},{7,6},{8,11},{9,8},{10,9... | collective-permute-start | bytes 1081352 | tf_op jit(solution)/shard_map/ppermute | solution.py:16
  57.1 2.4 %collective-permute-start.5 = (bf16[704,256]{1,0:T(8,128)(2,1)}, bf16[704,256]{1,0:T(8,128)(2,1)S(1)}, u32[]{:S(2)}, u32[]{:S(2)}) collective-permute-start(bf16[704,256]{1,0:T(8,128)(2,1)} %get-tuple-element.27), channel_id=1, source_target_pairs={{0,2},{1,3},{2,0},{3,1},{4,6},{5,7},{6,4},{7,5},{8,10},{9,11},{10,... | collective-permute-start | bytes 1081352 | tf_op jit(solution)/shard_map/ppermute | solution.py:16
  59.5 2.5 %collective-permute-start.4 = (bf16[704,256]{1,0:T(8,128)(2,1)}, bf16[704,256]{1,0:T(8,128)(2,1)S(1)}, u32[]{:S(2)}, u32[]{:S(2)}) collective-permute-start(bf16[704,256]{1,0:T(8,128)(2,1)} %get-tuple-element.27), channel_id=1, source_target_pairs={{0,1},{1,2},{2,3},{3,0},{4,5},{5,6},{6,7},{7,4},{8,9},{9,10},{10,1... | collective-permute-start | bytes 1081352 | tf_op jit(solution)/shard_map/ppermute | solution.py:16
  62.1 0.2 fusion.45
  62.4 0.2 fusion.44
  62.7 0.8 pad_maximum_fusion.3
  63.5 6.4 %all-to-all-start.1 = ((f32[128,4,128]{2,1,0:T(4,128)}), f32[128,4,128]{2,1,0:T(4,128)S(1)}, u32[]{:S(2)}, u32[]{:S(2)}) async-start(f32[128,4,128]{2,1,0:T(4,128)} %pad_maximum_fusion.3), calls=%async_computation.1 | async-start | bytes 524288 | tf_op jit(solution)/shard_map/all_to_all | solution.py:85
  69.9 0.2 collective-permute-done.5
  70.1 8.7 %collective-permute-done.4 = bf16[704,256]{1,0:T(8,128)(2,1)S(1)} collective-permute-done((bf16[704,256]{1,0:T(8,128)(2,1)}, bf16[704,256]{1,0:T(8,128)(2,1)S(1)}, u32[]{:S(2)}, u32[]{:S(2)}) %collective-permute-start.4) | collective-permute-done | bytes 360480 | tf_op jit(solution)/shard_map/ppermute | solution.py:16
  78.8 0.8 copy-done.8
  79.6 1.6 %pad_maximum_fusion = bf16[4,704,256]{2,1,0:T(8,128)(2,1)S(1)} fusion(bf16[1,704,256]{2,1,0:T(8,128)(2,1)} %bitcast.33, bf16[1,704,256]{2,1,0:T(8,128)(2,1)} %bitcast.36, bf16[1,704,256]{2,1,0:T(8,128)(2,1)} %bitcast.39, bf16[1,704,256]{2,1,0:T(8,128)(2,1)} %get-tuple-element.26), kind=kLoop, calls=%fused_computation.2 | loop fusion | flops 2162688 | bytes 2883584 | tf_op jit(solution)/shard_map/stack | solution.py:78
  81.3 0.4 fusion.2
  81.7 3.4 %fusion.43 = f32[928,128]{1,0:T(8,128)S(1)} fusion(f32[448,928]{1,0:T(8,128)S(1)} %convert_reduce_fusion, f32[448,128]{1,0:T(8,128)S(1)} %fusion.2), kind=kOutput, calls=%fused_computation.70 | convolution fusion | flops 638582784 | bytes 2367488 | tf_op jit(solution)/shard_map/dot_general | solution.py:24
  85.1 0.8 copy-done.10
  85.9 0.1 reduce_sum.37
  86.1 0.9 pad_maximum_fusion.1
  87.0 5.8 %all-to-all-start.2 = ((f32[128,6,128]{2,1,0:T(8,128)}), f32[128,6,128]{2,1,0:T(8,128)S(1)}, u32[]{:S(2)}, u32[]{:S(2)}) async-start(f32[128,6,128]{2,1,0:T(8,128)} %pad_maximum_fusion.1), calls=%async_computation.2 | async-start | bytes 1048576 | tf_op jit(solution)/shard_map/all_to_all | solution.py:112
  92.9 0.8 fusion.40
  93.7 7.4 %collective-permute-start.10 = (f32[56,128]{1,0:T(8,128)S(1)}, f32[56,128]{1,0:T(8,128)S(1)}, u32[]{:S(2)}, u32[]{:S(2)}) collective-permute-start(f32[56,128]{1,0:T(8,128)S(1)} %get-tuple-element.23), channel_id=1, source_target_pairs={{0,504},{4,508},{8,0},{12,4},{16,8},{20,12},{24,16},{28,20},{32,24... | collective-permute-start | bytes 86024 | tf_op jit(solution)/shard_map/ppermute | solution.py:16
  101.1 2.6 %collective-permute-start.9 = (f32[56,128]{1,0:T(8,128)S(1)}, f32[56,128]{1,0:T(8,128)S(1)}, u32[]{:S(2)}, u32[]{:S(2)}) collective-permute-start(f32[56,128]{1,0:T(8,128)S(1)} %get-tuple-element.24), channel_id=1, source_target_pairs={{0,508},{4,0},{8,4},{12,8},{16,12},{20,16},{24,20},{28,24},{32,28}... | collective-permute-start | bytes 86024 | tf_op jit(solution)/shard_map/ppermute | solution.py:16
  103.7 3.0 %collective-permute-start.8 = (f32[56,128]{1,0:T(8,128)S(1)}, f32[56,128]{1,0:T(8,128)S(1)}, u32[]{:S(2)}, u32[]{:S(2)}) collective-permute-start(f32[56,128]{1,0:T(8,128)S(1)} %get-tuple-element.25), channel_id=1, source_target_pairs={{0,4},{4,8},{8,12},{12,16},{16,20},{20,24},{24,28},{28,32},{32,36}... | collective-permute-start | bytes 86024 | tf_op jit(solution)/shard_map/ppermute | solution.py:16
  106.7 1.9 %collective-permute-start.7 = (f32[56,128]{1,0:T(8,128)S(1)}, f32[56,128]{1,0:T(8,128)S(1)}, u32[]{:S(2)}, u32[]{:S(2)}) collective-permute-start(f32[56,128]{1,0:T(8,128)S(1)} %get-tuple-element.22), channel_id=1, source_target_pairs={{0,8},{4,12},{8,16},{12,20},{16,24},{20,28},{24,32},{28,36},{32,40... | collective-permute-start | bytes 86024 | tf_op jit(solution)/shard_map/ppermute | solution.py:16
  108.7 1.4 %fusion.3 = f32[448,128]{1,0:T(8,128)S(1)} fusion(bf16[4,704,256]{2,1,0:T(8,128)(2,1)S(1)} %pad_maximum_fusion, bf16[1,704,256]{2,1,0:T(8,128)(2,1)S(1)} %bitcast.35, bf16[1,704,256]{2,1,0:T(8,128)(2,1)S(1)} %bitcast.38, bf16[1,704,256]{2,1,0:T(8,128)(2,1)} %bitcast.40, bf16[1,704,256]{2,1,0:T(8,128)(2,1)S(1)} %copy-done.1, f32[928,128]{1,0:T(8,128)} %copy-done.10), kind=kOutput, calls=%fused_computation.11 | convolution fusion | flops 118546432 | bytes 2818048 | tf_op jit(solution)/shard_map/dot_general | solution.py:91
  110.1 3.6 %all-to-all-done.2 = f32[128,6,128]{2,1,0:T(8,128)S(1)} async-done(((f32[128,6,128]{2,1,0:T(8,128)}), f32[128,6,128]{2,1,0:T(8,128)S(1)}, u32[]{:S(2)}, u32[]{:S(2)}) %all-to-all-start.2) | async-done | bytes 393248 | tf_op jit(solution)/shard_map/all_to_all | solution.py:112
  113.7 0.2 copy.25
  114.0 0.4 fusion.31
  114.5 0.5 collective-permute-done.7
  115.0 0.8 multiply_reduce_fusion
  115.7 0.2 add_convert_fusion
  116.0 0.7 copy.26
  116.8 0.7 squeeze.6
  117.5 0.7 squeeze.7
  (56 shorter events, 0.7 us)
Async XLA Ops:
  0.6 34.2 %copy-start.14 = (s32[448,15]{0,1:T(8,128)S(1)}, s32[448,15]{0,1:T(8,128)}, u32[]{:S(2)}) copy-start(s32[448,15]{0,1:T(8,128)} %param.17) | copy-start | bytes 80644
  2.7 35.8 %copy-start.12 = (bf16[128,256]{1,0:T(8,128)(2,1)S(1)}, bf16[128,256]{1,0:T(8,128)(2,1)}, u32[]{:S(2)}) copy-start(bf16[128,256]{1,0:T(8,128)(2,1)} %param.11) | copy-start | bytes 196612
  2.7 36.0 %collective-permute-start = (bf16[56,128]{1,0:T(8,128)(2,1)S(1)}, bf16[56,128]{1,0:T(8,128)(2,1)S(1)}, u32[]{:S(2)}, u32[]{:S(2)}) collective-permute-start(bf16[56,128]{1,0:T(8,128)(2,1)S(1)} %get-tuple-element.31), channel_id=1, source_target_pairs={{0,504},{4,508},{8,0},{12,4},{16,8},{20,12},{24,16},{28,20},{32,24... | collective-permute-start | bytes 43016 | tf_op jit(solution)/shard_map/ppermute | solution.py:16
  17.1 21.6 %collective-permute-start.1 = (bf16[56,128]{1,0:T(8,128)(2,1)S(1)}, bf16[56,128]{1,0:T(8,128)(2,1)S(1)}, u32[]{:S(2)}, u32[]{:S(2)}) collective-permute-start(bf16[56,128]{1,0:T(8,128)(2,1)S(1)} %get-tuple-element.30), channel_id=1, source_target_pairs={{0,508},{4,0},{8,4},{12,8},{16,12},{20,16},{24,20},{28,24},{32,28}... | collective-permute-start | bytes 43016 | tf_op jit(solution)/shard_map/ppermute | solution.py:16
  20.0 18.8 %collective-permute-start.2 = (bf16[56,128]{1,0:T(8,128)(2,1)S(1)}, bf16[56,128]{1,0:T(8,128)(2,1)S(1)}, u32[]{:S(2)}, u32[]{:S(2)}) collective-permute-start(bf16[56,128]{1,0:T(8,128)(2,1)S(1)} %get-tuple-element.29), channel_id=1, source_target_pairs={{0,4},{4,8},{8,12},{12,16},{16,20},{20,24},{24,28},{28,32},{32,36}... | collective-permute-start | bytes 43016 | tf_op jit(solution)/shard_map/ppermute | solution.py:16
  22.7 16.1 %collective-permute-start.3 = (bf16[56,128]{1,0:T(8,128)(2,1)S(1)}, bf16[56,128]{1,0:T(8,128)(2,1)S(1)}, u32[]{:S(2)}, u32[]{:S(2)}) collective-permute-start(bf16[56,128]{1,0:T(8,128)(2,1)S(1)} %get-tuple-element.28), channel_id=1, source_target_pairs={{0,8},{4,12},{8,16},{12,20},{16,24},{20,28},{24,32},{28,36},{32,40... | collective-permute-start | bytes 43016 | tf_op jit(solution)/shard_map/ppermute | solution.py:16
  26.2 23.8 %all-to-all-start = ((bf16[128,8,128]{2,1,0:T(8,128)(2,1)}), bf16[128,8,128]{2,1,0:T(8,128)(2,1)S(1)}, u32[]{:S(2)}, u32[]{:S(2)}) async-start(bf16[128,8,128]{2,1,0:T(8,128)(2,1)} %broadcast_in_dim.4), calls=%async_computation | async-start | bytes 524288 | tf_op jit(solution)/shard_map/all_to_all | solution.py:32
  38.7 11.8 %copy-start.13 = (bf16[128,256]{1,0:T(8,128)(2,1)S(1)}, bf16[128,256]{1,0:T(8,128)(2,1)}, u32[]{:S(2)}) copy-start(bf16[128,256]{1,0:T(8,128)(2,1)} %param.12) | copy-start | bytes 196612
  38.7 11.8 %copy-start.16 = (f32[256]{0:T(256)S(1)}, f32[256]{0:T(256)}, u32[]{:S(2)}) copy-start(f32[256]{0:T(256)} %param.13) | copy-start | bytes 3076
  52.7 17.1 %collective-permute-start.6 = (bf16[704,256]{1,0:T(8,128)(2,1)}, bf16[704,256]{1,0:T(8,128)(2,1)S(1)}, u32[]{:S(2)}, u32[]{:S(2)}) collective-permute-start(bf16[704,256]{1,0:T(8,128)(2,1)} %get-tuple-element.27), channel_id=1, source_target_pairs={{0,3},{1,0},{2,1},{3,2},{4,7},{5,4},{6,5},{7,6},{8,11},{9,8},{10,9... | collective-permute-start | bytes 1081352 | tf_op jit(solution)/shard_map/ppermute | solution.py:16
  57.1 13.0 %collective-permute-start.5 = (bf16[704,256]{1,0:T(8,128)(2,1)}, bf16[704,256]{1,0:T(8,128)(2,1)S(1)}, u32[]{:S(2)}, u32[]{:S(2)}) collective-permute-start(bf16[704,256]{1,0:T(8,128)(2,1)} %get-tuple-element.27), channel_id=1, source_target_pairs={{0,2},{1,3},{2,0},{3,1},{4,6},{5,7},{6,4},{7,5},{8,10},{9,11},{10,... | collective-permute-start | bytes 1081352 | tf_op jit(solution)/shard_map/ppermute | solution.py:16
  59.5 19.2 %collective-permute-start.4 = (bf16[704,256]{1,0:T(8,128)(2,1)}, bf16[704,256]{1,0:T(8,128)(2,1)S(1)}, u32[]{:S(2)}, u32[]{:S(2)}) collective-permute-start(bf16[704,256]{1,0:T(8,128)(2,1)} %get-tuple-element.27), channel_id=1, source_target_pairs={{0,1},{1,2},{2,3},{3,0},{4,5},{5,6},{6,7},{7,4},{8,9},{9,10},{10,1... | collective-permute-start | bytes 1081352 | tf_op jit(solution)/shard_map/ppermute | solution.py:16
  63.5 22.4 %all-to-all-start.1 = ((f32[128,4,128]{2,1,0:T(4,128)}), f32[128,4,128]{2,1,0:T(4,128)S(1)}, u32[]{:S(2)}, u32[]{:S(2)}) async-start(f32[128,4,128]{2,1,0:T(4,128)} %pad_maximum_fusion.3), calls=%async_computation.1 | async-start | bytes 524288 | tf_op jit(solution)/shard_map/all_to_all | solution.py:85
  69.8 8.9 %copy-start.2 = (bf16[704,256]{1,0:T(8,128)(2,1)}, bf16[704,256]{1,0:T(8,128)(2,1)S(1)}, u32[]{:S(2)}) copy-start(bf16[704,256]{1,0:T(8,128)(2,1)S(1)} %collective-permute-done.6) | copy-start | bytes 1081348
  70.1 8.7 %copy-start.5 = (bf16[704,256]{1,0:T(8,128)(2,1)}, bf16[704,256]{1,0:T(8,128)(2,1)S(1)}, u32[]{:S(2)}) copy-start(bf16[704,256]{1,0:T(8,128)(2,1)S(1)} %collective-permute-done.5) | copy-start | bytes 1081348
  78.8 0.8 copy-start.8
  79.5 1.6 %copy-start = (bf16[1,704,256]{2,1,0:T(8,128)(2,1)S(1)}, bf16[1,704,256]{2,1,0:T(8,128)(2,1)}, u32[]{:S(2)}) copy-start(bf16[1,704,256]{2,1,0:T(8,128)(2,1)} %get-tuple-element.26) | copy-start | bytes 1081348
  79.5 1.6 %copy-start.3 = (bf16[704,256]{1,0:T(8,128)(2,1)S(1)}, bf16[704,256]{1,0:T(8,128)(2,1)}, u32[]{:S(2)}) copy-start(bf16[704,256]{1,0:T(8,128)(2,1)} %copy-done.2) | copy-start | bytes 1081348
  79.6 1.6 %copy-start.6 = (bf16[704,256]{1,0:T(8,128)(2,1)S(1)}, bf16[704,256]{1,0:T(8,128)(2,1)}, u32[]{:S(2)}) copy-start(bf16[704,256]{1,0:T(8,128)(2,1)} %copy-done.5) | copy-start | bytes 1081348
  79.6 1.7 %copy-start.9 = (bf16[704,256]{1,0:T(8,128)(2,1)S(1)}, bf16[704,256]{1,0:T(8,128)(2,1)}, u32[]{:S(2)}) copy-start(bf16[704,256]{1,0:T(8,128)(2,1)} %copy-done.8) | copy-start | bytes 1081348
  85.1 0.8 copy-start.10
  85.9 22.8 %copy-start.1 = (bf16[1,704,256]{2,1,0:T(8,128)(2,1)S(1)}, bf16[1,704,256]{2,1,0:T(8,128)(2,1)}, u32[]{:S(2)}) copy-start(bf16[1,704,256]{2,1,0:T(8,128)(2,1)} %get-tuple-element.26) | copy-start | bytes 1081348
  85.9 22.8 %copy-start.4 = (bf16[704,256]{1,0:T(8,128)(2,1)S(1)}, bf16[704,256]{1,0:T(8,128)(2,1)}, u32[]{:S(2)}) copy-start(bf16[704,256]{1,0:T(8,128)(2,1)} %copy-done.2) | copy-start | bytes 1081348
  85.9 22.8 %copy-start.7 = (bf16[704,256]{1,0:T(8,128)(2,1)S(1)}, bf16[704,256]{1,0:T(8,128)(2,1)}, u32[]{:S(2)}) copy-start(bf16[704,256]{1,0:T(8,128)(2,1)} %copy-done.5) | copy-start | bytes 1081348
  87.0 26.6 %all-to-all-start.2 = ((f32[128,6,128]{2,1,0:T(8,128)}), f32[128,6,128]{2,1,0:T(8,128)S(1)}, u32[]{:S(2)}, u32[]{:S(2)}) async-start(f32[128,6,128]{2,1,0:T(8,128)} %pad_maximum_fusion.1), calls=%async_computation.2 | async-start | bytes 1048576 | tf_op jit(solution)/shard_map/all_to_all | solution.py:112
  93.7 20.8 %collective-permute-start.10 = (f32[56,128]{1,0:T(8,128)S(1)}, f32[56,128]{1,0:T(8,128)S(1)}, u32[]{:S(2)}, u32[]{:S(2)}) collective-permute-start(f32[56,128]{1,0:T(8,128)S(1)} %get-tuple-element.23), channel_id=1, source_target_pairs={{0,504},{4,508},{8,0},{12,4},{16,8},{20,12},{24,16},{28,20},{32,24... | collective-permute-start | bytes 86024 | tf_op jit(solution)/shard_map/ppermute | solution.py:16
  101.1 13.3 %collective-permute-start.9 = (f32[56,128]{1,0:T(8,128)S(1)}, f32[56,128]{1,0:T(8,128)S(1)}, u32[]{:S(2)}, u32[]{:S(2)}) collective-permute-start(f32[56,128]{1,0:T(8,128)S(1)} %get-tuple-element.24), channel_id=1, source_target_pairs={{0,508},{4,0},{8,4},{12,8},{16,12},{20,16},{24,20},{28,24},{32,28}... | collective-permute-start | bytes 86024 | tf_op jit(solution)/shard_map/ppermute | solution.py:16
  103.7 10.7 %collective-permute-start.8 = (f32[56,128]{1,0:T(8,128)S(1)}, f32[56,128]{1,0:T(8,128)S(1)}, u32[]{:S(2)}, u32[]{:S(2)}) collective-permute-start(f32[56,128]{1,0:T(8,128)S(1)} %get-tuple-element.25), channel_id=1, source_target_pairs={{0,4},{4,8},{8,12},{12,16},{16,20},{20,24},{24,28},{28,32},{32,36}... | collective-permute-start | bytes 86024 | tf_op jit(solution)/shard_map/ppermute | solution.py:16
  106.7 7.3 %copy-start.15 = (s32[1,2]{1,0:T(1,128)S(1)}, s32[1,2]{1,0:T(1,128)}, u32[]{:S(2)}) copy-start(s32[1,2]{1,0:T(1,128)} %param.15) | copy-start | bytes 28
  106.7 8.2 %collective-permute-start.7 = (f32[56,128]{1,0:T(8,128)S(1)}, f32[56,128]{1,0:T(8,128)S(1)}, u32[]{:S(2)}, u32[]{:S(2)}) collective-permute-start(f32[56,128]{1,0:T(8,128)S(1)} %get-tuple-element.22), channel_id=1, source_target_pairs={{0,8},{4,12},{8,16},{12,20},{16,24},{20,28},{24,32},{28,36},{32,40... | collective-permute-start | bytes 86024 | tf_op jit(solution)/shard_map/ppermute | solution.py:16
  110.1 5.7 %copy-start.11 = (bf16[448,128]{1,0:T(8,128)(2,1)S(1)}, bf16[448,128]{1,0:T(8,128)(2,1)}, u32[]{:S(2)}) copy-start(bf16[448,128]{1,0:T(8,128)(2,1)} %param.10) | copy-start | bytes 344068
